TPU v7x, 768 devices: a whole 4x8x12 slice. The times are simulated.
768 devices in a mesh: dp: 2 (over z_hi), ctx: 96 (over z_lo, y, core), fsdp: 4 (over x).
Axes of the slice: x: 4, y: 8, z: 12 (z_hi: 2, z_lo: 6; z = z_hi * 6 + z_lo), core: 2. Of those that a mesh axis runs over, the one named last changes fastest.
Arguments:
- query: bfloat16 [2, 49152, 2048], P('dp', 'ctx', 'fsdp'), may hold values from -6 to 6
- key: bfloat16 [2, 49152, 1024], P('dp', 'ctx', 'fsdp'), may hold values from -6 to 6
- value: bfloat16 [2, 49152, 1024], P('dp', 'ctx', 'fsdp'), may hold values from -6 to 6
- out_grad: bfloat16 [2, 49152, 2048], P('dp', 'ctx', 'fsdp'), may hold values from -48 to 48
- query_gain: float32 [128], replicated, may hold values from 0.25 to 1.75
- key_gain: float32 [128], replicated, may hold values from 0.25 to 1.75
- list_start: int32 [2, 49152], P('dp', 'ctx'), may hold values from 0 to 49151, as said below
Outputs:
- query_grad: bfloat16 [2, 49152, 2048], P('dp', 'ctx', 'fsdp')
- key_grad: bfloat16 [2, 49152, 1024], P('dp', 'ctx', 'fsdp')
- value_grad: bfloat16 [2, 49152, 1024], P('dp', 'ctx', 'fsdp')
- gain_grads: float32 [2, 128], replicated
Inputs may be any that keep to these rules, and one draw needn't show every extreme that they name: list_start of a token is at most its own position and never falls along a sequence; it equals the position where a new candidate list begins; positions 0 and 49151 each begin a list.
All inputs are finite; a program needn't handle non-finite values.
Results may differ from a plain program's by a relative error of at most 0.0078.
Values may be sent and summed in bfloat16 or wider, within the bound.
No kernel may reach another device: no remote copies, remote signals or barrier semaphores. Data moves between devices by JAX's collectives and lax.ppermute only.
A program may use at most 64 MiB of HBM per device.

v0:
```python
import jax
import jax.numpy as jnp
from jax import lax
from jax.sharding import PartitionSpec as P

HD = 128
HQ = 16
HK = 8
WINDOW = 1024
QSCALAR = 168


epsilon = 1e-06


def passed_along(value, axis, steps):
    count = lax.axis_size(axis)
    initial, last = (max(0, -steps), min(count, count - steps))
    return lax.ppermute(value, axis, [(source, source + steps) for source in range(initial, last)])


def normalize(raw, gain, factor):
    values = raw.astype(jnp.float32)
    inverse = lax.rsqrt(jnp.mean(values * values, axis=-1, keepdims=True) + epsilon)
    unit_rows = values * inverse
    return (unit_rows, inverse, (unit_rows * gain * factor).astype(jnp.bfloat16))


def norm_backward(grad_n, unit_rows, inverse, gain, factor):
    grad_hat = grad_n * gain * factor
    return (grad_hat - unit_rows * jnp.mean(grad_hat * unit_rows, axis=-1, keepdims=True)) * inverse


def shards(query, key, value, out_grad, query_gain, key_gain, list_start):
    tokens = query.shape[1]
    kv_heads = key.shape[2] // HD
    group_size = query.shape[2] // key.shape[2]
    factor = QSCALAR ** (-0.5)
    reach = WINDOW // tokens
    query_hat, query_inv, query_n = normalize(
        query[0].reshape(tokens, kv_heads, group_size, HD), query_gain, factor
    )
    key_hat, key_inv, key_n = normalize(key[0].reshape(tokens, kv_heads, HD), key_gain, 1.0)
    own_values = value[0].reshape(tokens, kv_heads, HD)
    grads_in = out_grad[0].reshape(tokens, kv_heads, group_size, HD)
    starts = list_start[0]
    anchor = lax.axis_index("ctx") * tokens
    query_place = anchor + jnp.arange(tokens, dtype=jnp.int32)
    blocks = [(key_n, own_values)]
    for distance in range(1, reach + 1):
        blocks.append(passed_along((key_n, own_values), "ctx", distance))
    allowed_sets = []
    for distance in range(reach + 1):
        key_place = anchor - distance * tokens + jnp.arange(tokens, dtype=jnp.int32)
        allowed_sets.append(
            (key_place[None, :] >= starts[:, None])
            & (key_place[None, :] <= query_place[:, None])
            & (query_place[:, None] - key_place[None, :] < WINDOW)
        )

    def forward_block(operands):
        allowed, key_block = operands
        scores = jnp.einsum(
            "tkgd,ukd->kgtu", query_n, key_block, preferred_element_type=jnp.float32
        )
        return jnp.where(allowed[None, None], jnp.exp(scores), 0.0)

    cached = [forward_block((allowed_sets[index], blocks[index][0])) for index in range(reach + 1)]
    denominator = jnp.sum(cached[0], axis=-1, keepdims=True)
    for weight in cached[1:]:
        denominator = denominator + jnp.sum(weight, axis=-1, keepdims=True)
    weights_bf = [(weight / denominator).astype(jnp.bfloat16) for weight in cached]
    attend_zero = jnp.zeros((tokens, kv_heads, group_size, HD), jnp.float32)
    attended = attend_zero
    for index in range(reach + 1):
        attend_prob = weights_bf[index]
        attend_value_block = blocks[index][1]
        attended = attended + jnp.einsum(
            "kgtu,ukd->tkgd", attend_prob, attend_value_block, preferred_element_type=jnp.float32
        )
    row_term = jnp.transpose(jnp.sum(grads_in.astype(jnp.float32) * attended, axis=-1), (1, 2, 0))[
        ..., None
    ]
    dquery_n = attend_zero
    pieces = []
    for index in range(reach + 1):
        prob = weights_bf[index]
        backward_key_block = blocks[index][0]
        value_block = blocks[index][1]
        products = jnp.einsum(
            "tkgd,ukd->kgtu", grads_in, value_block, preferred_element_type=jnp.float32
        )
        dscore = (prob.astype(jnp.float32) * (products - row_term)).astype(jnp.bfloat16)
        dquery_part = jnp.einsum(
            "kgtu,ukd->tkgd", dscore, backward_key_block, preferred_element_type=jnp.float32
        )
        dkey_part = jnp.einsum(
            "kgtu,tkgd->ukd", dscore, query_n, preferred_element_type=jnp.float32
        )
        dvalue_part = jnp.einsum(
            "kgtu,tkgd->ukd", prob, grads_in, preferred_element_type=jnp.float32
        )
        dquery_n = dquery_n + dquery_part
        pieces.append((dkey_part, dvalue_part))
    dkey_n = pieces[0][0]
    dvalue_sum = pieces[0][1]
    for distance in range(1, reach + 1):
        returned = passed_along(pieces[distance], "ctx", -distance)
        dkey_n = dkey_n + returned[0]
        dvalue_sum = dvalue_sum + returned[1]
    query_grad = (
        norm_backward(dquery_n, query_hat, query_inv, query_gain, factor)
        .astype(jnp.bfloat16)
        .reshape(1, tokens, -1)
    )
    key_grad = (
        norm_backward(dkey_n, key_hat, key_inv, key_gain, 1.0)
        .astype(jnp.bfloat16)
        .reshape(1, tokens, -1)
    )
    value_grad = dvalue_sum.astype(jnp.bfloat16).reshape(1, tokens, -1)
    partial_sums = jnp.stack(
        [
            jnp.sum(dquery_n * query_hat, axis=(0, 1, 2)) * factor,
            jnp.sum(dkey_n * key_hat, axis=(0, 1)),
        ]
    )
    summed = lax.psum(partial_sums, ("dp", "ctx", "fsdp"))
    counted = lax.axis_size("dp") * lax.axis_size("ctx") * tokens
    normalizers = jnp.array([[(counted * HQ) ** (-0.5)], [(counted * HK) ** (-0.5)]], jnp.float32)
    return (query_grad, key_grad, value_grad, summed * normalizers)


def solution(mesh):
    in_specs = (
        P("dp", "ctx", "fsdp"),
        P("dp", "ctx", "fsdp"),
        P("dp", "ctx", "fsdp"),
        P("dp", "ctx", "fsdp"),
        P(),
        P(),
        P("dp", "ctx"),
    )
    out_specs = (P("dp", "ctx", "fsdp"), P("dp", "ctx", "fsdp"), P("dp", "ctx", "fsdp"), P())
    return jax.shard_map(shards, mesh=mesh, in_specs=in_specs, out_specs=out_specs, check_vma=False)
```

profile of v0, /device:TPU:1, one launch (start us, length us, event | category | flops | bytes accessed | tf_op | source)
XLA Modules:
  0.0 192.6 jit_solution(5271174465513493600)
XLA Ops:
  0.6 1.1 copy.46
  2.0 1.0 multiply_convert_fusion.3
  3.1 4.7 %collective-permute-start = (bf16[512,2,128]{2,0,1:T(8,128)(2,1)S(1)}, bf16[512,2,128]{2,0,1:T(8,128)(2,1)S(1)}, u32[]{:S(2)}, u32[]{:S(2)}) collective-permute-start(bf16[512,2,128]{2,0,1:T(8,128)(2,1)S(1)} %multiply_convert_fusion.3), channel_id=1, source_target_pairs={{0,4},{4,8},{8,12},{12,16},{16,20},{20,24},{24,28},{28,32},{32,36}... | collective-permute-start | bytes 786440 | tf_op jit(solution)/shard_map/ppermute | solution.py:19
  7.8 3.2 %collective-permute-start.1 = (bf16[512,2,128]{2,0,1:T(8,128)(2,1)S(1)}, bf16[512,2,128]{2,0,1:T(8,128)(2,1)S(1)}, u32[]{:S(2)}, u32[]{:S(2)}) collective-permute-start(bf16[512,2,128]{2,0,1:T(8,128)(2,1)S(1)} %multiply_convert_fusion.3), channel_id=1, source_target_pairs={{0,8},{4,12},{8,16},{12,20},{16,24},{20,28},{24,32},{28,36},{32,40... | collective-permute-start | bytes 786440 | tf_op jit(solution)/shard_map/ppermute | solution.py:19
  11.2 2.2 %collective-permute-start.2 = (bf16[512,2,128]{0,2,1:T(8,128)(2,1)S(1)}, bf16[512,2,128]{0,2,1:T(8,128)(2,1)}, u32[]{:S(2)}, u32[]{:S(2)}) collective-permute-start(bf16[512,2,128]{0,2,1:T(8,128)(2,1)S(1)} %bitcast.196), channel_id=1, source_target_pairs={{0,4},{4,8},{8,12},{12,16},{16,20},{20,24},{24,28},{28,32},{32,36}... | collective-permute-start | bytes 786440 | tf_op jit(solution)/shard_map/ppermute | solution.py:19
  13.4 3.9 %collective-permute-start.3 = (bf16[512,2,128]{0,2,1:T(8,128)(2,1)S(1)}, bf16[512,2,128]{0,2,1:T(8,128)(2,1)}, u32[]{:S(2)}, u32[]{:S(2)}) collective-permute-start(bf16[512,2,128]{0,2,1:T(8,128)(2,1)S(1)} %bitcast.197), channel_id=1, source_target_pairs={{0,8},{4,12},{8,16},{12,20},{16,24},{20,28},{24,32},{28,36},{32,40... | collective-permute-start | bytes 786440 | tf_op jit(solution)/shard_map/ppermute | solution.py:19
  17.3 1.3 copy.48
  19.3 1.1 fusion.19
  20.4 1.0 fusion.6
  21.4 1.0 fusion.7
  22.5 1.0 fusion.8
  23.5 2.3 %divide_convert_fusion = (bf16[2,2,512,512]{2,3,1,0:T(8,128)(2,1)S(1)}, bf16[2,2,512,512]{2,3,1,0:T(8,128)(2,1)S(1)}, bf16[2,2,512,512]{2,3,1,0:T(8,128)(2,1)S(1)}) fusion(f32[2,512,512,2]{2,1,3,0:T(8,128)S(1)} %get-tuple-element.23, f32[2,2,512]{2,1,0:T(2,128)S(1)} %add_add_fusion, pred[512,512]{0,1:T(8,128)(4,1)S(1)} %get-tuple-element.20, ...), kind=kLoop, calls=%fused_computation.12 | loop fusion | flops 9437184 | bytes 19668992 | tf_op jit(solution)/shard_map/convert_element_type | solution.py:72
  26.3 1.4 convolution_add_fusion.1
  27.7 1.6 convolution_bitcast_fusion.1
  29.3 1.6 convolution_bitcast_fusion
  30.9 1.4 fusion.12
  33.1 1.9 fusion.1
  35.0 1.5 convolution_bitcast_fusion.3
  36.5 1.3 collective-permute-start.5
  37.8 1.7 fusion.3
  39.5 1.5 convolution_bitcast_fusion.4
  41.0 5.2 %collective-permute-start.4 = (f32[512,2,128]{2,0,1:T(8,128)}, f32[512,2,128]{2,0,1:T(8,128)}, u32[]{:S(2)}, u32[]{:S(2)}) collective-permute-start(f32[512,2,128]{2,0,1:T(8,128)} %convolution_bitcast_fusion.4), channel_id=1, source_target_pairs={{4,0},{8,4},{12,8},{16,12},{20,16},{24,20},{28,24},{32,28},{36,32}... | collective-permute-start | bytes 1572872 | tf_op jit(solution)/shard_map/ppermute | solution.py:19
  46.8 2.1 %collective-permute-start.6 = (f32[512,2,128]{0,2,1:T(8,128)}, f32[512,2,128]{0,2,1:T(8,128)}, u32[]{:S(2)}, u32[]{:S(2)}) collective-permute-start(f32[512,2,128]{0,2,1:T(8,128)} %convolution_bitcast_fusion.1), channel_id=1, source_target_pairs={{4,0},{8,4},{12,8},{16,12},{20,16},{24,20},{28,24},{32,28},{36,32}... | collective-permute-start | bytes 1572872 | tf_op jit(solution)/shard_map/ppermute | solution.py:19
  48.8 1.5 collective-permute-start.7
  51.6 1.1 multiply_convert_fusion
  52.7 2.0 %copy.81 = bf16[1,512,512]{2,1,0:T(8,128)(2,1)} copy(bf16[1,512,512]{1,2,0:T(8,128)(2,1)} %bitcast.200) | data formatting | bytes 1048576
  54.8 7.5 %collective-permute-done.4 = f32[512,2,128]{2,0,1:T(8,128)} collective-permute-done((f32[512,2,128]{2,0,1:T(8,128)}, f32[512,2,128]{2,0,1:T(8,128)}, u32[]{:S(2)}, u32[]{:S(2)}) %collective-permute-start.4) | collective-permute-done | bytes 524320 | tf_op jit(solution)/shard_map/ppermute | solution.py:19
  62.3 3.5 %multiply_reduce_fusion.3 = (f32[128]{0:T(128)S(1)}, f32[512,2]{0,1:T(2,128)S(1)}, f32[512,2,128]{2,0,1:T(8,128)}) fusion(f32[512,2,128]{2,0,1:T(8,128)} %copy-done.3, f32[512,2]{0,1:T(2,128)S(1)} %add_rsqrt_fusion.1, f32[128]{0:T(128)S(1)} %copy-done.13, f32[512,2,128]{2,0,1:T(8,128)} %collective-permute-done.5, ...), kind=kOutput, calls=%fused_computation.49 | convolution fusion | flops 269482880 | bytes 4727808 | tf_op jit(solution)/shard_map/kgtu,tkgd->ukd/dot_general | solution.py:97
  65.8 120.8 %psum.7 = f32[2,128]{1,0:T(2,128)S(1)} all-reduce(f32[2,128]{1,0:T(2,128)S(1)} %pad_maximum_fusion), channel_id=1, replica_groups=mesh['dp'=2,'ctx'=96,'fsdp'=4] {'dp','ctx','fsdp'}, use_global_device_ids=true, to_apply=%region_10.11 | all-reduce | flops 256 | bytes 2048 | tf_op jit(solution)/shard_map/psum | solution.py:128
  186.6 2.1 %fusion.17 = bf16[512,2,128]{0,2,1:T(8,128)(2,1)S(1)} fusion(f32[512,2,128]{0,2,1:T(8,128)} %collective-permute-done.7, f32[512,2,128]{0,2,1:T(8,128)} %collective-permute-done.6, bf16[2,2,512,512]{2,3,1,0:T(8,128)(2,1)S(1)} %get-tuple-element.18, bf16[512,2,2,128]{0,3,2,1:T(8,128)(2,1)S(1)} %bitcast.189), kind=kOutput, calls=%fused_computation.36 | convolution fusion | flops 268828672 | bytes 3932160 | tf_op jit(solution)/shard_map/kgtu,tkgd->ukd/dot_general | solution.py:100
  188.7 0.8 copy.83
  189.6 1.4 multiply_convert_fusion.2
  (64 shorter events, 5.7 us)
Async XLA Ops:
  0.6 10.4 %copy-start.12 = (bf16[1,512,256]{2,1,0:T(8,128)(2,1)S(1)}, bf16[1,512,256]{2,1,0:T(8,128)(2,1)}, u32[]{:S(2)}) copy-start(bf16[1,512,256]{2,1,0:T(8,128)(2,1)} %param.10) | copy-start | bytes 786436
  1.9 16.8 %copy-start.3 = (f32[512,2,128]{2,0,1:T(8,128)}, f32[512,2,128]{2,0,1:T(8,128)S(1)}, u32[]{:S(2)}) copy-start(f32[512,2,128]{2,0,1:T(8,128)S(1)} %copy.47) | copy-start | bytes 1572868
  2.0 16.7 %copy-start.11 = (bf16[1,512,512]{2,1,0:T(8,128)(2,1)S(1)}, bf16[1,512,512]{2,1,0:T(8,128)(2,1)}, u32[]{:S(2)}) copy-start(bf16[1,512,512]{2,1,0:T(8,128)(2,1)} %param.11) | copy-start | bytes 1572868
  3.0 17.3 %copy-start.5 = (bf16[512,2,128]{2,0,1:T(8,128)(2,1)}, bf16[512,2,128]{2,0,1:T(8,128)(2,1)S(1)}, u32[]{:S(2)}) copy-start(bf16[512,2,128]{2,0,1:T(8,128)(2,1)S(1)} %multiply_convert_fusion.3) | copy-start | bytes 786436
  3.0 15.9 %copy-start.14 = (f32[128]{0:T(128)S(1)}, f32[128]{0:T(128)}, u32[]{:S(2)}) copy-start(f32[128]{0:T(128)} %param.12) | copy-start | bytes 1540
  3.1 18.3 %collective-permute-start = (bf16[512,2,128]{2,0,1:T(8,128)(2,1)S(1)}, bf16[512,2,128]{2,0,1:T(8,128)(2,1)S(1)}, u32[]{:S(2)}, u32[]{:S(2)}) collective-permute-start(bf16[512,2,128]{2,0,1:T(8,128)(2,1)S(1)} %multiply_convert_fusion.3), channel_id=1, source_target_pairs={{0,4},{4,8},{8,12},{12,16},{16,20},{20,24},{24,28},{28,32},{32,36}... | collective-permute-start | bytes 786440 | tf_op jit(solution)/shard_map/ppermute | solution.py:19
  7.8 14.7 %collective-permute-start.1 = (bf16[512,2,128]{2,0,1:T(8,128)(2,1)S(1)}, bf16[512,2,128]{2,0,1:T(8,128)(2,1)S(1)}, u32[]{:S(2)}, u32[]{:S(2)}) collective-permute-start(bf16[512,2,128]{2,0,1:T(8,128)(2,1)S(1)} %multiply_convert_fusion.3), channel_id=1, source_target_pairs={{0,8},{4,12},{8,16},{12,20},{16,24},{20,28},{24,32},{28,36},{32,40... | collective-permute-start | bytes 786440 | tf_op jit(solution)/shard_map/ppermute | solution.py:19
  11.2 15.1 %collective-permute-start.2 = (bf16[512,2,128]{0,2,1:T(8,128)(2,1)S(1)}, bf16[512,2,128]{0,2,1:T(8,128)(2,1)}, u32[]{:S(2)}, u32[]{:S(2)}) collective-permute-start(bf16[512,2,128]{0,2,1:T(8,128)(2,1)S(1)} %bitcast.196), channel_id=1, source_target_pairs={{0,4},{4,8},{8,12},{12,16},{16,20},{20,24},{24,28},{28,32},{32,36}... | collective-permute-start | bytes 786440 | tf_op jit(solution)/shard_map/ppermute | solution.py:19
  13.4 17.5 %collective-permute-start.3 = (bf16[512,2,128]{0,2,1:T(8,128)(2,1)S(1)}, bf16[512,2,128]{0,2,1:T(8,128)(2,1)}, u32[]{:S(2)}, u32[]{:S(2)}) collective-permute-start(bf16[512,2,128]{0,2,1:T(8,128)(2,1)S(1)} %bitcast.197), channel_id=1, source_target_pairs={{0,8},{4,12},{8,16},{12,20},{16,24},{20,28},{24,32},{28,36},{32,40... | collective-permute-start | bytes 786440 | tf_op jit(solution)/shard_map/ppermute | solution.py:19
  18.5 1.8 copy-start
  18.5 0.7 copy-start.15
  21.4 1.0 copy-start.9
  22.5 1.0 copy-start.7
  33.1 13.2 %copy-start.2 = (bf16[2,2,512,512]{2,3,1,0:T(8,128)(2,1)}, bf16[2,2,512,512]{2,3,1,0:T(8,128)(2,1)S(1)}, u32[]{:S(2)}) copy-start(bf16[2,2,512,512]{2,3,1,0:T(8,128)(2,1)S(1)} %fusion.5) | copy-start | bytes 6291460
  36.5 18.3 %collective-permute-start.5 = (f32[512,2,128]{2,0,1:T(8,128)}, f32[512,2,128]{2,0,1:T(8,128)}, u32[]{:S(2)}, u32[]{:S(2)}) collective-permute-start(f32[512,2,128]{2,0,1:T(8,128)} %convolution_bitcast_fusion.3), channel_id=1, source_target_pairs={{8,0},{12,4},{16,8},{20,12},{24,16},{28,20},{32,24},{36,28},{40,32... | collective-permute-start | bytes 1572872 | tf_op jit(solution)/shard_map/ppermute | solution.py:19
  39.5 6.7 %copy-start.6 = (bf16[512,2,128]{2,0,1:T(8,128)(2,1)S(1)}, bf16[512,2,128]{2,0,1:T(8,128)(2,1)}, u32[]{:S(2)}) copy-start(bf16[512,2,128]{2,0,1:T(8,128)(2,1)} %copy-done.5) | copy-start | bytes 786436
  41.0 9.3 %copy-start.10 = (bf16[512,2,128]{2,0,1:T(8,128)(2,1)S(1)}, bf16[512,2,128]{2,0,1:T(8,128)(2,1)}, u32[]{:S(2)}) copy-start(bf16[512,2,128]{2,0,1:T(8,128)(2,1)} %copy-done.9) | copy-start | bytes 786436
  41.0 21.3 %collective-permute-start.4 = (f32[512,2,128]{2,0,1:T(8,128)}, f32[512,2,128]{2,0,1:T(8,128)}, u32[]{:S(2)}, u32[]{:S(2)}) collective-permute-start(f32[512,2,128]{2,0,1:T(8,128)} %convolution_bitcast_fusion.4), channel_id=1, source_target_pairs={{4,0},{8,4},{12,8},{16,12},{20,16},{24,20},{28,24},{32,28},{36,32}... | collective-permute-start | bytes 1572872 | tf_op jit(solution)/shard_map/ppermute | solution.py:19
  46.7 4.1 %copy-start.1 = (f32[1,512,512]{1,2,0:T(8,128)S(1)}, f32[1,512,512]{1,2,0:T(8,128)}, u32[]{:S(2)}) copy-start(f32[1,512,512]{1,2,0:T(8,128)} %copy-done) | copy-start | bytes 3145732
  46.8 4.1 %copy-start.8 = (bf16[512,2,128]{2,0,1:T(8,128)(2,1)S(1)}, bf16[512,2,128]{2,0,1:T(8,128)(2,1)}, u32[]{:S(2)}) copy-start(bf16[512,2,128]{2,0,1:T(8,128)(2,1)} %copy-done.7) | copy-start | bytes 786436
  46.8 139.9 %collective-permute-start.6 = (f32[512,2,128]{0,2,1:T(8,128)}, f32[512,2,128]{0,2,1:T(8,128)}, u32[]{:S(2)}, u32[]{:S(2)}) collective-permute-start(f32[512,2,128]{0,2,1:T(8,128)} %convolution_bitcast_fusion.1), channel_id=1, source_target_pairs={{4,0},{8,4},{12,8},{16,12},{20,16},{24,20},{28,24},{32,28},{36,32}... | collective-permute-start | bytes 1572872 | tf_op jit(solution)/shard_map/ppermute | solution.py:19
  48.8 137.8 %collective-permute-start.7 = (f32[512,2,128]{0,2,1:T(8,128)}, f32[512,2,128]{0,2,1:T(8,128)}, u32[]{:S(2)}, u32[]{:S(2)}) collective-permute-start(f32[512,2,128]{0,2,1:T(8,128)} %convolution_bitcast_fusion), channel_id=1, source_target_pairs={{8,0},{12,4},{16,8},{20,12},{24,16},{28,20},{32,24},{36,28},{40,32... | collective-permute-start | bytes 1572872 | tf_op jit(solution)/shard_map/ppermute | solution.py:19
  51.6 10.7 %copy-start.13 = (f32[128]{0:T(128)S(1)}, f32[128]{0:T(128)}, u32[]{:S(2)}) copy-start(f32[128]{0:T(128)} %param.13) | copy-start | bytes 1540
  186.6 2.9 %copy-start.4 = (f32[512,2,128]{2,0,1:T(8,128)S(1)}, f32[512,2,128]{2,0,1:T(8,128)}, u32[]{:S(2)}) copy-start(f32[512,2,128]{2,0,1:T(8,128)} %copy-done.3) | copy-start | bytes 1572868
  188.7 3.2 %copy-start.16 = (f32[2]{0:T(128)S(1)}, f32[2]{0:T(128)}, u32[]{:S(2)}) copy-start(f32[2]{0:T(128)} %constant.37) | copy-start | bytes 28
where the time goes:
time: 193 us
  blocking collectives  121 us (63%)
  matrix products  24.2 us (13%)
  starting transfers between devices  24.1 us (12%)
  other arithmetic  7.89 us (4%)
  waiting for transfers between devices  7.57 us (4%)
  local copies, waits for them, and re-layouts  6.95 us (4%)
    psum x1, blocking collectives, shards(): summed = lax.psum(partial_sums, ('dp', 'ctx', 'fsdp'))  121 us
    ppermute x8, starting transfers between devices, passed_along(): lax.ppermute(value, axis, [(source, source + steps) for source in range(i...  24.1 us
    ppermute x8, waiting for transfers between devices, passed_along(): lax.ppermute(value, axis, [(source, source + steps) for source in range(i...  7.57 us
    dot_general x3, matrix products, shards(): jnp.einsum('kgtu,tkgd->ukd', dscore, query_n, preferred_element_type=jnp....  6.51 us
    unnamed x40, local copies, waits for them, and re-layouts  5.42 us
    dot_general x3, matrix products, shards(): jnp.einsum('kgtu,tkgd->ukd', prob, grads_in, preferred_element_type=jnp.f...  5.28 us
    dot_general x3, matrix products, shards(): jnp.einsum('tkgd,ukd->kgtu', grads_in, value_block, preferred_element_typ...  4.34 us
  transfers between devices with their start and end apart: 8, of which 1 were waited for; matrix products, arithmetic and copies ran while one was open for 13% of the time, Pallas kernels for 0%

commit v1 on v0

--- a/solution.py
+++ b/solution.py
@@ -17,6 +17,40 @@
     count = lax.axis_size(axis)
     initial, last = (max(0, -steps), min(count, count - steps))
     return lax.ppermute(value, axis, [(source, source + steps) for source in range(initial, last)])
+
+
+def exchanged_sum(value, axis, stride):
+    count = lax.axis_size(axis)
+    return value + lax.ppermute(value, axis, [(source, source ^ stride) for source in range(count)])
+
+
+def three_way_sum(value, axis, stride):
+    count = lax.axis_size(axis)
+    digit = (lax.axis_index(axis) // stride) % 3
+    received = [value]
+    for shift in (1, 2):
+        pairs = []
+        for source in range(count):
+            place = (source // stride) % 3
+            pairs.append((source, source + ((place + shift) % 3 - place) * stride))
+        received.append(lax.ppermute(value, axis, pairs))
+    ordered = []
+    for place in range(3):
+        pick = received[0]
+        for shift in (1, 2):
+            pick = jnp.where((digit - shift) % 3 == place, received[shift], pick)
+        pick = jnp.where(digit == place, received[0], pick)
+        ordered.append(pick)
+    return ordered[0] + ordered[1] + ordered[2]
+
+
+def total_over_devices(value):
+    value = exchanged_sum(value, "fsdp", 1)
+    value = exchanged_sum(value, "fsdp", 2)
+    value = exchanged_sum(value, "dp", 1)
+    for stride in (1, 2, 4, 8, 16):
+        value = exchanged_sum(value, "ctx", stride)
+    return three_way_sum(value, "ctx", 32)
 
 
 def normalize(raw, gain, factor):
@@ -125,7 +159,7 @@
             jnp.sum(dkey_n * key_hat, axis=(0, 1)),
         ]
     )
-    summed = lax.psum(partial_sums, ("dp", "ctx", "fsdp"))
+    summed = total_over_devices(partial_sums)
     counted = lax.axis_size("dp") * lax.axis_size("ctx") * tokens
     normalizers = jnp.array([[(counted * HQ) ** (-0.5)], [(counted * HK) ** (-0.5)]], jnp.float32)
     return (query_grad, key_grad, value_grad, summed * normalizers)

time: 193 us -> 150 us (0.78)
  the two profiles are of different devices: /device:TPU:1 before, /device:TPU:16 now
where the time goes in v1:
time: 150 us; the launch traced here: 149 us
  starting transfers between devices  88.9 us (59%)
  matrix products  21.3 us (14%)
  waiting for transfers between devices  20.5 us (14%)
  local copies, waits for them, and re-layouts  8.83 us (6%)
  other arithmetic  8.32 us (6%)
    ppermute x8, starting transfers between devices, exchanged_sum(): lax.ppermute(value, axis, [(source, source ^ stride) for source in range(...  58 us
    ppermute x8, starting transfers between devices, passed_along(): lax.ppermute(value, axis, [(source, source + steps) for source in range(i...  22.8 us
    ppermute x8, waiting for transfers between devices, passed_along(): lax.ppermute(value, axis, [(source, source + steps) for source in range(i...  8.83 us
    ppermute x2, starting transfers between devices, three_way_sum(): received.append(lax.ppermute(value, axis, pairs))  8.04 us
    unnamed x34, local copies, waits for them, and re-layouts  7.3 us
    ppermute x8, waiting for transfers between devices, exchanged_sum(): lax.ppermute(value, axis, [(source, source ^ stride) for source in range(...  6.38 us
    ppermute x2, waiting for transfers between devices, three_way_sum(): received.append(lax.ppermute(value, axis, pairs))  5.26 us
    dot_general x3, matrix products, shards(): jnp.einsum('kgtu,tkgd->ukd', prob, grads_in, preferred_element_type=jnp.f...  5.21 us
  transfers between devices with their start and end apart: 18, of which 8 were waited for; matrix products, arithmetic and copies ran while one was open for 19% of the time, Pallas kernels for 0%

profile of v1, /device:TPU:16, one launch (start us, length us, event | category | flops | bytes accessed | tf_op | source)
XLA Modules:
  0.0 149.1 jit_solution(2799466374843967612)
XLA Ops:
  2.9 2.1 %collective-permute-start = (bf16[512,2,128]{2,0,1:T(8,128)(2,1)S(1)}, bf16[512,2,128]{2,0,1:T(8,128)(2,1)S(1)}, u32[]{:S(2)}, u32[]{:S(2)}) collective-permute-start(bf16[512,2,128]{2,0,1:T(8,128)(2,1)S(1)} %multiply_convert_fusion.3), channel_id=1, source_target_pairs={{0,4},{4,8},{8,12},{12,16},{16,20},{20,24},{24,28},{28,32},{32,36}... | collective-permute-start | bytes 786440 | tf_op jit(solution)/shard_map/ppermute | solution.py:19
  5.0 3.5 %collective-permute-start.1 = (bf16[512,2,128]{2,0,1:T(8,128)(2,1)S(1)}, bf16[512,2,128]{2,0,1:T(8,128)(2,1)S(1)}, u32[]{:S(2)}, u32[]{:S(2)}) collective-permute-start(bf16[512,2,128]{2,0,1:T(8,128)(2,1)S(1)} %multiply_convert_fusion.3), channel_id=1, source_target_pairs={{0,8},{4,12},{8,16},{12,20},{16,24},{20,28},{24,32},{28,36},{32,40... | collective-permute-start | bytes 786440 | tf_op jit(solution)/shard_map/ppermute | solution.py:19
  8.6 4.5 %collective-permute-start.2 = (bf16[512,2,128]{0,2,1:T(8,128)(2,1)S(1)}, bf16[512,2,128]{0,2,1:T(8,128)(2,1)}, u32[]{:S(2)}, u32[]{:S(2)}) collective-permute-start(bf16[512,2,128]{0,2,1:T(8,128)(2,1)S(1)} %bitcast.196), channel_id=1, source_target_pairs={{0,4},{4,8},{8,12},{12,16},{16,20},{20,24},{24,28},{28,32},{32,36}... | collective-permute-start | bytes 786440 | tf_op jit(solution)/shard_map/ppermute | solution.py:19
  13.1 2.6 %collective-permute-start.3 = (bf16[512,2,128]{0,2,1:T(8,128)(2,1)S(1)}, bf16[512,2,128]{0,2,1:T(8,128)(2,1)}, u32[]{:S(2)}, u32[]{:S(2)}) collective-permute-start(bf16[512,2,128]{0,2,1:T(8,128)(2,1)S(1)} %bitcast.197), channel_id=1, source_target_pairs={{0,8},{4,12},{8,16},{12,20},{16,24},{20,28},{24,32},{28,36},{32,40... | collective-permute-start | bytes 786440 | tf_op jit(solution)/shard_map/ppermute | solution.py:19
  23.2 2.3 %divide_convert_fusion = (bf16[2,2,512,512]{2,3,1,0:T(8,128)(2,1)S(1)}, bf16[2,2,512,512]{2,3,1,0:T(8,128)(2,1)S(1)}, bf16[2,2,512,512]{2,3,1,0:T(8,128)(2,1)S(1)}) fusion(f32[2,512,512,2]{2,1,3,0:T(8,128)S(1)} %get-tuple-element.23, f32[2,2,512]{2,1,0:T(2,128)S(1)} %add_add_fusion, pred[512,512]{0,1:T(8,128)(4,1)S(1)} %get-tuple-element.20, ...), kind=kLoop, calls=%fused_computation.12 | loop fusion | flops 9437184 | bytes 19668992 | tf_op jit(solution)/shard_map/convert_element_type | solution.py:106
  29.5 1.7 %fusion.1 = bf16[2,2,512,512]{2,3,1,0:T(8,128)(2,1)S(1)} fusion(bf16[2,2,512,512]{2,3,1,0:T(8,128)(2,1)S(1)} %get-tuple-element.16, bf16[512,2,2,128]{0,3,2,1:T(8,128)(2,1)S(1)} %bitcast.185, f32[2,2,512]{2,1,0:T(2,128)S(1)} %bitcast.204, bf16[512,2,128]{0,2,1:T(8,128)(2,1)} %collective-permute-done.3), kind=kOutput, calls=%fused_computation.2 | convolution fusion | flops 272629760 | bytes 4988928 | tf_op jit(solution)/shard_map/tkgd,ukd->kgtu/dot_general | solution.py:124
  31.9 3.3 %collective-permute-start.5 = (f32[512,2,128]{2,0,1:T(8,128)S(1)}, f32[512,2,128]{2,0,1:T(8,128)S(1)}, u32[]{:S(2)}, u32[]{:S(2)}) collective-permute-start(f32[512,2,128]{2,0,1:T(8,128)S(1)} %convolution_bitcast_fusion.3), channel_id=1, source_target_pairs={{8,0},{12,4},{16,8},{20,12},{24,16},{28,20},{32,24},{36,28},{40,32... | collective-permute-start | bytes 1572872 | tf_op jit(solution)/shard_map/ppermute | solution.py:19
  35.2 1.7 %fusion.3 = bf16[2,2,512,512]{2,3,1,0:T(8,128)(2,1)S(1)} fusion(bf16[2,2,512,512]{2,3,1,0:T(8,128)(2,1)S(1)} %get-tuple-element.17, bf16[512,2,2,128]{0,3,2,1:T(8,128)(2,1)S(1)} %bitcast.186, f32[2,2,512]{2,1,0:T(2,128)S(1)} %bitcast.205, bf16[512,2,128]{0,2,1:T(8,128)(2,1)} %collective-permute-done.2), kind=kOutput, calls=%fused_computation.5 | convolution fusion | flops 272629760 | bytes 4988928 | tf_op jit(solution)/shard_map/tkgd,ukd->kgtu/dot_general | solution.py:124
  37.6 2.2 %collective-permute-start.4 = (f32[512,2,128]{2,0,1:T(8,128)S(1)}, f32[512,2,128]{2,0,1:T(8,128)S(1)}, u32[]{:S(2)}, u32[]{:S(2)}) collective-permute-start(f32[512,2,128]{2,0,1:T(8,128)S(1)} %convolution_bitcast_fusion.4), channel_id=1, source_target_pairs={{4,0},{8,4},{12,8},{16,12},{20,16},{24,20},{28,24},{32,28},{36,32}... | collective-permute-start | bytes 1572872 | tf_op jit(solution)/shard_map/ppermute | solution.py:19
  41.7 1.7 %multiply_reduce_fusion = (f32[128]{0:T(128)S(1)}, f32[512,2,2]{0,2,1:T(2,128)S(1)}, f32[512,2,2,128]{0,3,2,1:T(8,128)}) fusion(f32[512,2,2,128]{0,3,2,1:T(8,128)S(1)} %bitcast.193, f32[512,2,2]{0,2,1:T(2,128)S(1)} %add_rsqrt_fusion, f32[128]{0:T(128)S(1)} %copy-done.11, f32[2,128,2,512]{3,1,2,0:T(8,128)S(1)} %convolution_add_fusion.3, ...), kind=kOutput, calls=%fused_computation.37 | convolution fusion | flops 270530432 | bytes 5522432 | tf_op jit(solution)/shard_map/kgtu,ukd->tkgd/dot_general | solution.py:128
  43.3 4.3 %collective-permute-done.5 = f32[512,2,128]{2,0,1:T(8,128)S(1)} collective-permute-done((f32[512,2,128]{2,0,1:T(8,128)S(1)}, f32[512,2,128]{2,0,1:T(8,128)S(1)}, u32[]{:S(2)}, u32[]{:S(2)}) %collective-permute-start.5) | collective-permute-done | bytes 524320 | tf_op jit(solution)/shard_map/ppermute | solution.py:19
  47.7 4.5 %collective-permute-done.4 = f32[512,2,128]{2,0,1:T(8,128)S(1)} collective-permute-done((f32[512,2,128]{2,0,1:T(8,128)S(1)}, f32[512,2,128]{2,0,1:T(8,128)S(1)}, u32[]{:S(2)}, u32[]{:S(2)}) %collective-permute-start.4) | collective-permute-done | bytes 524320 | tf_op jit(solution)/shard_map/ppermute | solution.py:19
  52.2 1.5 %multiply_reduce_fusion.3 = (f32[128]{0:T(128)S(1)}, f32[512,2]{0,1:T(2,128)S(1)}, f32[512,2,128]{2,0,1:T(8,128)}) fusion(f32[512,2,128]{2,0,1:T(8,128)S(1)} %copy.47, f32[512,2]{0,1:T(2,128)S(1)} %add_rsqrt_fusion.1, f32[128]{0:T(128)S(1)} %copy-done.10, f32[512,2,128]{2,0,1:T(8,128)S(1)} %collective-permute-done.5, ...), kind=kOutput, calls=%fused_computation.49 | convolution fusion | flops 269482880 | bytes 4727808 | tf_op jit(solution)/shard_map/kgtu,tkgd->ukd/dot_general | solution.py:131
  53.7 3.4 %collective-permute-start.8 = (f32[2,128]{1,0:T(2,128)S(1)}, f32[2,128]{1,0:T(2,128)S(1)}, u32[]{:S(2)}, u32[]{:S(2)}) collective-permute-start(f32[2,128]{1,0:T(2,128)S(1)} %pad_maximum_fusion), channel_id=1, source_target_pairs={{0,1},{1,0},{2,3},{3,2},{4,5},{5,4},{6,7},{7,6},{8,9},{9,8},{10,11... | collective-permute-start | bytes 3080 | tf_op jit(solution)/shard_map/ppermute | solution.py:24
  57.1 1.6 %convolution_bitcast_fusion.1 = f32[512,2,128]{0,2,1:T(8,128)} fusion(bf16[2,2,512,512]{2,3,1,0:T(8,128)(2,1)S(1)} %get-tuple-element.17, bf16[512,2,2,128]{0,3,2,1:T(8,128)(2,1)S(1)} %bitcast.187), kind=kOutput, calls=%fused_computation.27 | convolution fusion | flops 268435456 | bytes 3145728 | tf_op jit(solution)/shard_map/kgtu,tkgd->ukd/dot_general | solution.py:134
  59.2 4.9 %collective-permute-start.9 = (f32[2,128]{1,0:T(2,128)S(1)}, f32[2,128]{1,0:T(2,128)S(1)}, u32[]{:S(2)}, u32[]{:S(2)}) collective-permute-start(f32[2,128]{1,0:T(2,128)S(1)} %fusion.35), channel_id=1, source_target_pairs={{0,2},{1,3},{2,0},{3,1},{4,6},{5,7},{6,4},{7,5},{8,10},{9,11},{10,... | collective-permute-start | bytes 3080 | tf_op jit(solution)/shard_map/ppermute | solution.py:24
  64.1 1.6 %convolution_bitcast_fusion = f32[512,2,128]{0,2,1:T(8,128)} fusion(bf16[2,2,512,512]{2,3,1,0:T(8,128)(2,1)S(1)} %get-tuple-element.16, bf16[512,2,2,128]{0,3,2,1:T(8,128)(2,1)S(1)} %bitcast.188), kind=kOutput, calls=%fused_computation.26 | convolution fusion | flops 268435456 | bytes 3145728 | tf_op jit(solution)/shard_map/kgtu,tkgd->ukd/dot_general | solution.py:134
  65.7 2.5 %collective-permute-start.6 = (f32[512,2,128]{0,2,1:T(8,128)}, f32[512,2,128]{0,2,1:T(8,128)}, u32[]{:S(2)}, u32[]{:S(2)}) collective-permute-start(f32[512,2,128]{0,2,1:T(8,128)} %convolution_bitcast_fusion.1), channel_id=1, source_target_pairs={{4,0},{8,4},{12,8},{16,12},{20,16},{24,20},{28,24},{32,28},{36,32}... | collective-permute-start | bytes 1572872 | tf_op jit(solution)/shard_map/ppermute | solution.py:19
  68.2 2.2 %collective-permute-start.7 = (f32[512,2,128]{0,2,1:T(8,128)}, f32[512,2,128]{0,2,1:T(8,128)}, u32[]{:S(2)}, u32[]{:S(2)}) collective-permute-start(f32[512,2,128]{0,2,1:T(8,128)} %convolution_bitcast_fusion), channel_id=1, source_target_pairs={{8,0},{12,4},{16,8},{20,12},{24,16},{28,20},{32,24},{36,28},{40,32... | collective-permute-start | bytes 1572872 | tf_op jit(solution)/shard_map/ppermute | solution.py:19
  70.5 15.1 %collective-permute-start.10 = (f32[2,128]{1,0:T(2,128)S(1)}, f32[2,128]{1,0:T(2,128)S(1)}, u32[]{:S(2)}, u32[]{:S(2)}) collective-permute-start(f32[2,128]{1,0:T(2,128)S(1)} %fusion.63), channel_id=1, source_target_pairs={{0,384},{384,0},{1,385},{385,1},{2,386},{386,2},{3,387},{387,3},{4... | collective-permute-start | bytes 3080 | tf_op jit(solution)/shard_map/ppermute | solution.py:24
  87.2 1.9 %collective-permute-start.11 = (f32[2,128]{1,0:T(2,128)S(1)}, f32[2,128]{1,0:T(2,128)S(1)}, u32[]{:S(2)}, u32[]{:S(2)}) collective-permute-start(f32[2,128]{1,0:T(2,128)S(1)} %add.180), channel_id=1, source_target_pairs={{0,4},{4,0},{8,12},{12,8},{16,20},{20,16},{24,28},{28,24},{32,36},... | collective-permute-start | bytes 3080 | tf_op jit(solution)/shard_map/ppermute | solution.py:24
  90.2 3.6 %collective-permute-start.12 = (f32[2,128]{1,0:T(2,128)S(1)}, f32[2,128]{1,0:T(2,128)S(1)}, u32[]{:S(2)}, u32[]{:S(2)}) collective-permute-start(f32[2,128]{1,0:T(2,128)S(1)} %add.181), channel_id=1, source_target_pairs={{0,8},{4,12},{8,0},{12,4},{16,24},{20,28},{24,16},{28,20},{32,40},... | collective-permute-start | bytes 3080 | tf_op jit(solution)/shard_map/ppermute | solution.py:24
  93.9 1.8 %collective-permute-done.12 = f32[2,128]{1,0:T(2,128)S(1)} collective-permute-done((f32[2,128]{1,0:T(2,128)S(1)}, f32[2,128]{1,0:T(2,128)S(1)}, u32[]{:S(2)}, u32[]{:S(2)}) %collective-permute-start.12) | collective-permute-done | bytes 1056 | tf_op jit(solution)/shard_map/ppermute | solution.py:24
  95.7 1.9 %collective-permute-start.13 = (f32[2,128]{1,0:T(2,128)S(1)}, f32[2,128]{1,0:T(2,128)S(1)}, u32[]{:S(2)}, u32[]{:S(2)}) collective-permute-start(f32[2,128]{1,0:T(2,128)S(1)} %add.182), channel_id=1, source_target_pairs={{0,16},{4,20},{8,24},{12,28},{16,0},{20,4},{24,8},{28,12},{32,48},... | collective-permute-start | bytes 3080 | tf_op jit(solution)/shard_map/ppermute | solution.py:24
  97.6 2.6 %multiply_convert_fusion = bf16[512,2,2,128]{0,3,2,1:T(8,128)(2,1)} fusion(f32[512,2,2,128]{0,3,2,1:T(8,128)} %get-tuple-element.28, f32[512,2,2,128]{0,3,2,1:T(8,128)} %bitcast.192, f32[512,2,2]{0,2,1:T(2,128)S(1)} %broadcast_multiply_fusion, f32[128]{0:T(128)S(1)} %copy-done.11, f32[512,2,2]{0,2,1:T(2,128)S(1)} %add_rsqrt_fusion), kind=kLoop, calls=%fused_computation.38 | loop fusion | flops 1835008 | bytes 2638336 | tf_op jit(solution)/shard_map/convert_element_type | solution.py:147
  100.2 2.0 %copy.81 = bf16[1,512,512]{2,1,0:T(8,128)(2,1)} copy(bf16[1,512,512]{1,2,0:T(8,128)(2,1)} %bitcast.200) | data formatting | bytes 1048576
  102.3 7.4 %collective-permute-start.14 = (f32[2,128]{1,0:T(2,128)S(1)}, f32[2,128]{1,0:T(2,128)S(1)}, u32[]{:S(2)}, u32[]{:S(2)}) collective-permute-start(f32[2,128]{1,0:T(2,128)S(1)} %add.183), channel_id=1, source_target_pairs={{0,32},{4,36},{8,40},{12,44},{16,48},{20,52},{24,56},{28,60},{32,0... | collective-permute-start | bytes 3080 | tf_op jit(solution)/shard_map/ppermute | solution.py:24
  109.8 2.0 %fusion.17 = bf16[512,2,128]{0,2,1:T(8,128)(2,1)S(1)} fusion(f32[512,2,128]{0,2,1:T(8,128)} %collective-permute-done.7, f32[512,2,128]{0,2,1:T(8,128)} %collective-permute-done.6, bf16[2,2,512,512]{2,3,1,0:T(8,128)(2,1)S(1)} %get-tuple-element.18, bf16[512,2,2,128]{0,3,2,1:T(8,128)(2,1)S(1)} %bitcast.189), kind=kOutput, calls=%fused_computation.36 | convolution fusion | flops 268828672 | bytes 3932160 | tf_op jit(solution)/shard_map/kgtu,tkgd->ukd/dot_general | solution.py:134
  111.8 19.6 %collective-permute-start.15 = (f32[2,128]{1,0:T(2,128)S(1)}, f32[2,128]{1,0:T(2,128)S(1)}, u32[]{:S(2)}, u32[]{:S(2)}) collective-permute-start(f32[2,128]{1,0:T(2,128)S(1)} %add.184), channel_id=1, source_target_pairs={{0,64},{4,68},{8,72},{12,76},{16,80},{20,84},{24,88},{28,92},{32,9... | collective-permute-start | bytes 3080 | tf_op jit(solution)/shard_map/ppermute | solution.py:24
  133.0 6.1 %collective-permute-start.16 = (f32[2,128]{1,0:T(2,128)S(1)}, f32[2,128]{1,0:T(2,128)S(1)}, u32[]{:S(2)}, u32[]{:S(2)}) collective-permute-start(f32[2,128]{1,0:T(2,128)S(1)} %add.185), channel_id=1, source_target_pairs={{0,256},{4,260},{8,264},{12,268},{16,272},{20,276},{24,280},{28,28... | collective-permute-start | bytes 3080 | tf_op jit(solution)/shard_map/ppermute | solution.py:36
  139.1 1.9 %collective-permute-start.17 = (f32[2,128]{1,0:T(2,128)S(1)}, f32[2,128]{1,0:T(2,128)S(1)}, u32[]{:S(2)}, u32[]{:S(2)}) collective-permute-start(f32[2,128]{1,0:T(2,128)S(1)} %add.185), channel_id=1, source_target_pairs={{0,128},{4,132},{8,136},{12,140},{16,144},{20,148},{24,152},{28,15... | collective-permute-start | bytes 3080 | tf_op jit(solution)/shard_map/ppermute | solution.py:36
  143.2 5.3 %collective-permute-done.17 = f32[2,128]{1,0:T(2,128)S(1)} collective-permute-done((f32[2,128]{1,0:T(2,128)S(1)}, f32[2,128]{1,0:T(2,128)S(1)}, u32[]{:S(2)}, u32[]{:S(2)}) %collective-permute-start.17) | collective-permute-done | bytes 1056 | tf_op jit(solution)/shard_map/ppermute | solution.py:36
  (85 shorter events, 24.3 us)
Async XLA Ops:
  0.6 7.8 %copy-start.9 = (bf16[1,512,256]{2,1,0:T(8,128)(2,1)S(1)}, bf16[1,512,256]{2,1,0:T(8,128)(2,1)}, u32[]{:S(2)}) copy-start(bf16[1,512,256]{2,1,0:T(8,128)(2,1)} %param.10) | copy-start | bytes 786436
  2.9 17.1 %copy-start.2 = (bf16[512,2,128]{2,0,1:T(8,128)(2,1)}, bf16[512,2,128]{2,0,1:T(8,128)(2,1)S(1)}, u32[]{:S(2)}) copy-start(bf16[512,2,128]{2,0,1:T(8,128)(2,1)S(1)} %multiply_convert_fusion.3) | copy-start | bytes 786436
  2.9 15.8 %copy-start.11 = (f32[128]{0:T(128)S(1)}, f32[128]{0:T(128)}, u32[]{:S(2)}) copy-start(f32[128]{0:T(128)} %param.12) | copy-start | bytes 1540
  2.9 18.1 %collective-permute-start = (bf16[512,2,128]{2,0,1:T(8,128)(2,1)S(1)}, bf16[512,2,128]{2,0,1:T(8,128)(2,1)S(1)}, u32[]{:S(2)}, u32[]{:S(2)}) collective-permute-start(bf16[512,2,128]{2,0,1:T(8,128)(2,1)S(1)} %multiply_convert_fusion.3), channel_id=1, source_target_pairs={{0,4},{4,8},{8,12},{12,16},{16,20},{20,24},{24,28},{28,32},{32,36}... | collective-permute-start | bytes 786440 | tf_op jit(solution)/shard_map/ppermute | solution.py:19
  5.0 17.1 %collective-permute-start.1 = (bf16[512,2,128]{2,0,1:T(8,128)(2,1)S(1)}, bf16[512,2,128]{2,0,1:T(8,128)(2,1)S(1)}, u32[]{:S(2)}, u32[]{:S(2)}) collective-permute-start(bf16[512,2,128]{2,0,1:T(8,128)(2,1)S(1)} %multiply_convert_fusion.3), channel_id=1, source_target_pairs={{0,8},{4,12},{8,16},{12,20},{16,24},{20,28},{24,32},{28,36},{32,40... | collective-permute-start | bytes 786440 | tf_op jit(solution)/shard_map/ppermute | solution.py:19
  8.6 17.3 %collective-permute-start.2 = (bf16[512,2,128]{0,2,1:T(8,128)(2,1)S(1)}, bf16[512,2,128]{0,2,1:T(8,128)(2,1)}, u32[]{:S(2)}, u32[]{:S(2)}) collective-permute-start(bf16[512,2,128]{0,2,1:T(8,128)(2,1)S(1)} %bitcast.196), channel_id=1, source_target_pairs={{0,4},{4,8},{8,12},{12,16},{16,20},{20,24},{24,28},{28,32},{32,36}... | collective-permute-start | bytes 786440 | tf_op jit(solution)/shard_map/ppermute | solution.py:19
  13.1 14.2 %collective-permute-start.3 = (bf16[512,2,128]{0,2,1:T(8,128)(2,1)S(1)}, bf16[512,2,128]{0,2,1:T(8,128)(2,1)}, u32[]{:S(2)}, u32[]{:S(2)}) collective-permute-start(bf16[512,2,128]{0,2,1:T(8,128)(2,1)S(1)} %bitcast.197), channel_id=1, source_target_pairs={{0,8},{4,12},{8,16},{12,20},{16,24},{20,28},{24,32},{28,36},{32,40... | collective-permute-start | bytes 786440 | tf_op jit(solution)/shard_map/ppermute | solution.py:19
  17.0 3.0 %copy-start = (f32[1,512,512]{1,2,0:T(8,128)}, f32[1,512,512]{1,2,0:T(8,128)S(1)}, u32[]{:S(2)}) copy-start(f32[1,512,512]{1,2,0:T(8,128)S(1)} %copy.48) | copy-start | bytes 3145732
  17.0 1.8 %copy-start.12 = (s32[1,512]{1,0:T(1,128)S(1)}, s32[1,512]{1,0:T(1,128)}, u32[]{:S(2)}) copy-start(s32[1,512]{1,0:T(1,128)} %param.14) | copy-start | bytes 6148
  21.0 1.0 copy-start.7
  22.1 1.0 copy-start.5
  31.9 15.7 %collective-permute-start.5 = (f32[512,2,128]{2,0,1:T(8,128)S(1)}, f32[512,2,128]{2,0,1:T(8,128)S(1)}, u32[]{:S(2)}, u32[]{:S(2)}) collective-permute-start(f32[512,2,128]{2,0,1:T(8,128)S(1)} %convolution_bitcast_fusion.3), channel_id=1, source_target_pairs={{8,0},{12,4},{16,8},{20,12},{24,16},{28,20},{32,24},{36,28},{40,32... | collective-permute-start | bytes 1572872 | tf_op jit(solution)/shard_map/ppermute | solution.py:19
  36.9 3.0 %copy-start.3 = (bf16[512,2,128]{2,0,1:T(8,128)(2,1)S(1)}, bf16[512,2,128]{2,0,1:T(8,128)(2,1)}, u32[]{:S(2)}) copy-start(bf16[512,2,128]{2,0,1:T(8,128)(2,1)} %copy-done.2) | copy-start | bytes 786436
  37.6 2.8 %copy-start.8 = (bf16[512,2,128]{2,0,1:T(8,128)(2,1)S(1)}, bf16[512,2,128]{2,0,1:T(8,128)(2,1)}, u32[]{:S(2)}) copy-start(bf16[512,2,128]{2,0,1:T(8,128)(2,1)} %copy-done.7) | copy-start | bytes 786436
  37.6 14.5 %collective-permute-start.4 = (f32[512,2,128]{2,0,1:T(8,128)S(1)}, f32[512,2,128]{2,0,1:T(8,128)S(1)}, u32[]{:S(2)}, u32[]{:S(2)}) collective-permute-start(f32[512,2,128]{2,0,1:T(8,128)S(1)} %convolution_bitcast_fusion.4), channel_id=1, source_target_pairs={{4,0},{8,4},{12,8},{16,12},{20,16},{24,20},{28,24},{32,28},{36,32}... | collective-permute-start | bytes 1572872 | tf_op jit(solution)/shard_map/ppermute | solution.py:19
  40.4 1.2 copy-start.1
  40.4 1.3 copy-start.6
  41.7 10.5 %copy-start.10 = (f32[128]{0:T(128)S(1)}, f32[128]{0:T(128)}, u32[]{:S(2)}) copy-start(f32[128]{0:T(128)} %param.13) | copy-start | bytes 1540
  53.7 5.5 %collective-permute-start.8 = (f32[2,128]{1,0:T(2,128)S(1)}, f32[2,128]{1,0:T(2,128)S(1)}, u32[]{:S(2)}, u32[]{:S(2)}) collective-permute-start(f32[2,128]{1,0:T(2,128)S(1)} %pad_maximum_fusion), channel_id=1, source_target_pairs={{0,1},{1,0},{2,3},{3,2},{4,5},{5,4},{6,7},{7,6},{8,9},{9,8},{10,11... | collective-permute-start | bytes 3080 | tf_op jit(solution)/shard_map/ppermute | solution.py:24
  59.2 11.3 %collective-permute-start.9 = (f32[2,128]{1,0:T(2,128)S(1)}, f32[2,128]{1,0:T(2,128)S(1)}, u32[]{:S(2)}, u32[]{:S(2)}) collective-permute-start(f32[2,128]{1,0:T(2,128)S(1)} %fusion.35), channel_id=1, source_target_pairs={{0,2},{1,3},{2,0},{3,1},{4,6},{5,7},{6,4},{7,5},{8,10},{9,11},{10,... | collective-permute-start | bytes 3080 | tf_op jit(solution)/shard_map/ppermute | solution.py:24
  65.7 44.0 %collective-permute-start.6 = (f32[512,2,128]{0,2,1:T(8,128)}, f32[512,2,128]{0,2,1:T(8,128)}, u32[]{:S(2)}, u32[]{:S(2)}) collective-permute-start(f32[512,2,128]{0,2,1:T(8,128)} %convolution_bitcast_fusion.1), channel_id=1, source_target_pairs={{4,0},{8,4},{12,8},{16,12},{20,16},{24,20},{28,24},{32,28},{36,32}... | collective-permute-start | bytes 1572872 | tf_op jit(solution)/shard_map/ppermute | solution.py:19
  68.2 41.5 %collective-permute-start.7 = (f32[512,2,128]{0,2,1:T(8,128)}, f32[512,2,128]{0,2,1:T(8,128)}, u32[]{:S(2)}, u32[]{:S(2)}) collective-permute-start(f32[512,2,128]{0,2,1:T(8,128)} %convolution_bitcast_fusion), channel_id=1, source_target_pairs={{8,0},{12,4},{16,8},{20,12},{24,16},{28,20},{32,24},{36,28},{40,32... | collective-permute-start | bytes 1572872 | tf_op jit(solution)/shard_map/ppermute | solution.py:19
  70.5 16.7 %collective-permute-start.10 = (f32[2,128]{1,0:T(2,128)S(1)}, f32[2,128]{1,0:T(2,128)S(1)}, u32[]{:S(2)}, u32[]{:S(2)}) collective-permute-start(f32[2,128]{1,0:T(2,128)S(1)} %fusion.63), channel_id=1, source_target_pairs={{0,384},{384,0},{1,385},{385,1},{2,386},{386,2},{3,387},{387,3},{4... | collective-permute-start | bytes 3080 | tf_op jit(solution)/shard_map/ppermute | solution.py:24
  87.2 3.0 %collective-permute-start.11 = (f32[2,128]{1,0:T(2,128)S(1)}, f32[2,128]{1,0:T(2,128)S(1)}, u32[]{:S(2)}, u32[]{:S(2)}) collective-permute-start(f32[2,128]{1,0:T(2,128)S(1)} %add.180), channel_id=1, source_target_pairs={{0,4},{4,0},{8,12},{12,8},{16,20},{20,16},{24,28},{28,24},{32,36},... | collective-permute-start | bytes 3080 | tf_op jit(solution)/shard_map/ppermute | solution.py:24
  90.2 5.5 %collective-permute-start.12 = (f32[2,128]{1,0:T(2,128)S(1)}, f32[2,128]{1,0:T(2,128)S(1)}, u32[]{:S(2)}, u32[]{:S(2)}) collective-permute-start(f32[2,128]{1,0:T(2,128)S(1)} %add.181), channel_id=1, source_target_pairs={{0,8},{4,12},{8,0},{12,4},{16,24},{20,28},{24,16},{28,20},{32,40},... | collective-permute-start | bytes 3080 | tf_op jit(solution)/shard_map/ppermute | solution.py:24
  95.7 6.6 %collective-permute-start.13 = (f32[2,128]{1,0:T(2,128)S(1)}, f32[2,128]{1,0:T(2,128)S(1)}, u32[]{:S(2)}, u32[]{:S(2)}) collective-permute-start(f32[2,128]{1,0:T(2,128)S(1)} %add.182), channel_id=1, source_target_pairs={{0,16},{4,20},{8,24},{12,28},{16,0},{20,4},{24,8},{28,12},{32,48},... | collective-permute-start | bytes 3080 | tf_op jit(solution)/shard_map/ppermute | solution.py:24
  102.3 38.8 %copy-start.4 = (f32[512,2,128]{2,0,1:T(8,128)S(1)}, f32[512,2,128]{2,0,1:T(8,128)}, u32[]{:S(2)}) copy-start(f32[512,2,128]{2,0,1:T(8,128)} %get-tuple-element.29) | copy-start | bytes 1572868
  102.3 9.5 %collective-permute-start.14 = (f32[2,128]{1,0:T(2,128)S(1)}, f32[2,128]{1,0:T(2,128)S(1)}, u32[]{:S(2)}, u32[]{:S(2)}) collective-permute-start(f32[2,128]{1,0:T(2,128)S(1)} %add.183), channel_id=1, source_target_pairs={{0,32},{4,36},{8,40},{12,44},{16,48},{20,52},{24,56},{28,60},{32,0... | collective-permute-start | bytes 3080 | tf_op jit(solution)/shard_map/ppermute | solution.py:24
  111.8 36.7 %copy-start.13 = (f32[2]{0:T(128)S(1)}, f32[2]{0:T(128)}, u32[]{:S(2)}) copy-start(f32[2]{0:T(128)} %constant.81) | copy-start | bytes 28
  111.8 21.2 %collective-permute-start.15 = (f32[2,128]{1,0:T(2,128)S(1)}, f32[2,128]{1,0:T(2,128)S(1)}, u32[]{:S(2)}, u32[]{:S(2)}) collective-permute-start(f32[2,128]{1,0:T(2,128)S(1)} %add.184), channel_id=1, source_target_pairs={{0,64},{4,68},{8,72},{12,76},{16,80},{20,84},{24,88},{28,92},{32,9... | collective-permute-start | bytes 3080 | tf_op jit(solution)/shard_map/ppermute | solution.py:24
  133.0 10.3 %collective-permute-start.16 = (f32[2,128]{1,0:T(2,128)S(1)}, f32[2,128]{1,0:T(2,128)S(1)}, u32[]{:S(2)}, u32[]{:S(2)}) collective-permute-start(f32[2,128]{1,0:T(2,128)S(1)} %add.185), channel_id=1, source_target_pairs={{0,256},{4,260},{8,264},{12,268},{16,272},{20,276},{24,280},{28,28... | collective-permute-start | bytes 3080 | tf_op jit(solution)/shard_map/ppermute | solution.py:36
  139.1 9.4 %collective-permute-start.17 = (f32[2,128]{1,0:T(2,128)S(1)}, f32[2,128]{1,0:T(2,128)S(1)}, u32[]{:S(2)}, u32[]{:S(2)}) collective-permute-start(f32[2,128]{1,0:T(2,128)S(1)} %add.185), channel_id=1, source_target_pairs={{0,128},{4,132},{8,136},{12,140},{16,144},{20,148},{24,152},{28,15... | collective-permute-start | bytes 3080 | tf_op jit(solution)/shard_map/ppermute | solution.py:36

commit v2 on v1

--- a/solution.py
+++ b/solution.py
@@ -74,15 +74,21 @@
     query_hat, query_inv, query_n = normalize(
         query[0].reshape(tokens, kv_heads, group_size, HD), query_gain, factor
     )
-    key_hat, key_inv, key_n = normalize(key[0].reshape(tokens, kv_heads, HD), key_gain, 1.0)
+    key_raw = key[0].reshape(tokens, kv_heads, HD)
+    key_hat, key_inv, key_n = normalize(key_raw, key_gain, 1.0)
     own_values = value[0].reshape(tokens, kv_heads, HD)
     grads_in = out_grad[0].reshape(tokens, kv_heads, group_size, HD)
     starts = list_start[0]
     anchor = lax.axis_index("ctx") * tokens
     query_place = anchor + jnp.arange(tokens, dtype=jnp.int32)
+    packed = jnp.concatenate([key_raw, own_values], axis=-1)
     blocks = [(key_n, own_values)]
+    block_hats = [key_hat]
     for distance in range(1, reach + 1):
-        blocks.append(passed_along((key_n, own_values), "ctx", distance))
+        arrived = passed_along(packed, "ctx", distance)
+        arrived_hat, _, arrived_n = normalize(arrived[..., :HD], key_gain, 1.0)
+        blocks.append((arrived_n, arrived[..., HD:]))
+        block_hats.append(arrived_hat)
     allowed_sets = []
     for distance in range(reach + 1):
         key_place = anchor - distance * tokens + jnp.arange(tokens, dtype=jnp.int32)
@@ -136,12 +142,17 @@
         )
         dquery_n = dquery_n + dquery_part
         pieces.append((dkey_part, dvalue_part))
+    key_term = jnp.sum(pieces[0][0] * block_hats[0], axis=(0, 1))
+    for distance in range(1, reach + 1):
+        key_term = key_term + jnp.sum(pieces[distance][0] * block_hats[distance], axis=(0, 1))
+    partial_sums = jnp.stack([jnp.sum(dquery_n * query_hat, axis=(0, 1, 2)) * factor, key_term])
+    summed = total_over_devices(partial_sums)
     dkey_n = pieces[0][0]
     dvalue_sum = pieces[0][1]
     for distance in range(1, reach + 1):
-        returned = passed_along(pieces[distance], "ctx", -distance)
-        dkey_n = dkey_n + returned[0]
-        dvalue_sum = dvalue_sum + returned[1]
+        returned = passed_along(jnp.concatenate(pieces[distance], axis=-1), "ctx", -distance)
+        dkey_n = dkey_n + returned[..., :HD]
+        dvalue_sum = dvalue_sum + returned[..., HD:]
     query_grad = (
         norm_backward(dquery_n, query_hat, query_inv, query_gain, factor)
         .astype(jnp.bfloat16)
@@ -153,13 +164,6 @@
         .reshape(1, tokens, -1)
     )
     value_grad = dvalue_sum.astype(jnp.bfloat16).reshape(1, tokens, -1)
-    partial_sums = jnp.stack(
-        [
-            jnp.sum(dquery_n * query_hat, axis=(0, 1, 2)) * factor,
-            jnp.sum(dkey_n * key_hat, axis=(0, 1)),
-        ]
-    )
-    summed = total_over_devices(partial_sums)
     counted = lax.axis_size("dp") * lax.axis_size("ctx") * tokens
     normalizers = jnp.array([[(counted * HQ) ** (-0.5)], [(counted * HK) ** (-0.5)]], jnp.float32)
     return (query_grad, key_grad, value_grad, summed * normalizers)

time: 150 us -> 158 us (1.053)
  the two profiles are of different devices: /device:TPU:16 before, /device:TPU:30 now
where the time goes in v2:
time: 158 us; the launch traced here: 157 us
  waiting for transfers between devices  64.1 us (41%)
  starting transfers between devices  54.5 us (34%)
  matrix products  21.4 us (14%)
  local copies, waits for them, and re-layouts  8.31 us (5%)
  other arithmetic  7.46 us (5%)
    ppermute x4, waiting for transfers between devices, passed_along(): lax.ppermute(value, axis, [(source, source + steps) for source in range(i...  36 us
    ppermute x8, starting transfers between devices, exchanged_sum(): lax.ppermute(value, axis, [(source, source ^ stride) for source in range(...  34.8 us
    ppermute x8, waiting for transfers between devices, exchanged_sum(): lax.ppermute(value, axis, [(source, source ^ stride) for source in range(...  22.6 us
    ppermute x4, starting transfers between devices, passed_along(): lax.ppermute(value, axis, [(source, source + steps) for source in range(i...  11.1 us
    ppermute x2, starting transfers between devices, three_way_sum(): received.append(lax.ppermute(value, axis, pairs))  8.63 us
    unnamed x28, local copies, waits for them, and re-layouts  8.1 us
    dot_general x3, matrix products, forward_block(): jnp.einsum('tkgd,ukd->kgtu', query_n, key_block, preferred_element_type=j...  6.31 us
    ppermute x2, waiting for transfers between devices, three_way_sum(): received.append(lax.ppermute(value, axis, pairs))  5.64 us
  transfers between devices with their start and end apart: 14, of which 13 were waited for; matrix products, arithmetic and copies ran while one was open for 11% of the time, Pallas kernels for 0%

profile of v2, /device:TPU:30, one launch (start us, length us, event | category | flops | bytes accessed | tf_op | source)
XLA Modules:
  0.0 157.0 jit_solution(9280346529240394724)
XLA Ops:
  3.7 4.7 %collective-permute-start.1 = (bf16[512,2,256]{0,2,1:T(8,128)(2,1)}, bf16[512,2,256]{0,2,1:T(8,128)(2,1)}, u32[]{:S(2)}, u32[]{:S(2)}) collective-permute-start(bf16[512,2,256]{0,2,1:T(8,128)(2,1)} %pad_maximum_fusion.2), channel_id=1, source_target_pairs={{0,8},{4,12},{8,16},{12,20},{16,24},{20,28},{24,32},{28,36},{32,40... | collective-permute-start | bytes 1572872 | tf_op jit(solution)/shard_map/ppermute | solution.py:19
  8.4 1.9 %collective-permute-start = (bf16[512,2,256]{0,2,1:T(8,128)(2,1)}, bf16[512,2,256]{0,2,1:T(8,128)(2,1)S(1)}, u32[]{:S(2)}, u32[]{:S(2)}) collective-permute-start(bf16[512,2,256]{0,2,1:T(8,128)(2,1)} %pad_maximum_fusion.2), channel_id=1, source_target_pairs={{0,4},{4,8},{8,12},{12,16},{16,20},{20,24},{24,28},{28,32},{32,36}... | collective-permute-start | bytes 1572872 | tf_op jit(solution)/shard_map/ppermute | solution.py:19
  13.5 3.0 %fusion.6 = (f32[2,2,512]{2,1,0:T(2,128)S(1)}, f32[2,512,512,2]{2,1,3,0:T(8,128)}) fusion(pred[512,512]{0,1:T(8,128)(4,1)S(1)} %get-tuple-element.19, bf16[512,2,2,128]{0,3,2,1:T(8,128)(2,1)S(1)} %multiply_convert_fusion.1, bf16[512,2,128]{0,2,1:T(8,128)(2,1)S(1)} %bitcast.194, f32[128]{0:T(128)S(1)} %copy-done.7, f32[512,2]{0,1:T(2,128)S(1)} %add_rsqrt_fusion.3), kind=kOutput, calls=%fused_computation.15 | convolution fusion | flops 271054848 | bytes 5255680 | tf_op jit(solution)/shard_map/tkgd,ukd->kgtu/dot_general | solution.py:103
  17.7 3.3 %collective-permute-done.1 = bf16[512,2,256]{0,2,1:T(8,128)(2,1)} collective-permute-done((bf16[512,2,256]{0,2,1:T(8,128)(2,1)}, bf16[512,2,256]{0,2,1:T(8,128)(2,1)}, u32[]{:S(2)}, u32[]{:S(2)}) %collective-permute-start.1) | collective-permute-done | bytes 524320 | tf_op jit(solution)/shard_map/ppermute | solution.py:19
  22.1 3.0 %collective-permute-done = bf16[512,2,256]{0,2,1:T(8,128)(2,1)S(1)} collective-permute-done((bf16[512,2,256]{0,2,1:T(8,128)(2,1)}, bf16[512,2,256]{0,2,1:T(8,128)(2,1)S(1)}, u32[]{:S(2)}, u32[]{:S(2)}) %collective-permute-start) | collective-permute-done | bytes 524320 | tf_op jit(solution)/shard_map/ppermute | solution.py:19
  25.2 2.2 %fusion.8 = (f32[2,2,512]{2,1,0:T(2,128)S(1)}, f32[2,512,512,2]{2,1,3,0:T(8,128)S(1)}) fusion(pred[512,512]{0,1:T(8,128)(4,1)} %get-tuple-element.18, bf16[512,2,2,128]{0,3,2,1:T(8,128)(2,1)S(1)} %multiply_convert_fusion.1, f32[512,2]{0,1:T(2,128)S(1)} %add_rsqrt_fusion.1, f32[128]{0:T(128)S(1)} %copy-done.7, bf16[512,2,256]{0,2,1:T(8,128)(2,1)} %collective-permute-done.1), kind=kOutput, calls=%fused_computation.17 | convolution fusion | flops 271054848 | bytes 5255680 | tf_op jit(solution)/shard_map/tkgd,ukd->kgtu/dot_general | solution.py:103
  29.7 2.2 %divide_convert_fusion.1 = (bf16[2,2,512,512]{2,3,1,0:T(8,128)(2,1)S(1)}, bf16[2,2,512,512]{2,3,1,0:T(8,128)(2,1)S(1)}, bf16[2,2,512,512]{2,3,1,0:T(8,128)(2,1)S(1)}) fusion(f32[2,512,512,2]{2,1,3,0:T(8,128)S(1)} %get-tuple-element.25, f32[2,2,512]{2,1,0:T(2,128)S(1)} %add_add_fusion, pred[512,512]{0,1:T(8,128)(4,1)S(1)} %get-tuple-element.17, ...), kind=kLoop, calls=%fused_computation.13 | loop fusion | flops 9437184 | bytes 19668992 | tf_op jit(solution)/shard_map/convert_element_type | solution.py:112
  38.4 1.9 %collective-permute-start.2 = (f32[512,2,256]{0,2,1:T(8,128)S(1)}, f32[512,2,256]{0,2,1:T(8,128)S(1)}, u32[]{:S(2)}, u32[]{:S(2)}) collective-permute-start(f32[512,2,256]{0,2,1:T(8,128)S(1)} %pad_maximum_fusion), channel_id=1, source_target_pairs={{4,0},{8,4},{12,8},{16,12},{20,16},{24,20},{28,24},{32,28},{36,32}... | collective-permute-start | bytes 3145736 | tf_op jit(solution)/shard_map/ppermute | solution.py:19
  40.4 1.7 %fusion.1 = bf16[2,2,512,512]{2,3,1,0:T(8,128)(2,1)S(1)} fusion(bf16[2,2,512,512]{2,3,1,0:T(8,128)(2,1)S(1)} %get-tuple-element.15, bf16[512,2,2,128]{0,3,2,1:T(8,128)(2,1)S(1)} %bitcast.186, f32[2,2,512]{2,1,0:T(2,128)S(1)} %bitcast.206, bf16[512,2,256]{0,2,1:T(8,128)(2,1)} %collective-permute-done.1), kind=kOutput, calls=%fused_computation.2 | convolution fusion | flops 272629760 | bytes 4988928 | tf_op jit(solution)/shard_map/tkgd,ukd->kgtu/dot_general | solution.py:130
  42.1 1.9 %fusion.26 = (f32[128]{0:T(128)S(1)}, f32[512,2,128]{0,2,1:T(8,128)S(1)}) fusion(f32[512,2]{0,1:T(2,128)S(1)} %add_rsqrt_fusion.1, bf16[512,2,256]{0,2,1:T(8,128)(2,1)} %collective-permute-done.1, bf16[512,2,2,128]{0,3,2,1:T(8,128)(2,1)S(1)} %multiply_convert_fusion.1, bf16[2,2,512,512]{2,3,1,0:T(8,128)(2,1)S(1)} %fusion.1), kind=kOutput, calls=%fused_computation.63 | convolution fusion | flops 268959616 | bytes 3412480 | tf_op jit(solution)/shard_map/kgtu,tkgd->ukd/dot_general | solution.py:137
  44.0 2.6 %collective-permute-start.3 = (f32[512,2,256]{0,2,1:T(8,128)S(1)}, f32[512,2,256]{0,2,1:T(8,128)S(1)}, u32[]{:S(2)}, u32[]{:S(2)}) collective-permute-start(f32[512,2,256]{0,2,1:T(8,128)S(1)} %pad_maximum_fusion.1), channel_id=1, source_target_pairs={{8,0},{12,4},{16,8},{20,12},{24,16},{28,20},{32,24},{36,28},{40,32... | collective-permute-start | bytes 3145736 | tf_op jit(solution)/shard_map/ppermute | solution.py:19
  47.5 1.7 %multiply_reduce_fusion = (f32[128]{0:T(128)S(1)}, f32[512,2,2]{0,2,1:T(2,128)S(1)}, f32[512,2,2,128]{0,3,2,1:T(8,128)S(1)}) fusion(f32[512,2,2,128]{0,3,2,1:T(8,128)S(1)} %bitcast.190, f32[512,2,2]{0,2,1:T(2,128)S(1)} %add_rsqrt_fusion, f32[128]{0:T(128)S(1)} %copy-done.8, f32[2,128,2,512]{3,1,2,0:T(8,128)S(1)} %convolution_add_fusion.1, ...), kind=kOutput, calls=%fused_computation.36 | convolution fusion | flops 271054720 | bytes 5527040 | tf_op jit(solution)/shard_map/kgtu,ukd->tkgd/dot_general | solution.py:134
  50.0 8.3 %collective-permute-done.2 = f32[512,2,256]{0,2,1:T(8,128)S(1)} collective-permute-done((f32[512,2,256]{0,2,1:T(8,128)S(1)}, f32[512,2,256]{0,2,1:T(8,128)S(1)}, u32[]{:S(2)}, u32[]{:S(2)}) %collective-permute-start.2) | collective-permute-done | bytes 1048608 | tf_op jit(solution)/shard_map/ppermute | solution.py:19
  58.3 21.3 %collective-permute-done.3 = f32[512,2,256]{0,2,1:T(8,128)S(1)} collective-permute-done((f32[512,2,256]{0,2,1:T(8,128)S(1)}, f32[512,2,256]{0,2,1:T(8,128)S(1)}, u32[]{:S(2)}, u32[]{:S(2)}) %collective-permute-start.3) | collective-permute-done | bytes 1048608 | tf_op jit(solution)/shard_map/ppermute | solution.py:19
  79.6 1.7 %fusion.34 = (f32[128]{0:T(128)S(1)}, f32[512,2]{0,1:T(2,128)S(1)}, f32[512,2,128]{0,2,1:T(8,128)}, bf16[512,2,128]{0,2,1:T(8,128)(2,1)}) fusion(bf16[512,2,128]{0,2,1:T(8,128)(2,1)S(1)} %bitcast.196, f32[512,2]{0,1:T(2,128)S(1)} %add_rsqrt_fusion.3, f32[128]{0:T(128)S(1)} %copy-done.7, f32[512,2,256]{0,2,1:T(8,128)S(1)} %collective-permute-done.3, ...), kind=kOutput, calls=%fused_computation.71 | convolution fusion | flops 270007168 | bytes 6300672 | tf_op jit(solution)/shard_map/kgtu,tkgd->ukd/dot_general | solution.py:137
  81.3 2.9 %collective-permute-start.4 = (f32[2,128]{1,0:T(2,128)S(1)}, f32[2,128]{1,0:T(2,128)S(1)}, u32[]{:S(2)}, u32[]{:S(2)}) collective-permute-start(f32[2,128]{1,0:T(2,128)S(1)} %pad_maximum_fusion.3), channel_id=1, source_target_pairs={{0,1},{1,0},{2,3},{3,2},{4,5},{5,4},{6,7},{7,6},{8,9},{9,8},{10,11... | collective-permute-start | bytes 3080 | tf_op jit(solution)/shard_map/ppermute | solution.py:24
  84.2 2.7 %collective-permute-done.4 = f32[2,128]{1,0:T(2,128)S(1)} collective-permute-done((f32[2,128]{1,0:T(2,128)S(1)}, f32[2,128]{1,0:T(2,128)S(1)}, u32[]{:S(2)}, u32[]{:S(2)}) %collective-permute-start.4) | collective-permute-done | bytes 1056 | tf_op jit(solution)/shard_map/ppermute | solution.py:24
  86.9 3.3 %collective-permute-start.5 = (f32[2,128]{1,0:T(2,128)S(1)}, f32[2,128]{1,0:T(2,128)S(1)}, u32[]{:S(2)}, u32[]{:S(2)}) collective-permute-start(f32[2,128]{1,0:T(2,128)S(1)} %fusion.53), channel_id=1, source_target_pairs={{0,2},{1,3},{2,0},{3,1},{4,6},{5,7},{6,4},{7,5},{8,10},{9,11},{10,... | collective-permute-start | bytes 3080 | tf_op jit(solution)/shard_map/ppermute | solution.py:24
  90.3 3.7 %collective-permute-done.5 = f32[2,128]{1,0:T(2,128)S(1)} collective-permute-done((f32[2,128]{1,0:T(2,128)S(1)}, f32[2,128]{1,0:T(2,128)S(1)}, u32[]{:S(2)}, u32[]{:S(2)}) %collective-permute-start.5) | collective-permute-done | bytes 1056 | tf_op jit(solution)/shard_map/ppermute | solution.py:24
  93.9 15.1 %collective-permute-start.6 = (f32[2,128]{1,0:T(2,128)S(1)}, f32[2,128]{1,0:T(2,128)S(1)}, u32[]{:S(2)}, u32[]{:S(2)}) collective-permute-start(f32[2,128]{1,0:T(2,128)S(1)} %fusion.81), channel_id=1, source_target_pairs={{0,384},{384,0},{1,385},{385,1},{2,386},{386,2},{3,387},{387,3},{4... | collective-permute-start | bytes 3080 | tf_op jit(solution)/shard_map/ppermute | solution.py:24
  110.6 1.9 %collective-permute-start.7 = (f32[2,128]{1,0:T(2,128)S(1)}, f32[2,128]{1,0:T(2,128)S(1)}, u32[]{:S(2)}, u32[]{:S(2)}) collective-permute-start(f32[2,128]{1,0:T(2,128)S(1)} %add.216), channel_id=1, source_target_pairs={{0,4},{4,0},{8,12},{12,8},{16,20},{20,16},{24,28},{28,24},{32,36},... | collective-permute-start | bytes 3080 | tf_op jit(solution)/shard_map/ppermute | solution.py:24
  113.7 1.9 %collective-permute-start.8 = (f32[2,128]{1,0:T(2,128)S(1)}, f32[2,128]{1,0:T(2,128)S(1)}, u32[]{:S(2)}, u32[]{:S(2)}) collective-permute-start(f32[2,128]{1,0:T(2,128)S(1)} %add.217), channel_id=1, source_target_pairs={{0,8},{4,12},{8,0},{12,4},{16,24},{20,28},{24,16},{28,20},{32,40},... | collective-permute-start | bytes 3080 | tf_op jit(solution)/shard_map/ppermute | solution.py:24
  115.6 3.5 %collective-permute-done.8 = f32[2,128]{1,0:T(2,128)S(1)} collective-permute-done((f32[2,128]{1,0:T(2,128)S(1)}, f32[2,128]{1,0:T(2,128)S(1)}, u32[]{:S(2)}, u32[]{:S(2)}) %collective-permute-start.8) | collective-permute-done | bytes 1056 | tf_op jit(solution)/shard_map/ppermute | solution.py:24
  119.1 1.9 %collective-permute-start.9 = (f32[2,128]{1,0:T(2,128)S(1)}, f32[2,128]{1,0:T(2,128)S(1)}, u32[]{:S(2)}, u32[]{:S(2)}) collective-permute-start(f32[2,128]{1,0:T(2,128)S(1)} %add.218), channel_id=1, source_target_pairs={{0,16},{4,20},{8,24},{12,28},{16,0},{20,4},{24,8},{28,12},{32,48},... | collective-permute-start | bytes 3080 | tf_op jit(solution)/shard_map/ppermute | solution.py:24
  121.1 4.4 %collective-permute-done.9 = f32[2,128]{1,0:T(2,128)S(1)} collective-permute-done((f32[2,128]{1,0:T(2,128)S(1)}, f32[2,128]{1,0:T(2,128)S(1)}, u32[]{:S(2)}, u32[]{:S(2)}) %collective-permute-start.9) | collective-permute-done | bytes 1056 | tf_op jit(solution)/shard_map/ppermute | solution.py:24
  125.5 4.4 %collective-permute-start.10 = (f32[2,128]{1,0:T(2,128)S(1)}, f32[2,128]{1,0:T(2,128)S(1)}, u32[]{:S(2)}, u32[]{:S(2)}) collective-permute-start(f32[2,128]{1,0:T(2,128)S(1)} %add.219), channel_id=1, source_target_pairs={{0,32},{4,36},{8,40},{12,44},{16,48},{20,52},{24,56},{28,60},{32,0... | collective-permute-start | bytes 3080 | tf_op jit(solution)/shard_map/ppermute | solution.py:24
  131.3 3.6 %collective-permute-done.10 = f32[2,128]{1,0:T(2,128)S(1)} collective-permute-done((f32[2,128]{1,0:T(2,128)S(1)}, f32[2,128]{1,0:T(2,128)S(1)}, u32[]{:S(2)}, u32[]{:S(2)}) %collective-permute-start.10) | collective-permute-done | bytes 1056 | tf_op jit(solution)/shard_map/ppermute | solution.py:24
  134.9 3.4 %collective-permute-start.11 = (f32[2,128]{1,0:T(2,128)S(1)}, f32[2,128]{1,0:T(2,128)S(1)}, u32[]{:S(2)}, u32[]{:S(2)}) collective-permute-start(f32[2,128]{1,0:T(2,128)S(1)} %add.220), channel_id=1, source_target_pairs={{0,64},{4,68},{8,72},{12,76},{16,80},{20,84},{24,88},{28,92},{32,9... | collective-permute-start | bytes 3080 | tf_op jit(solution)/shard_map/ppermute | solution.py:24
  138.2 2.1 %collective-permute-done.11 = f32[2,128]{1,0:T(2,128)S(1)} collective-permute-done((f32[2,128]{1,0:T(2,128)S(1)}, f32[2,128]{1,0:T(2,128)S(1)}, u32[]{:S(2)}, u32[]{:S(2)}) %collective-permute-start.11) | collective-permute-done | bytes 1056 | tf_op jit(solution)/shard_map/ppermute | solution.py:24
  140.3 6.7 %collective-permute-start.12 = (f32[2,128]{1,0:T(2,128)S(1)}, f32[2,128]{1,0:T(2,128)S(1)}, u32[]{:S(2)}, u32[]{:S(2)}) collective-permute-start(f32[2,128]{1,0:T(2,128)S(1)} %add.221), channel_id=1, source_target_pairs={{0,256},{4,260},{8,264},{12,268},{16,272},{20,276},{24,280},{28,28... | collective-permute-start | bytes 3080 | tf_op jit(solution)/shard_map/ppermute | solution.py:36
  147.0 1.9 %collective-permute-start.13 = (f32[2,128]{1,0:T(2,128)S(1)}, f32[2,128]{1,0:T(2,128)S(1)}, u32[]{:S(2)}, u32[]{:S(2)}) collective-permute-start(f32[2,128]{1,0:T(2,128)S(1)} %add.221), channel_id=1, source_target_pairs={{0,128},{4,132},{8,136},{12,140},{16,144},{20,148},{24,152},{28,15... | collective-permute-start | bytes 3080 | tf_op jit(solution)/shard_map/ppermute | solution.py:36
  150.8 5.6 %collective-permute-done.13 = f32[2,128]{1,0:T(2,128)S(1)} collective-permute-done((f32[2,128]{1,0:T(2,128)S(1)}, f32[2,128]{1,0:T(2,128)S(1)}, u32[]{:S(2)}, u32[]{:S(2)}) %collective-permute-start.13) | collective-permute-done | bytes 1056 | tf_op jit(solution)/shard_map/ppermute | solution.py:36
  (76 shorter events, 25.4 us)
Async XLA Ops:
  0.6 9.8 %copy-start.6 = (bf16[1,512,512]{2,1,0:T(8,128)(2,1)S(1)}, bf16[1,512,512]{2,1,0:T(8,128)(2,1)}, u32[]{:S(2)}) copy-start(bf16[1,512,512]{2,1,0:T(8,128)(2,1)} %param.8) | copy-start | bytes 1572868
  2.9 8.0 %copy-start.8 = (f32[128]{0:T(128)S(1)}, f32[128]{0:T(128)}, u32[]{:S(2)}) copy-start(f32[128]{0:T(128)} %param.12) | copy-start | bytes 1540
  3.7 17.3 %collective-permute-start.1 = (bf16[512,2,256]{0,2,1:T(8,128)(2,1)}, bf16[512,2,256]{0,2,1:T(8,128)(2,1)}, u32[]{:S(2)}, u32[]{:S(2)}) collective-permute-start(bf16[512,2,256]{0,2,1:T(8,128)(2,1)} %pad_maximum_fusion.2), channel_id=1, source_target_pairs={{0,8},{4,12},{8,16},{12,20},{16,24},{20,28},{24,32},{28,36},{32,40... | collective-permute-start | bytes 1572872 | tf_op jit(solution)/shard_map/ppermute | solution.py:19
  8.4 16.7 %collective-permute-start = (bf16[512,2,256]{0,2,1:T(8,128)(2,1)}, bf16[512,2,256]{0,2,1:T(8,128)(2,1)S(1)}, u32[]{:S(2)}, u32[]{:S(2)}) collective-permute-start(bf16[512,2,256]{0,2,1:T(8,128)(2,1)} %pad_maximum_fusion.2), channel_id=1, source_target_pairs={{0,4},{4,8},{8,12},{12,16},{16,20},{20,24},{24,28},{28,32},{32,36}... | collective-permute-start | bytes 1572872 | tf_op jit(solution)/shard_map/ppermute | solution.py:19
  10.5 0.7 copy-start.9
  10.7 2.8 %copy-start.7 = (f32[128]{0:T(128)S(1)}, f32[128]{0:T(128)}, u32[]{:S(2)}) copy-start(f32[128]{0:T(128)} %param.13) | copy-start | bytes 1540
  12.8 0.7 copy-start.3
  27.4 2.2 %copy-start = (f32[2,512,512,2]{2,1,3,0:T(8,128)S(1)}, f32[2,512,512,2]{2,1,3,0:T(8,128)}, u32[]{:S(2)}) copy-start(f32[2,512,512,2]{2,1,3,0:T(8,128)} %get-tuple-element.23) | copy-start | bytes 12582916
  27.4 2.2 %copy-start.2 = (pred[512,512]{0,1:T(8,128)(4,1)S(1)}, pred[512,512]{0,1:T(8,128)(4,1)}, u32[]{:S(2)}) copy-start(pred[512,512]{0,1:T(8,128)(4,1)} %get-tuple-element.18) | copy-start | bytes 786436
  27.4 2.3 %copy-start.4 = (pred[512,512]{0,1:T(8,128)(4,1)S(1)}, pred[512,512]{0,1:T(8,128)(4,1)}, u32[]{:S(2)}) copy-start(pred[512,512]{0,1:T(8,128)(4,1)} %copy-done.3) | copy-start | bytes 786436
  38.4 19.9 %collective-permute-start.2 = (f32[512,2,256]{0,2,1:T(8,128)S(1)}, f32[512,2,256]{0,2,1:T(8,128)S(1)}, u32[]{:S(2)}, u32[]{:S(2)}) collective-permute-start(f32[512,2,256]{0,2,1:T(8,128)S(1)} %pad_maximum_fusion), channel_id=1, source_target_pairs={{4,0},{8,4},{12,8},{16,12},{20,16},{24,20},{28,24},{32,28},{36,32}... | collective-permute-start | bytes 3145736 | tf_op jit(solution)/shard_map/ppermute | solution.py:19
  44.0 35.6 %collective-permute-start.3 = (f32[512,2,256]{0,2,1:T(8,128)S(1)}, f32[512,2,256]{0,2,1:T(8,128)S(1)}, u32[]{:S(2)}, u32[]{:S(2)}) collective-permute-start(f32[512,2,256]{0,2,1:T(8,128)S(1)} %pad_maximum_fusion.1), channel_id=1, source_target_pairs={{8,0},{12,4},{16,8},{20,12},{24,16},{28,20},{32,24},{36,28},{40,32... | collective-permute-start | bytes 3145736 | tf_op jit(solution)/shard_map/ppermute | solution.py:19
  81.3 67.6 %copy-start.1 = (f32[512,2,128]{0,2,1:T(8,128)S(1)}, f32[512,2,128]{0,2,1:T(8,128)}, u32[]{:S(2)}) copy-start(f32[512,2,128]{0,2,1:T(8,128)} %get-tuple-element.12) | copy-start | bytes 1572868
  81.3 5.6 %collective-permute-start.4 = (f32[2,128]{1,0:T(2,128)S(1)}, f32[2,128]{1,0:T(2,128)S(1)}, u32[]{:S(2)}, u32[]{:S(2)}) collective-permute-start(f32[2,128]{1,0:T(2,128)S(1)} %pad_maximum_fusion.3), channel_id=1, source_target_pairs={{0,1},{1,0},{2,3},{3,2},{4,5},{5,4},{6,7},{7,6},{8,9},{9,8},{10,11... | collective-permute-start | bytes 3080 | tf_op jit(solution)/shard_map/ppermute | solution.py:24
  86.9 7.0 %collective-permute-start.5 = (f32[2,128]{1,0:T(2,128)S(1)}, f32[2,128]{1,0:T(2,128)S(1)}, u32[]{:S(2)}, u32[]{:S(2)}) collective-permute-start(f32[2,128]{1,0:T(2,128)S(1)} %fusion.53), channel_id=1, source_target_pairs={{0,2},{1,3},{2,0},{3,1},{4,6},{5,7},{6,4},{7,5},{8,10},{9,11},{10,... | collective-permute-start | bytes 3080 | tf_op jit(solution)/shard_map/ppermute | solution.py:24
  93.9 16.7 %collective-permute-start.6 = (f32[2,128]{1,0:T(2,128)S(1)}, f32[2,128]{1,0:T(2,128)S(1)}, u32[]{:S(2)}, u32[]{:S(2)}) collective-permute-start(f32[2,128]{1,0:T(2,128)S(1)} %fusion.81), channel_id=1, source_target_pairs={{0,384},{384,0},{1,385},{385,1},{2,386},{386,2},{3,387},{387,3},{4... | collective-permute-start | bytes 3080 | tf_op jit(solution)/shard_map/ppermute | solution.py:24
  110.6 3.0 %collective-permute-start.7 = (f32[2,128]{1,0:T(2,128)S(1)}, f32[2,128]{1,0:T(2,128)S(1)}, u32[]{:S(2)}, u32[]{:S(2)}) collective-permute-start(f32[2,128]{1,0:T(2,128)S(1)} %add.216), channel_id=1, source_target_pairs={{0,4},{4,0},{8,12},{12,8},{16,20},{20,16},{24,28},{28,24},{32,36},... | collective-permute-start | bytes 3080 | tf_op jit(solution)/shard_map/ppermute | solution.py:24
  113.7 5.5 %collective-permute-start.8 = (f32[2,128]{1,0:T(2,128)S(1)}, f32[2,128]{1,0:T(2,128)S(1)}, u32[]{:S(2)}, u32[]{:S(2)}) collective-permute-start(f32[2,128]{1,0:T(2,128)S(1)} %add.217), channel_id=1, source_target_pairs={{0,8},{4,12},{8,0},{12,4},{16,24},{20,28},{24,16},{28,20},{32,40},... | collective-permute-start | bytes 3080 | tf_op jit(solution)/shard_map/ppermute | solution.py:24
  119.1 6.4 %collective-permute-start.9 = (f32[2,128]{1,0:T(2,128)S(1)}, f32[2,128]{1,0:T(2,128)S(1)}, u32[]{:S(2)}, u32[]{:S(2)}) collective-permute-start(f32[2,128]{1,0:T(2,128)S(1)} %add.218), channel_id=1, source_target_pairs={{0,16},{4,20},{8,24},{12,28},{16,0},{20,4},{24,8},{28,12},{32,48},... | collective-permute-start | bytes 3080 | tf_op jit(solution)/shard_map/ppermute | solution.py:24
  125.5 9.4 %collective-permute-start.10 = (f32[2,128]{1,0:T(2,128)S(1)}, f32[2,128]{1,0:T(2,128)S(1)}, u32[]{:S(2)}, u32[]{:S(2)}) collective-permute-start(f32[2,128]{1,0:T(2,128)S(1)} %add.219), channel_id=1, source_target_pairs={{0,32},{4,36},{8,40},{12,44},{16,48},{20,52},{24,56},{28,60},{32,0... | collective-permute-start | bytes 3080 | tf_op jit(solution)/shard_map/ppermute | solution.py:24
  130.2 19.7 %copy-start.5 = (bf16[512,2,128]{0,2,1:T(8,128)(2,1)S(1)}, bf16[512,2,128]{0,2,1:T(8,128)(2,1)}, u32[]{:S(2)}) copy-start(bf16[512,2,128]{0,2,1:T(8,128)(2,1)} %get-tuple-element.13) | copy-start | bytes 786436
  130.2 26.2 %copy-start.10 = (f32[2]{0:T(128)S(1)}, f32[2]{0:T(128)}, u32[]{:S(2)}) copy-start(f32[2]{0:T(128)} %constant.83) | copy-start | bytes 28
  134.9 5.5 %collective-permute-start.11 = (f32[2,128]{1,0:T(2,128)S(1)}, f32[2,128]{1,0:T(2,128)S(1)}, u32[]{:S(2)}, u32[]{:S(2)}) collective-permute-start(f32[2,128]{1,0:T(2,128)S(1)} %add.220), channel_id=1, source_target_pairs={{0,64},{4,68},{8,72},{12,76},{16,80},{20,84},{24,88},{28,92},{32,9... | collective-permute-start | bytes 3080 | tf_op jit(solution)/shard_map/ppermute | solution.py:24
  140.3 10.5 %collective-permute-start.12 = (f32[2,128]{1,0:T(2,128)S(1)}, f32[2,128]{1,0:T(2,128)S(1)}, u32[]{:S(2)}, u32[]{:S(2)}) collective-permute-start(f32[2,128]{1,0:T(2,128)S(1)} %add.221), channel_id=1, source_target_pairs={{0,256},{4,260},{8,264},{12,268},{16,272},{20,276},{24,280},{28,28... | collective-permute-start | bytes 3080 | tf_op jit(solution)/shard_map/ppermute | solution.py:36
  147.0 9.4 %collective-permute-start.13 = (f32[2,128]{1,0:T(2,128)S(1)}, f32[2,128]{1,0:T(2,128)S(1)}, u32[]{:S(2)}, u32[]{:S(2)}) collective-permute-start(f32[2,128]{1,0:T(2,128)S(1)} %add.221), channel_id=1, source_target_pairs={{0,128},{4,132},{8,136},{12,140},{16,144},{20,148},{24,152},{28,15... | collective-permute-start | bytes 3080 | tf_op jit(solution)/shard_map/ppermute | solution.py:36

commit v3 on v2

--- a/solution.py
+++ b/solution.py
@@ -147,10 +147,14 @@
         key_term = key_term + jnp.sum(pieces[distance][0] * block_hats[distance], axis=(0, 1))
     partial_sums = jnp.stack([jnp.sum(dquery_n * query_hat, axis=(0, 1, 2)) * factor, key_term])
     summed = total_over_devices(partial_sums)
+    returns = [
+        passed_along(jnp.concatenate(pieces[distance], axis=-1), "ctx", -distance)
+        for distance in range(1, reach + 1)
+    ]
+    summed, *returns = lax.optimization_barrier((summed, *returns))
     dkey_n = pieces[0][0]
     dvalue_sum = pieces[0][1]
-    for distance in range(1, reach + 1):
-        returned = passed_along(jnp.concatenate(pieces[distance], axis=-1), "ctx", -distance)
+    for returned in returns:
         dkey_n = dkey_n + returned[..., :HD]
         dvalue_sum = dvalue_sum + returned[..., HD:]
     query_grad = (

time: 158 us -> 146 us (0.924)
  the two profiles are of different devices: /device:TPU:30 before, /device:TPU:2 now
where the time goes in v3:
time: 146 us; the launch traced here: 145 us
  starting transfers between devices  79.6 us (55%)
  matrix products  20.8 us (14%)
  waiting for transfers between devices  19.8 us (14%)
  local copies, waits for them, and re-layouts  12.2 us (8%)
  other arithmetic  11 us (8%)
    ppermute x8, starting transfers between devices, exchanged_sum(): lax.ppermute(value, axis, [(source, source ^ stride) for source in range(...  63.7 us
    ppermute x8, waiting for transfers between devices, exchanged_sum(): lax.ppermute(value, axis, [(source, source ^ stride) for source in range(...  13.4 us
    unnamed x44, local copies, waits for them, and re-layouts  12 us
    ppermute x2, starting transfers between devices, three_way_sum(): received.append(lax.ppermute(value, axis, pairs))  8.05 us
    ppermute x4, starting transfers between devices, passed_along(): lax.ppermute(value, axis, [(source, source + steps) for source in range(i...  7.86 us
    dot_general x3, matrix products, forward_block(): jnp.einsum('tkgd,ukd->kgtu', query_n, key_block, preferred_element_type=j...  6.43 us
    dot_general x3, matrix products, shards(): jnp.einsum('kgtu,tkgd->ukd', prob, grads_in, preferred_element_type=jnp.f...  4.71 us
    ppermute x4, waiting for transfers between devices, passed_along(): lax.ppermute(value, axis, [(source, source + steps) for source in range(i...  3.64 us
  transfers between devices with their start and end apart: 14, of which 9 were waited for; matrix products, arithmetic and copies ran while one was open for 11% of the time, Pallas kernels for 0%

profile of v3, /device:TPU:2, one launch (start us, length us, event | category | flops | bytes accessed | tf_op | source)
XLA Modules:
  0.0 144.7 jit_solution(4232242020964800639)
XLA Ops:
  3.8 3.5 %collective-permute-start.1 = (bf16[512,2,256]{0,2,1:T(8,128)(2,1)}, bf16[512,2,256]{0,2,1:T(8,128)(2,1)S(1)}, u32[]{:S(2)}, u32[]{:S(2)}) collective-permute-start(bf16[512,2,256]{0,2,1:T(8,128)(2,1)} %pad_maximum_fusion.2), channel_id=1, source_target_pairs={{0,8},{4,12},{8,16},{12,20},{16,24},{20,28},{24,32},{28,36},{32,40... | collective-permute-start | bytes 1572872 | tf_op jit(solution)/shard_map/ppermute | solution.py:19
  7.3 1.5 %collective-permute-start = (bf16[512,2,256]{0,2,1:T(8,128)(2,1)}, bf16[512,2,256]{0,2,1:T(8,128)(2,1)S(1)}, u32[]{:S(2)}, u32[]{:S(2)}) collective-permute-start(bf16[512,2,256]{0,2,1:T(8,128)(2,1)} %pad_maximum_fusion.2), channel_id=1, source_target_pairs={{0,4},{4,8},{8,12},{12,16},{16,20},{20,24},{24,28},{28,32},{32,36}... | collective-permute-start | bytes 1572872 | tf_op jit(solution)/shard_map/ppermute | solution.py:19
  9.6 1.7 %fusion.15 = (pred[512,512]{0,1:T(8,128)(4,1)}, pred[512,512]{0,1:T(8,128)(4,1)}, pred[512,512]{0,1:T(8,128)(4,1)S(1)}) fusion(s32[512]{0:T(512)S(1)} %iota_add_fusion.2, s32[512]{0:T(512)S(1)} %bitcast.208, s32[512]{0:T(512)S(1)} %get-tuple-element.39, s32[512]{0:T(512)S(1)} %get-tuple-element.38), kind=kLoop, calls=%fused_computation.46 | loop fusion | flops 4718592 | bytes 794624 | tf_op jit(solution)/shard_map/and | solution.py:96
  12.0 3.0 %fusion.6 = (f32[2,2,512]{2,1,0:T(2,128)S(1)}, f32[2,512,512,2]{2,1,3,0:T(8,128)}) fusion(pred[512,512]{0,1:T(8,128)(4,1)S(1)} %get-tuple-element.24, bf16[512,2,2,128]{0,3,2,1:T(8,128)(2,1)S(1)} %multiply_convert_fusion.1, bf16[512,2,128]{0,2,1:T(8,128)(2,1)S(1)} %bitcast.194, f32[128]{0:T(128)S(1)} %copy-done.15, f32[512,2]{0,1:T(2,128)S(1)} %add_rsqrt_fusion.3), kind=kOutput, calls=%fused_computation.15 | convolution fusion | flops 271054848 | bytes 5255680 | tf_op jit(solution)/shard_map/tkgd,ukd->kgtu/dot_general | solution.py:103
  16.2 3.6 %collective-permute-done.1 = bf16[512,2,256]{0,2,1:T(8,128)(2,1)S(1)} collective-permute-done((bf16[512,2,256]{0,2,1:T(8,128)(2,1)}, bf16[512,2,256]{0,2,1:T(8,128)(2,1)S(1)}, u32[]{:S(2)}, u32[]{:S(2)}) %collective-permute-start.1) | collective-permute-done | bytes 524320 | tf_op jit(solution)/shard_map/ppermute | solution.py:19
  20.1 2.3 %fusion.8 = (f32[2,2,512]{2,1,0:T(2,128)S(1)}, f32[2,512,512,2]{2,1,3,0:T(8,128)S(1)}) fusion(pred[512,512]{0,1:T(8,128)(4,1)} %get-tuple-element.23, bf16[512,2,2,128]{0,3,2,1:T(8,128)(2,1)S(1)} %multiply_convert_fusion.1, f32[512,2]{0,1:T(2,128)S(1)} %add_rsqrt_fusion.1, f32[128]{0:T(128)S(1)} %copy-done.15, ...), kind=kOutput, calls=%fused_computation.17 | convolution fusion | flops 271054848 | bytes 5255680 | tf_op jit(solution)/shard_map/tkgd,ukd->kgtu/dot_general | solution.py:103
  24.7 2.2 %divide_convert_fusion.1 = (bf16[2,2,512,512]{2,3,1,0:T(8,128)(2,1)S(1)}, bf16[2,2,512,512]{2,3,1,0:T(8,128)(2,1)S(1)}, bf16[2,2,512,512]{2,3,1,0:T(8,128)(2,1)S(1)}) fusion(f32[2,512,512,2]{2,1,3,0:T(8,128)S(1)} %get-tuple-element.30, f32[2,2,512]{2,1,0:T(2,128)S(1)} %add_add_fusion, pred[512,512]{0,1:T(8,128)(4,1)S(1)} %copy-done.10, ...), kind=kLoop, calls=%fused_computation.13 | loop fusion | flops 9437184 | bytes 19668992 | tf_op jit(solution)/shard_map/convert_element_type | solution.py:112
  32.0 1.6 %fusion.30 = (f32[128]{0:T(128)S(1)}, f32[512,2,128]{0,2,1:T(8,128)}) fusion(bf16[512,2,128]{0,2,1:T(8,128)(2,1)S(1)} %bitcast.195, f32[512,2]{0,1:T(2,128)S(1)} %add_rsqrt_fusion.3, bf16[512,2,2,128]{0,3,2,1:T(8,128)(2,1)S(1)} %multiply_convert_fusion.1, bf16[2,2,512,512]{2,3,1,0:T(8,128)(2,1)S(1)} %fusion.5), kind=kOutput, calls=%fused_computation.67 | convolution fusion | flops 268959616 | bytes 3412480 | tf_op jit(solution)/shard_map/kgtu,tkgd->ukd/dot_general | solution.py:137
  36.8 1.5 %collective-permute-start.13 = (f32[512,2,256]{0,2,1:T(8,128)}, f32[512,2,256]{0,2,1:T(8,128)}, u32[]{:S(2)}, u32[]{:S(2)}) collective-permute-start(f32[512,2,256]{0,2,1:T(8,128)} %pad_maximum_fusion.1), channel_id=1, source_target_pairs={{8,0},{12,4},{16,8},{20,12},{24,16},{28,20},{32,24},{36,28},{40,32... | collective-permute-start | bytes 3145736 | tf_op jit(solution)/shard_map/ppermute | solution.py:19
  40.3 1.6 %multiply_reduce_fusion = (f32[128]{0:T(128)S(1)}, f32[512,2,2]{0,2,1:T(2,128)S(1)}, f32[512,2,2,128]{0,3,2,1:T(8,128)}) fusion(f32[512,2,2,128]{0,3,2,1:T(8,128)S(1)} %bitcast.191, f32[512,2,2]{0,2,1:T(2,128)S(1)} %add_rsqrt_fusion, f32[128]{0:T(128)S(1)} %copy-done.16, f32[2,128,2,512]{3,1,2,0:T(8,128)S(1)} %convolution_add_fusion.1, ...), kind=kOutput, calls=%fused_computation.36 | convolution fusion | flops 271054720 | bytes 5527040 | tf_op jit(solution)/shard_map/kgtu,ukd->tkgd/dot_general | solution.py:134
  42.8 6.9 %collective-permute-start.2 = (f32[2,128]{1,0:T(2,128)S(1)}, f32[2,128]{1,0:T(2,128)S(1)}, u32[]{:S(2)}, u32[]{:S(2)}) collective-permute-start(f32[2,128]{1,0:T(2,128)S(1)} %pad_maximum_fusion.3), channel_id=1, source_target_pairs={{0,1},{1,0},{2,3},{3,2},{4,5},{5,4},{6,7},{7,6},{8,9},{9,8},{10,11... | collective-permute-start | bytes 3080 | tf_op jit(solution)/shard_map/ppermute | solution.py:24
  50.8 1.4 collective-permute-start.12
  52.3 1.9 %collective-permute-start.3 = (f32[2,128]{1,0:T(2,128)S(1)}, f32[2,128]{1,0:T(2,128)S(1)}, u32[]{:S(2)}, u32[]{:S(2)}) collective-permute-start(f32[2,128]{1,0:T(2,128)S(1)} %fusion.51), channel_id=1, source_target_pairs={{0,2},{1,3},{2,0},{3,1},{4,6},{5,7},{6,4},{7,5},{8,10},{9,11},{10,... | collective-permute-start | bytes 3080 | tf_op jit(solution)/shard_map/ppermute | solution.py:24
  54.2 5.0 %collective-permute-done.3 = f32[2,128]{1,0:T(2,128)S(1)} collective-permute-done((f32[2,128]{1,0:T(2,128)S(1)}, f32[2,128]{1,0:T(2,128)S(1)}, u32[]{:S(2)}, u32[]{:S(2)}) %collective-permute-start.3) | collective-permute-done | bytes 1056 | tf_op jit(solution)/shard_map/ppermute | solution.py:24
  59.2 11.2 %collective-permute-start.4 = (f32[2,128]{1,0:T(2,128)S(1)}, f32[2,128]{1,0:T(2,128)S(1)}, u32[]{:S(2)}, u32[]{:S(2)}) collective-permute-start(f32[2,128]{1,0:T(2,128)S(1)} %fusion.78), channel_id=1, source_target_pairs={{0,384},{384,0},{1,385},{385,1},{2,386},{386,2},{3,387},{387,3},{4... | collective-permute-start | bytes 3080 | tf_op jit(solution)/shard_map/ppermute | solution.py:24
  70.4 1.5 %collective-permute-done.4 = f32[2,128]{1,0:T(2,128)S(1)} collective-permute-done((f32[2,128]{1,0:T(2,128)S(1)}, f32[2,128]{1,0:T(2,128)S(1)}, u32[]{:S(2)}, u32[]{:S(2)}) %collective-permute-start.4) | collective-permute-done | bytes 1056 | tf_op jit(solution)/shard_map/ppermute | solution.py:24
  72.0 4.1 %collective-permute-start.5 = (f32[2,128]{1,0:T(2,128)S(1)}, f32[2,128]{1,0:T(2,128)S(1)}, u32[]{:S(2)}, u32[]{:S(2)}) collective-permute-start(f32[2,128]{1,0:T(2,128)S(1)} %add.212), channel_id=1, source_target_pairs={{0,4},{4,0},{8,12},{12,8},{16,20},{20,16},{24,28},{28,24},{32,36},... | collective-permute-start | bytes 3080 | tf_op jit(solution)/shard_map/ppermute | solution.py:24
  76.9 7.4 %collective-permute-start.6 = (f32[2,128]{1,0:T(2,128)S(1)}, f32[2,128]{1,0:T(2,128)S(1)}, u32[]{:S(2)}, u32[]{:S(2)}) collective-permute-start(f32[2,128]{1,0:T(2,128)S(1)} %add.213), channel_id=1, source_target_pairs={{0,8},{4,12},{8,0},{12,4},{16,24},{20,28},{24,16},{28,20},{32,40},... | collective-permute-start | bytes 3080 | tf_op jit(solution)/shard_map/ppermute | solution.py:24
  84.4 1.5 %collective-permute-done.6 = f32[2,128]{1,0:T(2,128)S(1)} collective-permute-done((f32[2,128]{1,0:T(2,128)S(1)}, f32[2,128]{1,0:T(2,128)S(1)}, u32[]{:S(2)}, u32[]{:S(2)}) %collective-permute-start.6) | collective-permute-done | bytes 1056 | tf_op jit(solution)/shard_map/ppermute | solution.py:24
  85.9 5.4 %collective-permute-start.7 = (f32[2,128]{1,0:T(2,128)S(1)}, f32[2,128]{1,0:T(2,128)S(1)}, u32[]{:S(2)}, u32[]{:S(2)}) collective-permute-start(f32[2,128]{1,0:T(2,128)S(1)} %add.214), channel_id=1, source_target_pairs={{0,16},{4,20},{8,24},{12,28},{16,0},{20,4},{24,8},{28,12},{32,48},... | collective-permute-start | bytes 3080 | tf_op jit(solution)/shard_map/ppermute | solution.py:24
  91.3 1.5 %collective-permute-done.7 = f32[2,128]{1,0:T(2,128)S(1)} collective-permute-done((f32[2,128]{1,0:T(2,128)S(1)}, f32[2,128]{1,0:T(2,128)S(1)}, u32[]{:S(2)}, u32[]{:S(2)}) %collective-permute-start.7) | collective-permute-done | bytes 1056 | tf_op jit(solution)/shard_map/ppermute | solution.py:24
  92.8 8.8 %collective-permute-start.8 = (f32[2,128]{1,0:T(2,128)S(1)}, f32[2,128]{1,0:T(2,128)S(1)}, u32[]{:S(2)}, u32[]{:S(2)}) collective-permute-start(f32[2,128]{1,0:T(2,128)S(1)} %add.215), channel_id=1, source_target_pairs={{0,32},{4,36},{8,40},{12,44},{16,48},{20,52},{24,56},{28,60},{32,0... | collective-permute-start | bytes 3080 | tf_op jit(solution)/shard_map/ppermute | solution.py:24
  101.7 1.5 %collective-permute-done.8 = f32[2,128]{1,0:T(2,128)S(1)} collective-permute-done((f32[2,128]{1,0:T(2,128)S(1)}, f32[2,128]{1,0:T(2,128)S(1)}, u32[]{:S(2)}, u32[]{:S(2)}) %collective-permute-start.8) | collective-permute-done | bytes 1056 | tf_op jit(solution)/shard_map/ppermute | solution.py:24
  103.2 17.9 %collective-permute-start.9 = (f32[2,128]{1,0:T(2,128)S(1)}, f32[2,128]{1,0:T(2,128)S(1)}, u32[]{:S(2)}, u32[]{:S(2)}) collective-permute-start(f32[2,128]{1,0:T(2,128)S(1)} %add.216), channel_id=1, source_target_pairs={{0,64},{4,68},{8,72},{12,76},{16,80},{20,84},{24,88},{28,92},{32,9... | collective-permute-start | bytes 3080 | tf_op jit(solution)/shard_map/ppermute | solution.py:24
  121.1 1.5 %collective-permute-done.9 = f32[2,128]{1,0:T(2,128)S(1)} collective-permute-done((f32[2,128]{1,0:T(2,128)S(1)}, f32[2,128]{1,0:T(2,128)S(1)}, u32[]{:S(2)}, u32[]{:S(2)}) %collective-permute-start.9) | collective-permute-done | bytes 1056 | tf_op jit(solution)/shard_map/ppermute | solution.py:24
  122.6 6.1 %collective-permute-start.10 = (f32[2,128]{1,0:T(2,128)S(1)}, f32[2,128]{1,0:T(2,128)S(1)}, u32[]{:S(2)}, u32[]{:S(2)}) collective-permute-start(f32[2,128]{1,0:T(2,128)S(1)} %add.217), channel_id=1, source_target_pairs={{0,256},{4,260},{8,264},{12,268},{16,272},{20,276},{24,280},{28,28... | collective-permute-start | bytes 3080 | tf_op jit(solution)/shard_map/ppermute | solution.py:36
  128.7 1.9 %collective-permute-start.11 = (f32[2,128]{1,0:T(2,128)S(1)}, f32[2,128]{1,0:T(2,128)S(1)}, u32[]{:S(2)}, u32[]{:S(2)}) collective-permute-start(f32[2,128]{1,0:T(2,128)S(1)} %add.217), channel_id=1, source_target_pairs={{0,128},{4,132},{8,136},{12,140},{16,144},{20,148},{24,152},{28,15... | collective-permute-start | bytes 3080 | tf_op jit(solution)/shard_map/ppermute | solution.py:36
  130.7 2.7 %multiply_convert_fusion = bf16[512,2,2,128]{0,3,2,1:T(8,128)(2,1)} fusion(f32[512,2,2,128]{0,3,2,1:T(8,128)} %get-tuple-element.31, f32[512,2,2,128]{0,3,2,1:T(8,128)} %bitcast.190, f32[512,2,2]{0,2,1:T(2,128)S(1)} %broadcast_multiply_fusion, f32[128]{0:T(128)S(1)} %copy-done.16, f32[512,2,2]{0,2,1:T(2,128)S(1)} %add_rsqrt_fusion), kind=kLoop, calls=%fused_computation.37 | loop fusion | flops 1835008 | bytes 2638336 | tf_op jit(solution)/shard_map/convert_element_type | solution.py:162
  133.3 2.0 %copy.40 = bf16[1,512,512]{2,1,0:T(8,128)(2,1)} copy(bf16[1,512,512]{1,2,0:T(8,128)(2,1)} %bitcast.202) | data formatting | bytes 1048576
  135.4 2.7 %collective-permute-done.11 = f32[2,128]{1,0:T(2,128)S(1)} collective-permute-done((f32[2,128]{1,0:T(2,128)S(1)}, f32[2,128]{1,0:T(2,128)S(1)}, u32[]{:S(2)}, u32[]{:S(2)}) %collective-permute-start.11) | collective-permute-done | bytes 1056 | tf_op jit(solution)/shard_map/ppermute | solution.py:36
  138.2 3.1 %fusion.31 = (f32[512,2]{0,1:T(2,128)S(1)}, f32[512,2,128]{0,2,1:T(8,128)S(1)}, bf16[512,2,128]{0,2,1:T(8,128)(2,1)}) fusion(bf16[512,2,128]{0,2,1:T(8,128)(2,1)S(1)} %bitcast.197, f32[512,2]{0,1:T(2,128)S(1)} %add_rsqrt_fusion.3, f32[128]{0:T(128)S(1)} %copy-done.15, f32[512,2,256]{0,2,1:T(8,128)} %collective-permute-done.13, ...), kind=kOutput, calls=%fused_computation.68 | convolution fusion | flops 269745152 | bytes 6300160 | tf_op jit(solution)/shard_map/kgtu,tkgd->ukd/dot_general | solution.py:140
  142.2 1.8 %copy.42 = bf16[1,512,256]{2,1,0:T(8,128)(2,1)} copy(bf16[1,512,256]{1,2,0:T(8,128)(2,1)} %bitcast.203) | data formatting | bytes 524288
  (93 shorter events, 22.8 us)
Async XLA Ops:
  0.6 8.3 %copy-start.14 = (bf16[1,512,512]{2,1,0:T(8,128)(2,1)S(1)}, bf16[1,512,512]{2,1,0:T(8,128)(2,1)}, u32[]{:S(2)}) copy-start(bf16[1,512,512]{2,1,0:T(8,128)(2,1)} %param.8) | copy-start | bytes 1572868
  2.9 6.0 %copy-start.2 = (bf16[1,512,256]{1,2,0:T(8,128)(2,1)}, bf16[1,512,256]{1,2,0:T(8,128)(2,1)S(1)}, u32[]{:S(2)}) copy-start(bf16[1,512,256]{1,2,0:T(8,128)(2,1)S(1)} %copy.16) | copy-start | bytes 786436
  2.9 6.4 %copy-start.16 = (f32[128]{0:T(128)S(1)}, f32[128]{0:T(128)}, u32[]{:S(2)}) copy-start(f32[128]{0:T(128)} %param.12) | copy-start | bytes 1540
  3.8 16.1 %collective-permute-start.1 = (bf16[512,2,256]{0,2,1:T(8,128)(2,1)}, bf16[512,2,256]{0,2,1:T(8,128)(2,1)S(1)}, u32[]{:S(2)}, u32[]{:S(2)}) collective-permute-start(bf16[512,2,256]{0,2,1:T(8,128)(2,1)} %pad_maximum_fusion.2), channel_id=1, source_target_pairs={{0,8},{4,12},{8,16},{12,20},{16,24},{20,28},{24,32},{28,36},{32,40... | collective-permute-start | bytes 1572872 | tf_op jit(solution)/shard_map/ppermute | solution.py:19
  7.3 12.7 %collective-permute-start = (bf16[512,2,256]{0,2,1:T(8,128)(2,1)}, bf16[512,2,256]{0,2,1:T(8,128)(2,1)S(1)}, u32[]{:S(2)}, u32[]{:S(2)}) collective-permute-start(bf16[512,2,256]{0,2,1:T(8,128)(2,1)} %pad_maximum_fusion.2), channel_id=1, source_target_pairs={{0,4},{4,8},{8,12},{12,16},{16,20},{20,24},{24,28},{28,32},{32,36}... | collective-permute-start | bytes 1572872 | tf_op jit(solution)/shard_map/ppermute | solution.py:19
  9.1 2.2 %copy-start = (f32[1,512,512]{1,2,0:T(8,128)}, f32[1,512,512]{1,2,0:T(8,128)S(1)}, u32[]{:S(2)}) copy-start(f32[1,512,512]{1,2,0:T(8,128)S(1)} %copy.13) | copy-start | bytes 3145732
  9.1 2.9 %copy-start.15 = (f32[128]{0:T(128)S(1)}, f32[128]{0:T(128)}, u32[]{:S(2)}) copy-start(f32[128]{0:T(128)} %param.13) | copy-start | bytes 1540
  11.3 0.7 copy-start.12
  19.9 2.5 %copy-start.7 = (bf16[512,2,256]{0,2,1:T(8,128)(2,1)}, bf16[512,2,256]{0,2,1:T(8,128)(2,1)S(1)}, u32[]{:S(2)}) copy-start(bf16[512,2,256]{0,2,1:T(8,128)(2,1)S(1)} %collective-permute-done.1) | copy-start | bytes 1572868
  20.0 2.4 %copy-start.5 = (bf16[512,2,256]{0,2,1:T(8,128)(2,1)}, bf16[512,2,256]{0,2,1:T(8,128)(2,1)S(1)}, u32[]{:S(2)}) copy-start(bf16[512,2,256]{0,2,1:T(8,128)(2,1)S(1)} %collective-permute-done) | copy-start | bytes 1572868
  20.1 2.3 %copy-start.10 = (pred[512,512]{0,1:T(8,128)(4,1)S(1)}, pred[512,512]{0,1:T(8,128)(4,1)}, u32[]{:S(2)}) copy-start(pred[512,512]{0,1:T(8,128)(4,1)} %get-tuple-element.22) | copy-start | bytes 786436
  22.4 2.2 %copy-start.4 = (f32[2,512,512,2]{2,1,3,0:T(8,128)S(1)}, f32[2,512,512,2]{2,1,3,0:T(8,128)}, u32[]{:S(2)}) copy-start(f32[2,512,512,2]{2,1,3,0:T(8,128)} %get-tuple-element.28) | copy-start | bytes 12582916
  22.4 2.2 %copy-start.11 = (pred[512,512]{0,1:T(8,128)(4,1)S(1)}, pred[512,512]{0,1:T(8,128)(4,1)}, u32[]{:S(2)}) copy-start(pred[512,512]{0,1:T(8,128)(4,1)} %get-tuple-element.23) | copy-start | bytes 786436
  22.4 2.3 %copy-start.13 = (pred[512,512]{0,1:T(8,128)(4,1)S(1)}, pred[512,512]{0,1:T(8,128)(4,1)}, u32[]{:S(2)}) copy-start(pred[512,512]{0,1:T(8,128)(4,1)} %copy-done.12) | copy-start | bytes 786436
  27.7 1.0 copy-start.3
  28.6 1.1 copy-start.8
  29.6 1.0 copy-start.6
  36.8 101.3 %collective-permute-start.13 = (f32[512,2,256]{0,2,1:T(8,128)}, f32[512,2,256]{0,2,1:T(8,128)}, u32[]{:S(2)}, u32[]{:S(2)}) collective-permute-start(f32[512,2,256]{0,2,1:T(8,128)} %pad_maximum_fusion.1), channel_id=1, source_target_pairs={{8,0},{12,4},{16,8},{20,12},{24,16},{28,20},{32,24},{36,28},{40,32... | collective-permute-start | bytes 3145736 | tf_op jit(solution)/shard_map/ppermute | solution.py:19
  39.0 1.2 copy-start.1
  42.8 9.4 %collective-permute-start.2 = (f32[2,128]{1,0:T(2,128)S(1)}, f32[2,128]{1,0:T(2,128)S(1)}, u32[]{:S(2)}, u32[]{:S(2)}) collective-permute-start(f32[2,128]{1,0:T(2,128)S(1)} %pad_maximum_fusion.3), channel_id=1, source_target_pairs={{0,1},{1,0},{2,3},{3,2},{4,5},{5,4},{6,7},{7,6},{8,9},{9,8},{10,11... | collective-permute-start | bytes 3080 | tf_op jit(solution)/shard_map/ppermute | solution.py:24
  50.8 87.3 %copy-start.9 = (f32[512,2,128]{0,2,1:T(8,128)S(1)}, f32[512,2,128]{0,2,1:T(8,128)}, u32[]{:S(2)}) copy-start(f32[512,2,128]{0,2,1:T(8,128)} %get-tuple-element.35) | copy-start | bytes 1572868
  50.8 87.3 %collective-permute-start.12 = (f32[512,2,256]{0,2,1:T(8,128)}, f32[512,2,256]{0,2,1:T(8,128)}, u32[]{:S(2)}, u32[]{:S(2)}) collective-permute-start(f32[512,2,256]{0,2,1:T(8,128)} %pad_maximum_fusion), channel_id=1, source_target_pairs={{4,0},{8,4},{12,8},{16,12},{20,16},{24,20},{28,24},{32,28},{36,32}... | collective-permute-start | bytes 3145736 | tf_op jit(solution)/shard_map/ppermute | solution.py:19
  52.3 7.0 %collective-permute-start.3 = (f32[2,128]{1,0:T(2,128)S(1)}, f32[2,128]{1,0:T(2,128)S(1)}, u32[]{:S(2)}, u32[]{:S(2)}) collective-permute-start(f32[2,128]{1,0:T(2,128)S(1)} %fusion.51), channel_id=1, source_target_pairs={{0,2},{1,3},{2,0},{3,1},{4,6},{5,7},{6,4},{7,5},{8,10},{9,11},{10,... | collective-permute-start | bytes 3080 | tf_op jit(solution)/shard_map/ppermute | solution.py:24
  59.2 12.7 %collective-permute-start.4 = (f32[2,128]{1,0:T(2,128)S(1)}, f32[2,128]{1,0:T(2,128)S(1)}, u32[]{:S(2)}, u32[]{:S(2)}) collective-permute-start(f32[2,128]{1,0:T(2,128)S(1)} %fusion.78), channel_id=1, source_target_pairs={{0,384},{384,0},{1,385},{385,1},{2,386},{386,2},{3,387},{387,3},{4... | collective-permute-start | bytes 3080 | tf_op jit(solution)/shard_map/ppermute | solution.py:24
  72.0 4.9 %collective-permute-start.5 = (f32[2,128]{1,0:T(2,128)S(1)}, f32[2,128]{1,0:T(2,128)S(1)}, u32[]{:S(2)}, u32[]{:S(2)}) collective-permute-start(f32[2,128]{1,0:T(2,128)S(1)} %add.212), channel_id=1, source_target_pairs={{0,4},{4,0},{8,12},{12,8},{16,20},{20,16},{24,28},{28,24},{32,36},... | collective-permute-start | bytes 3080 | tf_op jit(solution)/shard_map/ppermute | solution.py:24
  76.9 9.0 %collective-permute-start.6 = (f32[2,128]{1,0:T(2,128)S(1)}, f32[2,128]{1,0:T(2,128)S(1)}, u32[]{:S(2)}, u32[]{:S(2)}) collective-permute-start(f32[2,128]{1,0:T(2,128)S(1)} %add.213), channel_id=1, source_target_pairs={{0,8},{4,12},{8,0},{12,4},{16,24},{20,28},{24,16},{28,20},{32,40},... | collective-permute-start | bytes 3080 | tf_op jit(solution)/shard_map/ppermute | solution.py:24
  85.9 6.9 %collective-permute-start.7 = (f32[2,128]{1,0:T(2,128)S(1)}, f32[2,128]{1,0:T(2,128)S(1)}, u32[]{:S(2)}, u32[]{:S(2)}) collective-permute-start(f32[2,128]{1,0:T(2,128)S(1)} %add.214), channel_id=1, source_target_pairs={{0,16},{4,20},{8,24},{12,28},{16,0},{20,4},{24,8},{28,12},{32,48},... | collective-permute-start | bytes 3080 | tf_op jit(solution)/shard_map/ppermute | solution.py:24
  92.8 10.4 %collective-permute-start.8 = (f32[2,128]{1,0:T(2,128)S(1)}, f32[2,128]{1,0:T(2,128)S(1)}, u32[]{:S(2)}, u32[]{:S(2)}) collective-permute-start(f32[2,128]{1,0:T(2,128)S(1)} %add.215), channel_id=1, source_target_pairs={{0,32},{4,36},{8,40},{12,44},{16,48},{20,52},{24,56},{28,60},{32,0... | collective-permute-start | bytes 3080 | tf_op jit(solution)/shard_map/ppermute | solution.py:24
  103.2 19.4 %collective-permute-start.9 = (f32[2,128]{1,0:T(2,128)S(1)}, f32[2,128]{1,0:T(2,128)S(1)}, u32[]{:S(2)}, u32[]{:S(2)}) collective-permute-start(f32[2,128]{1,0:T(2,128)S(1)} %add.216), channel_id=1, source_target_pairs={{0,64},{4,68},{8,72},{12,76},{16,80},{20,84},{24,88},{28,92},{32,9... | collective-permute-start | bytes 3080 | tf_op jit(solution)/shard_map/ppermute | solution.py:24
  122.6 12.8 %collective-permute-start.10 = (f32[2,128]{1,0:T(2,128)S(1)}, f32[2,128]{1,0:T(2,128)S(1)}, u32[]{:S(2)}, u32[]{:S(2)}) collective-permute-start(f32[2,128]{1,0:T(2,128)S(1)} %add.217), channel_id=1, source_target_pairs={{0,256},{4,260},{8,264},{12,268},{16,272},{20,276},{24,280},{28,28... | collective-permute-start | bytes 3080 | tf_op jit(solution)/shard_map/ppermute | solution.py:36
  128.7 9.4 %collective-permute-start.11 = (f32[2,128]{1,0:T(2,128)S(1)}, f32[2,128]{1,0:T(2,128)S(1)}, u32[]{:S(2)}, u32[]{:S(2)}) collective-permute-start(f32[2,128]{1,0:T(2,128)S(1)} %add.217), channel_id=1, source_target_pairs={{0,128},{4,132},{8,136},{12,140},{16,144},{20,148},{24,152},{28,15... | collective-permute-start | bytes 3080 | tf_op jit(solution)/shard_map/ppermute | solution.py:36
  141.3 2.8 %copy-start.18 = (f32[2]{0:T(128)S(1)}, f32[2]{0:T(128)}, u32[]{:S(2)}) copy-start(f32[2]{0:T(128)} %constant.83) | copy-start | bytes 28
  (1 other events, 0.7 us)

commit v4 on v3

--- a/solution.py
+++ b/solution.py
@@ -148,7 +148,9 @@
     partial_sums = jnp.stack([jnp.sum(dquery_n * query_hat, axis=(0, 1, 2)) * factor, key_term])
     summed = total_over_devices(partial_sums)
     returns = [
-        passed_along(jnp.concatenate(pieces[distance], axis=-1), "ctx", -distance)
+        passed_along(
+            jnp.concatenate(pieces[distance], axis=-1).astype(jnp.bfloat16), "ctx", -distance
+        ).astype(jnp.float32)
         for distance in range(1, reach + 1)
     ]
     summed, *returns = lax.optimization_barrier((summed, *returns))

time: 146 us -> 138 us (0.945)
  starting transfers between devices: 79.6 us -> 67.6 us
  waiting for transfers between devices: 19.8 us -> 22.2 us
    ppermute x8, starting transfers between devices: 63.7 us -> 51.5 us  [exchanged_sum(): lax.ppermute(value, axis, [(source, source ^ stride) for source in range(...]
    convert_element_type x0 -> x2, other arithmetic: none -> 2.31 us  [shards(): returns = [passed_along(jnp.concatenate(pieces[distance], axis=-1).astype...]
    convert_element_type x1, other arithmetic: 2.66 us -> 1.13 us  [shards(): query_grad = norm_backward(dquery_n, query_hat, query_inv, query_gain, fa...]
    unnamed x44 -> x58, local copies, waits for them, and re-layouts: 12 us -> 12.1 us
  transfers between devices with their start and end apart: 14 -> 14, of which waited for: 9 -> 7; matrix products, arithmetic and copies ran while one was open for 11% -> 12% of each run, Pallas kernels for 0% -> 0%
where the time goes in v4:
time: 138 us; the launch traced here: 137 us
  starting transfers between devices  67.6 us (49%)
  matrix products  22.2 us (16%)
  waiting for transfers between devices  22.2 us (16%)
  local copies, waits for them, and re-layouts  12.3 us (9%)
  other arithmetic  11.3 us (8%)
  between operations  1.41 us (1%)
    ppermute x8, starting transfers between devices, exchanged_sum(): lax.ppermute(value, axis, [(source, source ^ stride) for source in range(...  51.5 us
    ppermute x8, waiting for transfers between devices, exchanged_sum(): lax.ppermute(value, axis, [(source, source ^ stride) for source in range(...  14.4 us
    unnamed x58, local copies, waits for them, and re-layouts  12.1 us
    ppermute x2, starting transfers between devices, three_way_sum(): received.append(lax.ppermute(value, axis, pairs))  8.63 us
    ppermute x4, starting transfers between devices, passed_along(): lax.ppermute(value, axis, [(source, source + steps) for source in range(i...  7.55 us
    dot_general x3, matrix products, forward_block(): jnp.einsum('tkgd,ukd->kgtu', query_n, key_block, preferred_element_type=j...  6.43 us
    dot_general x3, matrix products, shards(): jnp.einsum('kgtu,tkgd->ukd', prob, grads_in, preferred_element_type=jnp.f...  4.8 us
    dot_general x3, matrix products, shards(): jnp.einsum('kgtu,tkgd->ukd', dscore, query_n, preferred_element_type=jnp....  4.66 us
  transfers between devices with their start and end apart: 14, of which 7 were waited for; matrix products, arithmetic and copies ran while one was open for 12% of the time, Pallas kernels for 0%

profile of v4, /device:TPU:2, one launch (start us, length us, event | category | flops | bytes accessed | tf_op | source)
XLA Modules:
  0.0 137.0 jit_solution(10231291699075278605)
XLA Ops:
  3.8 3.5 %collective-permute-start.1 = (bf16[512,2,256]{0,2,1:T(8,128)(2,1)}, bf16[512,2,256]{0,2,1:T(8,128)(2,1)S(1)}, u32[]{:S(2)}, u32[]{:S(2)}) collective-permute-start(bf16[512,2,256]{0,2,1:T(8,128)(2,1)} %pad_maximum_fusion), channel_id=1, source_target_pairs={{0,8},{4,12},{8,16},{12,20},{16,24},{20,28},{24,32},{28,36},{32,40... | collective-permute-start | bytes 1572872 | tf_op jit(solution)/shard_map/ppermute | solution.py:19
  7.3 1.5 %collective-permute-start = (bf16[512,2,256]{0,2,1:T(8,128)(2,1)}, bf16[512,2,256]{0,2,1:T(8,128)(2,1)S(1)}, u32[]{:S(2)}, u32[]{:S(2)}) collective-permute-start(bf16[512,2,256]{0,2,1:T(8,128)(2,1)} %pad_maximum_fusion), channel_id=1, source_target_pairs={{0,4},{4,8},{8,12},{12,16},{16,20},{20,24},{24,28},{28,32},{32,36}... | collective-permute-start | bytes 1572872 | tf_op jit(solution)/shard_map/ppermute | solution.py:19
  9.6 1.7 %fusion.19 = (pred[512,512]{0,1:T(8,128)(4,1)}, pred[512,512]{0,1:T(8,128)(4,1)}, pred[512,512]{0,1:T(8,128)(4,1)S(1)}) fusion(s32[512]{0:T(512)S(1)} %iota_add_fusion.2, s32[512]{0:T(512)S(1)} %bitcast.216, s32[512]{0:T(512)S(1)} %get-tuple-element.39, s32[512]{0:T(512)S(1)} %get-tuple-element.38), kind=kLoop, calls=%fused_computation.48 | loop fusion | flops 4718592 | bytes 794624 | tf_op jit(solution)/shard_map/and | solution.py:96
  12.0 3.0 %fusion.6 = (f32[2,2,512]{2,1,0:T(2,128)S(1)}, f32[2,512,512,2]{2,1,3,0:T(8,128)}) fusion(pred[512,512]{0,1:T(8,128)(4,1)S(1)} %get-tuple-element.28, bf16[512,2,2,128]{0,3,2,1:T(8,128)(2,1)S(1)} %multiply_convert_fusion.1, bf16[512,2,128]{0,2,1:T(8,128)(2,1)S(1)} %bitcast.202, f32[128]{0:T(128)S(1)} %copy-done.22, f32[512,2]{0,1:T(2,128)S(1)} %add_rsqrt_fusion.3), kind=kOutput, calls=%fused_computation.15 | convolution fusion | flops 271054848 | bytes 5255680 | tf_op jit(solution)/shard_map/tkgd,ukd->kgtu/dot_general | solution.py:103
  16.2 3.6 %collective-permute-done.1 = bf16[512,2,256]{0,2,1:T(8,128)(2,1)S(1)} collective-permute-done((bf16[512,2,256]{0,2,1:T(8,128)(2,1)}, bf16[512,2,256]{0,2,1:T(8,128)(2,1)S(1)}, u32[]{:S(2)}, u32[]{:S(2)}) %collective-permute-start.1) | collective-permute-done | bytes 524320 | tf_op jit(solution)/shard_map/ppermute | solution.py:19
  20.1 2.3 %fusion.8 = (f32[2,2,512]{2,1,0:T(2,128)S(1)}, f32[2,512,512,2]{2,1,3,0:T(8,128)S(1)}) fusion(pred[512,512]{0,1:T(8,128)(4,1)} %get-tuple-element.27, bf16[512,2,2,128]{0,3,2,1:T(8,128)(2,1)S(1)} %multiply_convert_fusion.1, f32[512,2]{0,1:T(2,128)S(1)} %add_rsqrt_fusion.1, f32[128]{0:T(128)S(1)} %copy-done.22, ...), kind=kOutput, calls=%fused_computation.17 | convolution fusion | flops 271054848 | bytes 5255680 | tf_op jit(solution)/shard_map/tkgd,ukd->kgtu/dot_general | solution.py:103
  24.7 2.2 %divide_convert_fusion.1 = (bf16[2,2,512,512]{2,3,1,0:T(8,128)(2,1)S(1)}, bf16[2,2,512,512]{2,3,1,0:T(8,128)(2,1)S(1)}, bf16[2,2,512,512]{2,3,1,0:T(8,128)(2,1)S(1)}) fusion(f32[2,512,512,2]{2,1,3,0:T(8,128)S(1)} %get-tuple-element.34, f32[2,2,512]{2,1,0:T(2,128)S(1)} %add_add_fusion, pred[512,512]{0,1:T(8,128)(4,1)S(1)} %copy-done.15, ...), kind=kLoop, calls=%fused_computation.13 | loop fusion | flops 9437184 | bytes 19668992 | tf_op jit(solution)/shard_map/convert_element_type | solution.py:112
  30.3 1.6 %fusion.34 = (f32[128]{0:T(128)S(1)}, f32[512,2,128]{0,2,1:T(8,128)}) fusion(bf16[512,2,128]{0,2,1:T(8,128)(2,1)S(1)} %bitcast.203, f32[512,2]{0,1:T(2,128)S(1)} %add_rsqrt_fusion.3, bf16[512,2,2,128]{0,3,2,1:T(8,128)(2,1)S(1)} %multiply_convert_fusion.1, bf16[2,2,512,512]{2,3,1,0:T(8,128)(2,1)S(1)} %fusion.5), kind=kOutput, calls=%fused_computation.69 | convolution fusion | flops 268959616 | bytes 3412480 | tf_op jit(solution)/shard_map/kgtu,tkgd->ukd/dot_general | solution.py:137
  35.2 1.6 %multiply_reduce_fusion = (f32[128]{0:T(128)S(1)}, f32[512,2,2]{0,2,1:T(2,128)S(1)}, f32[512,2,2,128]{0,3,2,1:T(8,128)}) fusion(f32[512,2,2,128]{0,3,2,1:T(8,128)S(1)} %bitcast.198, f32[512,2,2]{0,2,1:T(2,128)S(1)} %add_rsqrt_fusion, f32[128]{0:T(128)S(1)} %copy-done.23, f32[2,128,2,512]{3,1,2,0:T(8,128)S(1)} %convolution_add_fusion.1, ...), kind=kOutput, calls=%fused_computation.38 | convolution fusion | flops 271054720 | bytes 5527040 | tf_op jit(solution)/shard_map/kgtu,ukd->tkgd/dot_general | solution.py:134
  36.8 1.5 %fusion.56 = (bf16[512,2,128]{0,2,1:T(8,128)(2,1)}, f32[128]{0:T(128)S(1)}) fusion(f32[512,2]{0,1:T(2,128)S(1)} %add_rsqrt_fusion.1, bf16[512,2,256]{0,2,1:T(8,128)(2,1)S(1)} %copy-done.13, bf16[512,2,2,128]{0,3,2,1:T(8,128)(2,1)S(1)} %multiply_convert_fusion.1, bf16[2,2,512,512]{2,3,1,0:T(8,128)(2,1)S(1)} %fusion.1), kind=kOutput, calls=%fused_computation.107 | convolution fusion | flops 269090688 | bytes 3150336 | tf_op jit(solution)/shard_map/kgtu,tkgd->ukd/dot_general | solution.py:137
  38.3 1.5 %fusion.57 = (bf16[512,2,128]{0,2,1:T(8,128)(2,1)}, f32[128]{0:T(128)S(1)}) fusion(f32[512,2]{0,1:T(2,128)S(1)} %add_rsqrt_fusion.2, bf16[512,2,256]{0,2,1:T(8,128)(2,1)S(1)} %copy-done.11, bf16[512,2,2,128]{0,3,2,1:T(8,128)(2,1)S(1)} %multiply_convert_fusion.1, bf16[2,2,512,512]{2,3,1,0:T(8,128)(2,1)S(1)} %fusion.3), kind=kOutput, calls=%fused_computation.108 | convolution fusion | flops 269090688 | bytes 3150336 | tf_op jit(solution)/shard_map/kgtu,tkgd->ukd/dot_general | solution.py:137
  39.9 6.9 %collective-permute-start.2 = (f32[2,128]{1,0:T(2,128)S(1)}, f32[2,128]{1,0:T(2,128)S(1)}, u32[]{:S(2)}, u32[]{:S(2)}) collective-permute-start(f32[2,128]{1,0:T(2,128)S(1)} %pad_maximum_fusion.3), channel_id=1, source_target_pairs={{0,1},{1,0},{2,3},{3,2},{4,5},{5,4},{6,7},{7,6},{8,9},{9,8},{10,11... | collective-permute-start | bytes 3080 | tf_op jit(solution)/shard_map/ppermute | solution.py:24
  46.8 1.5 %collective-permute-done.2 = f32[2,128]{1,0:T(2,128)S(1)} collective-permute-done((f32[2,128]{1,0:T(2,128)S(1)}, f32[2,128]{1,0:T(2,128)S(1)}, u32[]{:S(2)}, u32[]{:S(2)}) %collective-permute-start.2) | collective-permute-done | bytes 1056 | tf_op jit(solution)/shard_map/ppermute | solution.py:24
  48.4 1.9 %collective-permute-start.3 = (f32[2,128]{1,0:T(2,128)S(1)}, f32[2,128]{1,0:T(2,128)S(1)}, u32[]{:S(2)}, u32[]{:S(2)}) collective-permute-start(f32[2,128]{1,0:T(2,128)S(1)} %fusion.55), channel_id=1, source_target_pairs={{0,2},{1,3},{2,0},{3,1},{4,6},{5,7},{6,4},{7,5},{8,10},{9,11},{10,... | collective-permute-start | bytes 3080 | tf_op jit(solution)/shard_map/ppermute | solution.py:24
  50.3 5.0 %collective-permute-done.3 = f32[2,128]{1,0:T(2,128)S(1)} collective-permute-done((f32[2,128]{1,0:T(2,128)S(1)}, f32[2,128]{1,0:T(2,128)S(1)}, u32[]{:S(2)}, u32[]{:S(2)}) %collective-permute-start.3) | collective-permute-done | bytes 1056 | tf_op jit(solution)/shard_map/ppermute | solution.py:24
  55.3 12.1 %collective-permute-start.4 = (f32[2,128]{1,0:T(2,128)S(1)}, f32[2,128]{1,0:T(2,128)S(1)}, u32[]{:S(2)}, u32[]{:S(2)}) collective-permute-start(f32[2,128]{1,0:T(2,128)S(1)} %fusion.84), channel_id=1, source_target_pairs={{0,384},{384,0},{1,385},{385,1},{2,386},{386,2},{3,387},{387,3},{4... | collective-permute-start | bytes 3080 | tf_op jit(solution)/shard_map/ppermute | solution.py:24
  67.5 1.5 %collective-permute-done.4 = f32[2,128]{1,0:T(2,128)S(1)} collective-permute-done((f32[2,128]{1,0:T(2,128)S(1)}, f32[2,128]{1,0:T(2,128)S(1)}, u32[]{:S(2)}, u32[]{:S(2)}) %collective-permute-start.4) | collective-permute-done | bytes 1056 | tf_op jit(solution)/shard_map/ppermute | solution.py:24
  69.0 3.3 %collective-permute-start.5 = (f32[2,128]{1,0:T(2,128)S(1)}, f32[2,128]{1,0:T(2,128)S(1)}, u32[]{:S(2)}, u32[]{:S(2)}) collective-permute-start(f32[2,128]{1,0:T(2,128)S(1)} %add.212), channel_id=1, source_target_pairs={{0,4},{4,0},{8,12},{12,8},{16,20},{20,16},{24,28},{28,24},{32,36},... | collective-permute-start | bytes 3080 | tf_op jit(solution)/shard_map/ppermute | solution.py:24
  72.4 2.4 %fusion.16 = bf16[512,2,128]{0,2,1:T(8,128)(2,1)S(1)} fusion(bf16[2,2,512,512]{2,3,1,0:T(8,128)(2,1)} %copy-done.2, bf16[512,2,2,128]{0,3,2,1:T(8,128)(2,1)S(1)} %bitcast.193), kind=kOutput, calls=%fused_computation.36 | convolution fusion | flops 268566528 | bytes 2883584 | tf_op jit(solution)/shard_map/kgtu,tkgd->ukd/dot_general | solution.py:140
  74.8 7.5 %collective-permute-start.6 = (f32[2,128]{1,0:T(2,128)S(1)}, f32[2,128]{1,0:T(2,128)S(1)}, u32[]{:S(2)}, u32[]{:S(2)}) collective-permute-start(f32[2,128]{1,0:T(2,128)S(1)} %add.213), channel_id=1, source_target_pairs={{0,8},{4,12},{8,0},{12,4},{16,24},{20,28},{24,16},{28,20},{32,40},... | collective-permute-start | bytes 3080 | tf_op jit(solution)/shard_map/ppermute | solution.py:24
  83.9 4.9 %collective-permute-start.7 = (f32[2,128]{1,0:T(2,128)S(1)}, f32[2,128]{1,0:T(2,128)S(1)}, u32[]{:S(2)}, u32[]{:S(2)}) collective-permute-start(f32[2,128]{1,0:T(2,128)S(1)} %add.214), channel_id=1, source_target_pairs={{0,16},{4,20},{8,24},{12,28},{16,0},{20,4},{24,8},{28,12},{32,48},... | collective-permute-start | bytes 3080 | tf_op jit(solution)/shard_map/ppermute | solution.py:24
  89.7 1.3 collective-permute-start.13
  91.0 8.6 %collective-permute-start.8 = (f32[2,128]{1,0:T(2,128)S(1)}, f32[2,128]{1,0:T(2,128)S(1)}, u32[]{:S(2)}, u32[]{:S(2)}) collective-permute-start(f32[2,128]{1,0:T(2,128)S(1)} %add.215), channel_id=1, source_target_pairs={{0,32},{4,36},{8,40},{12,44},{16,48},{20,52},{24,56},{28,60},{32,0... | collective-permute-start | bytes 3080 | tf_op jit(solution)/shard_map/ppermute | solution.py:24
  100.4 1.3 collective-permute-start.12
  101.8 6.1 %collective-permute-start.9 = (f32[2,128]{1,0:T(2,128)S(1)}, f32[2,128]{1,0:T(2,128)S(1)}, u32[]{:S(2)}, u32[]{:S(2)}) collective-permute-start(f32[2,128]{1,0:T(2,128)S(1)} %add.216), channel_id=1, source_target_pairs={{0,64},{4,68},{8,72},{12,76},{16,80},{20,84},{24,88},{28,92},{32,9... | collective-permute-start | bytes 3080 | tf_op jit(solution)/shard_map/ppermute | solution.py:24
  107.9 5.7 %collective-permute-done.9 = f32[2,128]{1,0:T(2,128)S(1)} collective-permute-done((f32[2,128]{1,0:T(2,128)S(1)}, f32[2,128]{1,0:T(2,128)S(1)}, u32[]{:S(2)}, u32[]{:S(2)}) %collective-permute-start.9) | collective-permute-done | bytes 1056 | tf_op jit(solution)/shard_map/ppermute | solution.py:24
  113.6 6.7 %collective-permute-start.10 = (f32[2,128]{1,0:T(2,128)S(1)}, f32[2,128]{1,0:T(2,128)S(1)}, u32[]{:S(2)}, u32[]{:S(2)}) collective-permute-start(f32[2,128]{1,0:T(2,128)S(1)} %add.217), channel_id=1, source_target_pairs={{0,256},{4,260},{8,264},{12,268},{16,272},{20,276},{24,280},{28,28... | collective-permute-start | bytes 3080 | tf_op jit(solution)/shard_map/ppermute | solution.py:36
  120.3 1.9 %collective-permute-start.11 = (f32[2,128]{1,0:T(2,128)S(1)}, f32[2,128]{1,0:T(2,128)S(1)}, u32[]{:S(2)}, u32[]{:S(2)}) collective-permute-start(f32[2,128]{1,0:T(2,128)S(1)} %add.217), channel_id=1, source_target_pairs={{0,128},{4,132},{8,136},{12,140},{16,144},{20,148},{24,152},{28,15... | collective-permute-start | bytes 3080 | tf_op jit(solution)/shard_map/ppermute | solution.py:36
  123.4 2.2 %copy.40 = bf16[1,512,512]{2,1,0:T(8,128)(2,1)} copy(bf16[1,512,512]{1,2,0:T(8,128)(2,1)} %bitcast.210) | data formatting | bytes 1048576
  125.6 4.1 %collective-permute-done.11 = f32[2,128]{1,0:T(2,128)S(1)} collective-permute-done((f32[2,128]{1,0:T(2,128)S(1)}, f32[2,128]{1,0:T(2,128)S(1)}, u32[]{:S(2)}, u32[]{:S(2)}) %collective-permute-start.11) | collective-permute-done | bytes 1056 | tf_op jit(solution)/shard_map/ppermute | solution.py:36
  132.0 1.6 %fusion.35 = (f32[512,2]{0,1:T(2,128)S(1)}, f32[512,2,128]{0,2,1:T(8,128)S(1)}, bf16[512,2,128]{0,2,1:T(8,128)(2,1)}) fusion(bf16[512,2,128]{0,2,1:T(8,128)(2,1)S(1)} %bitcast.205, f32[512,2]{0,1:T(2,128)S(1)} %add_rsqrt_fusion.3, f32[128]{0:T(128)S(1)} %copy-done.22, f32[512,2,256]{0,2,1:T(8,128)S(1)} %convert_element_type.103, ...), kind=kOutput, calls=%fused_computation.70 | convolution fusion | flops 269745152 | bytes 6300160 | tf_op jit(solution)/shard_map/kgtu,tkgd->ukd/dot_general | solution.py:140
  134.6 1.8 %copy.42 = bf16[1,512,256]{2,1,0:T(8,128)(2,1)} copy(bf16[1,512,256]{1,2,0:T(8,128)(2,1)} %bitcast.211) | data formatting | bytes 524288
  (109 shorter events, 23.0 us)
Async XLA Ops:
  0.6 8.2 %copy-start.21 = (bf16[1,512,512]{2,1,0:T(8,128)(2,1)S(1)}, bf16[1,512,512]{2,1,0:T(8,128)(2,1)}, u32[]{:S(2)}) copy-start(bf16[1,512,512]{2,1,0:T(8,128)(2,1)} %param.8) | copy-start | bytes 1572868
  2.9 6.6 %copy-start.7 = (bf16[1,512,256]{1,2,0:T(8,128)(2,1)}, bf16[1,512,256]{1,2,0:T(8,128)(2,1)S(1)}, u32[]{:S(2)}) copy-start(bf16[1,512,256]{1,2,0:T(8,128)(2,1)S(1)} %copy.16) | copy-start | bytes 786436
  2.9 6.4 %copy-start.23 = (f32[128]{0:T(128)S(1)}, f32[128]{0:T(128)}, u32[]{:S(2)}) copy-start(f32[128]{0:T(128)} %param.12) | copy-start | bytes 1540
  3.8 16.1 %collective-permute-start.1 = (bf16[512,2,256]{0,2,1:T(8,128)(2,1)}, bf16[512,2,256]{0,2,1:T(8,128)(2,1)S(1)}, u32[]{:S(2)}, u32[]{:S(2)}) collective-permute-start(bf16[512,2,256]{0,2,1:T(8,128)(2,1)} %pad_maximum_fusion), channel_id=1, source_target_pairs={{0,8},{4,12},{8,16},{12,20},{16,24},{20,28},{24,32},{28,36},{32,40... | collective-permute-start | bytes 1572872 | tf_op jit(solution)/shard_map/ppermute | solution.py:19
  7.3 12.7 %collective-permute-start = (bf16[512,2,256]{0,2,1:T(8,128)(2,1)}, bf16[512,2,256]{0,2,1:T(8,128)(2,1)S(1)}, u32[]{:S(2)}, u32[]{:S(2)}) collective-permute-start(bf16[512,2,256]{0,2,1:T(8,128)(2,1)} %pad_maximum_fusion), channel_id=1, source_target_pairs={{0,4},{4,8},{8,12},{12,16},{16,20},{20,24},{24,28},{28,32},{32,36}... | collective-permute-start | bytes 1572872 | tf_op jit(solution)/shard_map/ppermute | solution.py:19
  9.1 5.8 %copy-start.3 = (f32[1,512,512]{1,2,0:T(8,128)}, f32[1,512,512]{1,2,0:T(8,128)S(1)}, u32[]{:S(2)}) copy-start(f32[1,512,512]{1,2,0:T(8,128)S(1)} %copy.13) | copy-start | bytes 3145732
  9.1 2.8 %copy-start.22 = (f32[128]{0:T(128)S(1)}, f32[128]{0:T(128)}, u32[]{:S(2)}) copy-start(f32[128]{0:T(128)} %param.13) | copy-start | bytes 1540
  19.9 2.5 %copy-start.12 = (bf16[512,2,256]{0,2,1:T(8,128)(2,1)}, bf16[512,2,256]{0,2,1:T(8,128)(2,1)S(1)}, u32[]{:S(2)}) copy-start(bf16[512,2,256]{0,2,1:T(8,128)(2,1)S(1)} %collective-permute-done.1) | copy-start | bytes 1572868
  20.0 2.4 %copy-start.10 = (bf16[512,2,256]{0,2,1:T(8,128)(2,1)}, bf16[512,2,256]{0,2,1:T(8,128)(2,1)S(1)}, u32[]{:S(2)}) copy-start(bf16[512,2,256]{0,2,1:T(8,128)(2,1)S(1)} %collective-permute-done) | copy-start | bytes 1572868
  20.1 2.3 %copy-start.15 = (pred[512,512]{0,1:T(8,128)(4,1)S(1)}, pred[512,512]{0,1:T(8,128)(4,1)}, u32[]{:S(2)}) copy-start(pred[512,512]{0,1:T(8,128)(4,1)} %get-tuple-element.26) | copy-start | bytes 786436
  24.7 2.3 %copy-start.8 = (bf16[1,512,256]{1,2,0:T(8,128)(2,1)S(1)}, bf16[1,512,256]{1,2,0:T(8,128)(2,1)}, u32[]{:S(2)}) copy-start(bf16[1,512,256]{1,2,0:T(8,128)(2,1)} %copy-done.7) | copy-start | bytes 786436
  26.9 2.6 %copy-start = (bf16[2,2,512,512]{2,3,1,0:T(8,128)(2,1)}, bf16[2,2,512,512]{2,3,1,0:T(8,128)(2,1)S(1)}, u32[]{:S(2)}) copy-start(bf16[2,2,512,512]{2,3,1,0:T(8,128)(2,1)S(1)} %get-tuple-element.25) | copy-start | bytes 6291460
  27.0 5.5 %copy-start.2 = (bf16[2,2,512,512]{2,3,1,0:T(8,128)(2,1)}, bf16[2,2,512,512]{2,3,1,0:T(8,128)(2,1)S(1)}, u32[]{:S(2)}) copy-start(bf16[2,2,512,512]{2,3,1,0:T(8,128)(2,1)S(1)} %get-tuple-element.24) | copy-start | bytes 6291460
  39.9 8.5 %collective-permute-start.2 = (f32[2,128]{1,0:T(2,128)S(1)}, f32[2,128]{1,0:T(2,128)S(1)}, u32[]{:S(2)}, u32[]{:S(2)}) collective-permute-start(f32[2,128]{1,0:T(2,128)S(1)} %pad_maximum_fusion.3), channel_id=1, source_target_pairs={{0,1},{1,0},{2,3},{3,2},{4,5},{5,4},{6,7},{7,6},{8,9},{9,8},{10,11... | collective-permute-start | bytes 3080 | tf_op jit(solution)/shard_map/ppermute | solution.py:24
  48.4 7.0 %collective-permute-start.3 = (f32[2,128]{1,0:T(2,128)S(1)}, f32[2,128]{1,0:T(2,128)S(1)}, u32[]{:S(2)}, u32[]{:S(2)}) collective-permute-start(f32[2,128]{1,0:T(2,128)S(1)} %fusion.55), channel_id=1, source_target_pairs={{0,2},{1,3},{2,0},{3,1},{4,6},{5,7},{6,4},{7,5},{8,10},{9,11},{10,... | collective-permute-start | bytes 3080 | tf_op jit(solution)/shard_map/ppermute | solution.py:24
  55.3 13.7 %collective-permute-start.4 = (f32[2,128]{1,0:T(2,128)S(1)}, f32[2,128]{1,0:T(2,128)S(1)}, u32[]{:S(2)}, u32[]{:S(2)}) collective-permute-start(f32[2,128]{1,0:T(2,128)S(1)} %fusion.84), channel_id=1, source_target_pairs={{0,384},{384,0},{1,385},{385,1},{2,386},{386,2},{3,387},{387,3},{4... | collective-permute-start | bytes 3080 | tf_op jit(solution)/shard_map/ppermute | solution.py:24
  69.0 5.8 %collective-permute-start.5 = (f32[2,128]{1,0:T(2,128)S(1)}, f32[2,128]{1,0:T(2,128)S(1)}, u32[]{:S(2)}, u32[]{:S(2)}) collective-permute-start(f32[2,128]{1,0:T(2,128)S(1)} %add.212), channel_id=1, source_target_pairs={{0,4},{4,0},{8,12},{12,8},{16,20},{20,16},{24,28},{28,24},{32,36},... | collective-permute-start | bytes 3080 | tf_op jit(solution)/shard_map/ppermute | solution.py:24
  74.8 14.0 %copy-start.20 = (bf16[512,2,128]{0,2,1:T(8,128)(2,1)S(1)}, bf16[512,2,128]{0,2,1:T(8,128)(2,1)}, u32[]{:S(2)}) copy-start(bf16[512,2,128]{0,2,1:T(8,128)(2,1)} %get-tuple-element.19) | copy-start | bytes 786436
  74.8 24.8 %copy-start.19 = (bf16[512,2,128]{0,2,1:T(8,128)(2,1)S(1)}, bf16[512,2,128]{0,2,1:T(8,128)(2,1)}, u32[]{:S(2)}) copy-start(bf16[512,2,128]{0,2,1:T(8,128)(2,1)} %get-tuple-element.21) | copy-start | bytes 786436
  74.8 47.4 %copy-start.5 = (f32[1,512,512]{1,2,0:T(8,128)S(1)}, f32[1,512,512]{1,2,0:T(8,128)}, u32[]{:S(2)}) copy-start(f32[1,512,512]{1,2,0:T(8,128)} %copy-done.3) | copy-start | bytes 3145732
  74.8 47.4 %copy-start.6 = (f32[512,2,2,128]{0,3,2,1:T(8,128)S(1)}, f32[512,2,2,128]{0,3,2,1:T(8,128)}, u32[]{:S(2)}) copy-start(f32[512,2,2,128]{0,3,2,1:T(8,128)} %get-tuple-element.35) | copy-start | bytes 3145732
  74.8 9.0 %collective-permute-start.6 = (f32[2,128]{1,0:T(2,128)S(1)}, f32[2,128]{1,0:T(2,128)S(1)}, u32[]{:S(2)}, u32[]{:S(2)}) collective-permute-start(f32[2,128]{1,0:T(2,128)S(1)} %add.213), channel_id=1, source_target_pairs={{0,8},{4,12},{8,0},{12,4},{16,24},{20,28},{24,16},{28,20},{32,40},... | collective-permute-start | bytes 3080 | tf_op jit(solution)/shard_map/ppermute | solution.py:24
  83.9 7.1 %collective-permute-start.7 = (f32[2,128]{1,0:T(2,128)S(1)}, f32[2,128]{1,0:T(2,128)S(1)}, u32[]{:S(2)}, u32[]{:S(2)}) collective-permute-start(f32[2,128]{1,0:T(2,128)S(1)} %add.214), channel_id=1, source_target_pairs={{0,16},{4,20},{8,24},{12,28},{16,0},{20,4},{24,8},{28,12},{32,48},... | collective-permute-start | bytes 3080 | tf_op jit(solution)/shard_map/ppermute | solution.py:24
  89.7 40.0 %collective-permute-start.13 = (bf16[512,2,256]{0,2,1:T(8,128)(2,1)}, bf16[512,2,256]{0,2,1:T(8,128)(2,1)}, u32[]{:S(2)}, u32[]{:S(2)}) collective-permute-start(bf16[512,2,256]{0,2,1:T(8,128)(2,1)} %pad_maximum_fusion.2), channel_id=1, source_target_pairs={{8,0},{12,4},{16,8},{20,12},{24,16},{28,20},{32,24},{36,28},{40,32... | collective-permute-start | bytes 1572872 | tf_op jit(solution)/shard_map/ppermute | solution.py:19
  91.0 10.8 %collective-permute-start.8 = (f32[2,128]{1,0:T(2,128)S(1)}, f32[2,128]{1,0:T(2,128)S(1)}, u32[]{:S(2)}, u32[]{:S(2)}) collective-permute-start(f32[2,128]{1,0:T(2,128)S(1)} %add.215), channel_id=1, source_target_pairs={{0,32},{4,36},{8,40},{12,44},{16,48},{20,52},{24,56},{28,60},{32,0... | collective-permute-start | bytes 3080 | tf_op jit(solution)/shard_map/ppermute | solution.py:24
  100.4 30.4 %collective-permute-start.12 = (bf16[512,2,256]{0,2,1:T(8,128)(2,1)}, bf16[512,2,256]{0,2,1:T(8,128)(2,1)}, u32[]{:S(2)}, u32[]{:S(2)}) collective-permute-start(bf16[512,2,256]{0,2,1:T(8,128)(2,1)} %pad_maximum_fusion.1), channel_id=1, source_target_pairs={{4,0},{8,4},{12,8},{16,12},{20,16},{24,20},{28,24},{32,28},{36,32}... | collective-permute-start | bytes 1572872 | tf_op jit(solution)/shard_map/ppermute | solution.py:19
  101.8 11.8 %collective-permute-start.9 = (f32[2,128]{1,0:T(2,128)S(1)}, f32[2,128]{1,0:T(2,128)S(1)}, u32[]{:S(2)}, u32[]{:S(2)}) collective-permute-start(f32[2,128]{1,0:T(2,128)S(1)} %add.216), channel_id=1, source_target_pairs={{0,64},{4,68},{8,72},{12,76},{16,80},{20,84},{24,88},{28,92},{32,9... | collective-permute-start | bytes 3080 | tf_op jit(solution)/shard_map/ppermute | solution.py:24
  113.6 12.0 %collective-permute-start.10 = (f32[2,128]{1,0:T(2,128)S(1)}, f32[2,128]{1,0:T(2,128)S(1)}, u32[]{:S(2)}, u32[]{:S(2)}) collective-permute-start(f32[2,128]{1,0:T(2,128)S(1)} %add.217), channel_id=1, source_target_pairs={{0,256},{4,260},{8,264},{12,268},{16,272},{20,276},{24,280},{28,28... | collective-permute-start | bytes 3080 | tf_op jit(solution)/shard_map/ppermute | solution.py:36
  120.3 9.4 %collective-permute-start.11 = (f32[2,128]{1,0:T(2,128)S(1)}, f32[2,128]{1,0:T(2,128)S(1)}, u32[]{:S(2)}, u32[]{:S(2)}) collective-permute-start(f32[2,128]{1,0:T(2,128)S(1)} %add.217), channel_id=1, source_target_pairs={{0,128},{4,132},{8,136},{12,140},{16,144},{20,148},{24,152},{28,15... | collective-permute-start | bytes 3080 | tf_op jit(solution)/shard_map/ppermute | solution.py:36
  123.4 8.7 %copy-start.1 = (bf16[2,2,512,512]{2,3,1,0:T(8,128)(2,1)S(1)}, bf16[2,2,512,512]{2,3,1,0:T(8,128)(2,1)}, u32[]{:S(2)}) copy-start(bf16[2,2,512,512]{2,3,1,0:T(8,128)(2,1)} %copy-done) | copy-start | bytes 6291460
  123.4 8.7 %copy-start.14 = (f32[512,2,128]{0,2,1:T(8,128)S(1)}, f32[512,2,128]{0,2,1:T(8,128)}, u32[]{:S(2)}) copy-start(f32[512,2,128]{0,2,1:T(8,128)} %get-tuple-element.37) | copy-start | bytes 1572868
  133.6 2.8 %copy-start.25 = (f32[2]{0:T(128)S(1)}, f32[2]{0:T(128)}, u32[]{:S(2)}) copy-start(f32[2]{0:T(128)} %constant.83) | copy-start | bytes 28
  (8 other events, 12.3 us)

commit v5 on v4

--- a/solution.py
+++ b/solution.py
@@ -109,7 +109,14 @@
     denominator = jnp.sum(cached[0], axis=-1, keepdims=True)
     for weight in cached[1:]:
         denominator = denominator + jnp.sum(weight, axis=-1, keepdims=True)
-    weights_bf = [(weight / denominator).astype(jnp.bfloat16) for weight in cached]
+    again_query_n = lax.optimization_barrier(query_n)
+    weights_bf = []
+    for index in range(reach + 1):
+        scores = jnp.einsum(
+            "tkgd,ukd->kgtu", again_query_n, blocks[index][0], preferred_element_type=jnp.float32
+        )
+        weight = jnp.where(allowed_sets[index][None, None], jnp.exp(scores), 0.0)
+        weights_bf.append((weight / denominator).astype(jnp.bfloat16))
     attend_zero = jnp.zeros((tokens, kv_heads, group_size, HD), jnp.float32)
     attended = attend_zero
     for index in range(reach + 1):

time: 138 us -> 139 us (level)
  the two profiles are of different devices: /device:TPU:2 before, /device:TPU:4 now
where the time goes in v5:
time: 139 us; the launch traced here: 138 us
  starting transfers between devices  67.2 us (48%)
  matrix products  29.6 us (21%)
  waiting for transfers between devices  21.7 us (16%)
  other arithmetic  9.94 us (7%)
  local copies, waits for them, and re-layouts  8.72 us (6%)
    ppermute x8, starting transfers between devices, exchanged_sum(): lax.ppermute(value, axis, [(source, source ^ stride) for source in range(...  49.8 us
    ppermute x8, waiting for transfers between devices, exchanged_sum(): lax.ppermute(value, axis, [(source, source ^ stride) for source in range(...  11.7 us
    ppermute x4, starting transfers between devices, passed_along(): lax.ppermute(value, axis, [(source, source + steps) for source in range(i...  8.77 us
    ppermute x2, starting transfers between devices, three_way_sum(): received.append(lax.ppermute(value, axis, pairs))  8.64 us
    unnamed x38, local copies, waits for them, and re-layouts  8.51 us
    ppermute x4, waiting for transfers between devices, passed_along(): lax.ppermute(value, axis, [(source, source + steps) for source in range(i...  5.84 us
    dot_general x3, matrix products, shards(): jnp.einsum('kgtu,tkgd->ukd', dscore, query_n, preferred_element_type=jnp....  5.58 us
    dot_general x3, matrix products, forward_block(): jnp.einsum('tkgd,ukd->kgtu', query_n, key_block, preferred_element_type=j...  5.33 us
  transfers between devices with their start and end apart: 14, of which 7 were waited for; matrix products, arithmetic and copies ran while one was open for 11% of the time, Pallas kernels for 0%

profile of v5, /device:TPU:4, one launch (start us, length us, event | category | flops | bytes accessed | tf_op | source)
XLA Modules:
  0.0 138.5 jit_solution(15270170202261174131)
XLA Ops:
  3.7 1.8 %collective-permute-start = (bf16[512,2,256]{0,2,1:T(8,128)(2,1)}, bf16[512,2,256]{0,2,1:T(8,128)(2,1)S(1)}, u32[]{:S(2)}, u32[]{:S(2)}) collective-permute-start(bf16[512,2,256]{0,2,1:T(8,128)(2,1)} %pad_maximum_fusion), channel_id=1, source_target_pairs={{0,4},{4,8},{8,12},{12,16},{16,20},{20,24},{24,28},{28,32},{32,36}... | collective-permute-start | bytes 1572872 | tf_op jit(solution)/shard_map/ppermute | solution.py:19
  5.5 4.5 %collective-permute-start.1 = (bf16[512,2,256]{0,2,1:T(8,128)(2,1)}, bf16[512,2,256]{0,2,1:T(8,128)(2,1)}, u32[]{:S(2)}, u32[]{:S(2)}) collective-permute-start(bf16[512,2,256]{0,2,1:T(8,128)(2,1)} %pad_maximum_fusion), channel_id=1, source_target_pairs={{0,8},{4,12},{8,16},{12,20},{16,24},{20,28},{24,32},{28,36},{32,40... | collective-permute-start | bytes 1572872 | tf_op jit(solution)/shard_map/ppermute | solution.py:19
  10.6 1.7 %fusion.25 = (pred[512,512]{0,1:T(8,128)(4,1)}, pred[512,512]{0,1:T(8,128)(4,1)S(1)}, pred[512,512]{0,1:T(8,128)(4,1)}) fusion(s32[512]{0:T(512)S(1)} %iota_add_fusion.2, s32[512]{0:T(512)S(1)} %bitcast.232, s32[512]{0:T(512)S(1)} %get-tuple-element.30, s32[512]{0:T(512)S(1)} %get-tuple-element.29), kind=kLoop, calls=%fused_computation.54 | loop fusion | flops 4718592 | bytes 794624 | tf_op jit(solution)/shard_map/and | solution.py:96
  13.7 2.1 %fusion.12 = f32[2,2,512]{2,1,0:T(2,128)S(1)} fusion(bf16[512,2,2,128]{0,3,2,1:T(8,128)(2,1)S(1)} %multiply_convert_fusion.1, pred[512,512]{0,1:T(8,128)(4,1)} %get-tuple-element.25, bf16[512,2,128]{0,2,1:T(8,128)(2,1)S(1)} %bitcast.217, f32[128]{0:T(128)S(1)} %copy-done.12, f32[512,2]{0,1:T(2,128)S(1)} %add_rsqrt_fusion.3), kind=kOutput, calls=%fused_computation.20 | convolution fusion | flops 271054848 | bytes 1061376 | tf_op jit(solution)/shard_map/tkgd,ukd->kgtu/dot_general | solution.py:103
  15.9 5.8 %collective-permute-done.1 = bf16[512,2,256]{0,2,1:T(8,128)(2,1)} collective-permute-done((bf16[512,2,256]{0,2,1:T(8,128)(2,1)}, bf16[512,2,256]{0,2,1:T(8,128)(2,1)}, u32[]{:S(2)}, u32[]{:S(2)}) %collective-permute-start.1) | collective-permute-done | bytes 524320 | tf_op jit(solution)/shard_map/ppermute | solution.py:19
  23.9 2.1 %fusion.10 = f32[2,2,512]{2,1,0:T(2,128)S(1)} fusion(bf16[512,2,2,128]{0,3,2,1:T(8,128)(2,1)S(1)} %multiply_convert_fusion.1, pred[512,512]{0,1:T(8,128)(4,1)S(1)} %get-tuple-element.24, f32[512,2]{0,1:T(2,128)S(1)} %add_rsqrt_fusion.1, f32[128]{0:T(128)S(1)} %copy-done.12, bf16[512,2,256]{0,2,1:T(8,128)(2,1)} %collective-permute-done.1), kind=kOutput, calls=%fused_computation.16 | convolution fusion | flops 271054848 | bytes 1061376 | tf_op jit(solution)/shard_map/tkgd,ukd->kgtu/dot_general | solution.py:103
  28.9 2.3 %fusion.5 = bf16[2,2,512,512]{2,3,1,0:T(8,128)(2,1)S(1)} fusion(bf16[512,2,2,128]{0,3,2,1:T(8,128)(2,1)S(1)} %multiply_convert_fusion.1, f32[2,2,512]{2,1,0:T(2,128)S(1)} %add_add_fusion, pred[512,512]{0,1:T(8,128)(4,1)S(1)} %get-tuple-element.24, f32[512,2]{0,1:T(2,128)S(1)} %add_rsqrt_fusion.1, f32[128]{0:T(128)S(1)} %copy-done.12, ...), kind=kOutput, calls=%fused_computation.8 | convolution fusion | flops 272105472 | bytes 3158528 | tf_op jit(solution)/shard_map/tkgd,ukd->kgtu/dot_general | solution.py:115
  31.2 1.6 %convolution_bitcast_fusion.1 = f32[512,2,2,128]{0,3,2,1:T(8,128)S(1)} fusion(bf16[2,2,512,512]{2,3,1,0:T(8,128)(2,1)S(1)} %fusion.5, bf16[512,2,256]{0,2,1:T(8,128)(2,1)} %collective-permute-done.1), kind=kOutput, calls=%fused_computation.25 | convolution fusion | flops 268435456 | bytes 3407872 | tf_op jit(solution)/shard_map/kgtu,ukd->tkgd/dot_general | solution.py:125
  34.1 1.6 %fusion.40 = (f32[128]{0:T(128)S(1)}, f32[512,2,128]{0,2,1:T(8,128)}) fusion(bf16[512,2,128]{0,2,1:T(8,128)(2,1)S(1)} %bitcast.219, f32[512,2]{0,1:T(2,128)S(1)} %add_rsqrt_fusion.3, bf16[512,2,2,128]{0,3,2,1:T(8,128)(2,1)S(1)} %multiply_convert_fusion.1, bf16[2,2,512,512]{2,3,1,0:T(8,128)(2,1)S(1)} %fusion.9), kind=kOutput, calls=%fused_computation.75 | convolution fusion | flops 268959616 | bytes 3412480 | tf_op jit(solution)/shard_map/kgtu,tkgd->ukd/dot_general | solution.py:144
  36.2 1.7 %fusion.1 = bf16[2,2,512,512]{2,3,1,0:T(8,128)(2,1)S(1)} fusion(bf16[2,2,512,512]{2,3,1,0:T(8,128)(2,1)S(1)} %fusion.5, bf16[512,2,2,128]{0,3,2,1:T(8,128)(2,1)S(1)} %bitcast.206, f32[2,2,512]{2,1,0:T(2,128)S(1)} %bitcast.230, bf16[512,2,256]{0,2,1:T(8,128)(2,1)} %collective-permute-done.1), kind=kOutput, calls=%fused_computation.2 | convolution fusion | flops 272629760 | bytes 4988928 | tf_op jit(solution)/shard_map/tkgd,ukd->kgtu/dot_general | solution.py:137
  39.2 2.6 %multiply_reduce_fusion = (f32[128]{0:T(128)S(1)}, f32[512,2,2]{0,2,1:T(2,128)S(1)}, f32[512,2,2,128]{0,3,2,1:T(8,128)}) fusion(f32[512,2,2,128]{0,3,2,1:T(8,128)S(1)} %bitcast.213, f32[512,2,2]{0,2,1:T(2,128)S(1)} %add_rsqrt_fusion, f32[128]{0:T(128)S(1)} %copy-done.13, f32[2,128,2,512]{3,1,2,0:T(8,128)S(1)} %convolution_add_fusion.1, ...), kind=kOutput, calls=%fused_computation.44 | convolution fusion | flops 271054720 | bytes 5527040 | tf_op jit(solution)/shard_map/kgtu,ukd->tkgd/dot_general | solution.py:141
  41.8 2.5 %fusion.62 = (bf16[512,2,128]{0,2,1:T(8,128)(2,1)}, f32[128]{0:T(128)S(1)}) fusion(f32[512,2]{0,1:T(2,128)S(1)} %add_rsqrt_fusion.1, bf16[512,2,256]{0,2,1:T(8,128)(2,1)} %collective-permute-done.1, bf16[512,2,2,128]{0,3,2,1:T(8,128)(2,1)S(1)} %multiply_convert_fusion.1, bf16[2,2,512,512]{2,3,1,0:T(8,128)(2,1)S(1)} %fusion.1), kind=kOutput, calls=%fused_computation.110 | convolution fusion | flops 269090688 | bytes 3150336 | tf_op jit(solution)/shard_map/kgtu,tkgd->ukd/dot_general | solution.py:144
  44.2 1.5 %fusion.63 = (bf16[512,2,128]{0,2,1:T(8,128)(2,1)}, f32[128]{0:T(128)S(1)}) fusion(f32[512,2]{0,1:T(2,128)S(1)} %add_rsqrt_fusion.2, bf16[512,2,256]{0,2,1:T(8,128)(2,1)S(1)} %collective-permute-done, bf16[512,2,2,128]{0,3,2,1:T(8,128)(2,1)S(1)} %multiply_convert_fusion.1, bf16[2,2,512,512]{2,3,1,0:T(8,128)(2,1)S(1)} %fusion.3), kind=kOutput, calls=%fused_computation.111 | convolution fusion | flops 269090688 | bytes 3150336 | tf_op jit(solution)/shard_map/kgtu,tkgd->ukd/dot_general | solution.py:144
  45.8 3.1 %collective-permute-start.2 = (f32[2,128]{1,0:T(2,128)S(1)}, f32[2,128]{1,0:T(2,128)S(1)}, u32[]{:S(2)}, u32[]{:S(2)}) collective-permute-start(f32[2,128]{1,0:T(2,128)S(1)} %pad_maximum_fusion.3), channel_id=1, source_target_pairs={{0,1},{1,0},{2,3},{3,2},{4,5},{5,4},{6,7},{7,6},{8,9},{9,8},{10,11... | collective-permute-start | bytes 3080 | tf_op jit(solution)/shard_map/ppermute | solution.py:24
  48.9 2.3 %collective-permute-done.2 = f32[2,128]{1,0:T(2,128)S(1)} collective-permute-done((f32[2,128]{1,0:T(2,128)S(1)}, f32[2,128]{1,0:T(2,128)S(1)}, u32[]{:S(2)}, u32[]{:S(2)}) %collective-permute-start.2) | collective-permute-done | bytes 1056 | tf_op jit(solution)/shard_map/ppermute | solution.py:24
  51.2 5.5 %collective-permute-start.3 = (f32[2,128]{1,0:T(2,128)S(1)}, f32[2,128]{1,0:T(2,128)S(1)}, u32[]{:S(2)}, u32[]{:S(2)}) collective-permute-start(f32[2,128]{1,0:T(2,128)S(1)} %fusion.61), channel_id=1, source_target_pairs={{0,2},{1,3},{2,0},{3,1},{4,6},{5,7},{6,4},{7,5},{8,10},{9,11},{10,... | collective-permute-start | bytes 3080 | tf_op jit(solution)/shard_map/ppermute | solution.py:24
  56.8 1.5 %collective-permute-done.3 = f32[2,128]{1,0:T(2,128)S(1)} collective-permute-done((f32[2,128]{1,0:T(2,128)S(1)}, f32[2,128]{1,0:T(2,128)S(1)}, u32[]{:S(2)}, u32[]{:S(2)}) %collective-permute-start.3) | collective-permute-done | bytes 1056 | tf_op jit(solution)/shard_map/ppermute | solution.py:24
  58.3 15.0 %collective-permute-start.4 = (f32[2,128]{1,0:T(2,128)S(1)}, f32[2,128]{1,0:T(2,128)S(1)}, u32[]{:S(2)}, u32[]{:S(2)}) collective-permute-start(f32[2,128]{1,0:T(2,128)S(1)} %fusion.93), channel_id=1, source_target_pairs={{0,384},{384,0},{1,385},{385,1},{2,386},{386,2},{3,387},{387,3},{4... | collective-permute-start | bytes 3080 | tf_op jit(solution)/shard_map/ppermute | solution.py:24
  73.4 1.5 %collective-permute-done.4 = f32[2,128]{1,0:T(2,128)S(1)} collective-permute-done((f32[2,128]{1,0:T(2,128)S(1)}, f32[2,128]{1,0:T(2,128)S(1)}, u32[]{:S(2)}, u32[]{:S(2)}) %collective-permute-start.4) | collective-permute-done | bytes 1056 | tf_op jit(solution)/shard_map/ppermute | solution.py:24
  74.9 2.0 %collective-permute-start.5 = (f32[2,128]{1,0:T(2,128)S(1)}, f32[2,128]{1,0:T(2,128)S(1)}, u32[]{:S(2)}, u32[]{:S(2)}) collective-permute-start(f32[2,128]{1,0:T(2,128)S(1)} %add.212), channel_id=1, source_target_pairs={{0,4},{4,0},{8,12},{12,8},{16,20},{20,16},{24,28},{28,24},{32,36},... | collective-permute-start | bytes 3080 | tf_op jit(solution)/shard_map/ppermute | solution.py:24
  76.9 2.4 %fusion.22 = bf16[512,2,128]{0,2,1:T(8,128)(2,1)S(1)} fusion(bf16[2,2,512,512]{2,3,1,0:T(8,128)(2,1)} %copy-done.4, bf16[512,2,2,128]{0,3,2,1:T(8,128)(2,1)S(1)} %bitcast.208), kind=kOutput, calls=%fused_computation.42 | convolution fusion | flops 268566528 | bytes 2883584 | tf_op jit(solution)/shard_map/kgtu,tkgd->ukd/dot_general | solution.py:147
  79.4 4.4 %collective-permute-start.6 = (f32[2,128]{1,0:T(2,128)S(1)}, f32[2,128]{1,0:T(2,128)S(1)}, u32[]{:S(2)}, u32[]{:S(2)}) collective-permute-start(f32[2,128]{1,0:T(2,128)S(1)} %add.213), channel_id=1, source_target_pairs={{0,8},{4,12},{8,0},{12,4},{16,24},{20,28},{24,16},{28,20},{32,40},... | collective-permute-start | bytes 3080 | tf_op jit(solution)/shard_map/ppermute | solution.py:24
  85.4 4.9 %collective-permute-start.7 = (f32[2,128]{1,0:T(2,128)S(1)}, f32[2,128]{1,0:T(2,128)S(1)}, u32[]{:S(2)}, u32[]{:S(2)}) collective-permute-start(f32[2,128]{1,0:T(2,128)S(1)} %add.214), channel_id=1, source_target_pairs={{0,16},{4,20},{8,24},{12,28},{16,0},{20,4},{24,8},{28,12},{32,48},... | collective-permute-start | bytes 3080 | tf_op jit(solution)/shard_map/ppermute | solution.py:24
  92.4 8.6 %collective-permute-start.8 = (f32[2,128]{1,0:T(2,128)S(1)}, f32[2,128]{1,0:T(2,128)S(1)}, u32[]{:S(2)}, u32[]{:S(2)}) collective-permute-start(f32[2,128]{1,0:T(2,128)S(1)} %add.215), channel_id=1, source_target_pairs={{0,32},{4,36},{8,40},{12,44},{16,48},{20,52},{24,56},{28,60},{32,0... | collective-permute-start | bytes 3080 | tf_op jit(solution)/shard_map/ppermute | solution.py:24
  103.2 6.1 %collective-permute-start.9 = (f32[2,128]{1,0:T(2,128)S(1)}, f32[2,128]{1,0:T(2,128)S(1)}, u32[]{:S(2)}, u32[]{:S(2)}) collective-permute-start(f32[2,128]{1,0:T(2,128)S(1)} %add.216), channel_id=1, source_target_pairs={{0,64},{4,68},{8,72},{12,76},{16,80},{20,84},{24,88},{28,92},{32,9... | collective-permute-start | bytes 3080 | tf_op jit(solution)/shard_map/ppermute | solution.py:24
  109.4 5.7 %collective-permute-done.9 = f32[2,128]{1,0:T(2,128)S(1)} collective-permute-done((f32[2,128]{1,0:T(2,128)S(1)}, f32[2,128]{1,0:T(2,128)S(1)}, u32[]{:S(2)}, u32[]{:S(2)}) %collective-permute-start.9) | collective-permute-done | bytes 1056 | tf_op jit(solution)/shard_map/ppermute | solution.py:24
  115.0 6.7 %collective-permute-start.10 = (f32[2,128]{1,0:T(2,128)S(1)}, f32[2,128]{1,0:T(2,128)S(1)}, u32[]{:S(2)}, u32[]{:S(2)}) collective-permute-start(f32[2,128]{1,0:T(2,128)S(1)} %add.217), channel_id=1, source_target_pairs={{0,256},{4,260},{8,264},{12,268},{16,272},{20,276},{24,280},{28,28... | collective-permute-start | bytes 3080 | tf_op jit(solution)/shard_map/ppermute | solution.py:36
  121.8 1.9 %collective-permute-start.11 = (f32[2,128]{1,0:T(2,128)S(1)}, f32[2,128]{1,0:T(2,128)S(1)}, u32[]{:S(2)}, u32[]{:S(2)}) collective-permute-start(f32[2,128]{1,0:T(2,128)S(1)} %add.217), channel_id=1, source_target_pairs={{0,128},{4,132},{8,136},{12,140},{16,144},{20,148},{24,152},{28,15... | collective-permute-start | bytes 3080 | tf_op jit(solution)/shard_map/ppermute | solution.py:36
  124.8 2.2 %copy.46 = bf16[1,512,512]{2,1,0:T(8,128)(2,1)} copy(bf16[1,512,512]{1,2,0:T(8,128)(2,1)} %bitcast.226) | data formatting | bytes 1048576
  127.0 4.1 %collective-permute-done.11 = f32[2,128]{1,0:T(2,128)S(1)} collective-permute-done((f32[2,128]{1,0:T(2,128)S(1)}, f32[2,128]{1,0:T(2,128)S(1)}, u32[]{:S(2)}, u32[]{:S(2)}) %collective-permute-start.11) | collective-permute-done | bytes 1056 | tf_op jit(solution)/shard_map/ppermute | solution.py:36
  133.5 1.6 %fusion.41 = (f32[512,2]{0,1:T(2,128)S(1)}, f32[512,2,128]{0,2,1:T(8,128)S(1)}, bf16[512,2,128]{0,2,1:T(8,128)(2,1)}) fusion(bf16[512,2,128]{0,2,1:T(8,128)(2,1)S(1)} %bitcast.221, f32[512,2]{0,1:T(2,128)S(1)} %add_rsqrt_fusion.3, f32[128]{0:T(128)S(1)} %copy-done.12, f32[512,2,256]{0,2,1:T(8,128)S(1)} %convert_element_type.103, ...), kind=kOutput, calls=%fused_computation.76 | convolution fusion | flops 269745152 | bytes 6300160 | tf_op jit(solution)/shard_map/kgtu,tkgd->ukd/dot_general | solution.py:147
  136.1 1.8 %copy.48 = bf16[1,512,256]{2,1,0:T(8,128)(2,1)} copy(bf16[1,512,256]{1,2,0:T(8,128)(2,1)} %bitcast.227) | data formatting | bytes 524288
  (91 shorter events, 24.0 us)
Async XLA Ops:
  0.6 9.3 %copy-start.9 = (bf16[1,512,512]{2,1,0:T(8,128)(2,1)S(1)}, bf16[1,512,512]{2,1,0:T(8,128)(2,1)}, u32[]{:S(2)}) copy-start(bf16[1,512,512]{2,1,0:T(8,128)(2,1)} %param.8) | copy-start | bytes 1572868
  1.8 8.6 %copy-start.13 = (f32[128]{0:T(128)S(1)}, f32[128]{0:T(128)}, u32[]{:S(2)}) copy-start(f32[128]{0:T(128)} %param.12) | copy-start | bytes 1540
  3.7 12.1 %collective-permute-start = (bf16[512,2,256]{0,2,1:T(8,128)(2,1)}, bf16[512,2,256]{0,2,1:T(8,128)(2,1)S(1)}, u32[]{:S(2)}, u32[]{:S(2)}) collective-permute-start(bf16[512,2,256]{0,2,1:T(8,128)(2,1)} %pad_maximum_fusion), channel_id=1, source_target_pairs={{0,4},{4,8},{8,12},{12,16},{16,20},{20,24},{24,28},{28,32},{32,36}... | collective-permute-start | bytes 1572872 | tf_op jit(solution)/shard_map/ppermute | solution.py:19
  5.5 16.3 %collective-permute-start.1 = (bf16[512,2,256]{0,2,1:T(8,128)(2,1)}, bf16[512,2,256]{0,2,1:T(8,128)(2,1)}, u32[]{:S(2)}, u32[]{:S(2)}) collective-permute-start(bf16[512,2,256]{0,2,1:T(8,128)(2,1)} %pad_maximum_fusion), channel_id=1, source_target_pairs={{0,8},{4,12},{8,16},{12,20},{16,24},{20,28},{24,32},{28,36},{32,40... | collective-permute-start | bytes 1572872 | tf_op jit(solution)/shard_map/ppermute | solution.py:19
  10.0 0.7 copy-start.14
  10.3 3.4 %copy-start.12 = (f32[128]{0:T(128)S(1)}, f32[128]{0:T(128)}, u32[]{:S(2)}) copy-start(f32[128]{0:T(128)} %param.13) | copy-start | bytes 1540
  13.7 9.1 %copy-start.10 = (pred[512,512]{0,1:T(8,128)(4,1)S(1)}, pred[512,512]{0,1:T(8,128)(4,1)}, u32[]{:S(2)}) copy-start(pred[512,512]{0,1:T(8,128)(4,1)} %get-tuple-element.23) | copy-start | bytes 786436
  23.9 2.2 %copy-start.11 = (pred[512,512]{0,1:T(8,128)(4,1)S(1)}, pred[512,512]{0,1:T(8,128)(4,1)}, u32[]{:S(2)}) copy-start(pred[512,512]{0,1:T(8,128)(4,1)} %get-tuple-element.25) | copy-start | bytes 786436
  27.2 6.1 %copy-start.2 = (bf16[2,2,512,512]{2,3,1,0:T(8,128)(2,1)}, bf16[2,2,512,512]{2,3,1,0:T(8,128)(2,1)S(1)}, u32[]{:S(2)}) copy-start(bf16[2,2,512,512]{2,3,1,0:T(8,128)(2,1)S(1)} %fusion.14) | copy-start | bytes 6291460
  28.9 9.1 %copy-start = (bf16[2,2,512,512]{2,3,1,0:T(8,128)(2,1)}, bf16[2,2,512,512]{2,3,1,0:T(8,128)(2,1)S(1)}, u32[]{:S(2)}) copy-start(bf16[2,2,512,512]{2,3,1,0:T(8,128)(2,1)S(1)} %fusion.7) | copy-start | bytes 6291460
  31.2 5.0 %copy-start.4 = (bf16[2,2,512,512]{2,3,1,0:T(8,128)(2,1)}, bf16[2,2,512,512]{2,3,1,0:T(8,128)(2,1)S(1)}, u32[]{:S(2)}) copy-start(bf16[2,2,512,512]{2,3,1,0:T(8,128)(2,1)S(1)} %fusion.5) | copy-start | bytes 6291460
  45.8 5.5 %collective-permute-start.2 = (f32[2,128]{1,0:T(2,128)S(1)}, f32[2,128]{1,0:T(2,128)S(1)}, u32[]{:S(2)}, u32[]{:S(2)}) collective-permute-start(f32[2,128]{1,0:T(2,128)S(1)} %pad_maximum_fusion.3), channel_id=1, source_target_pairs={{0,1},{1,0},{2,3},{3,2},{4,5},{5,4},{6,7},{7,6},{8,9},{9,8},{10,11... | collective-permute-start | bytes 3080 | tf_op jit(solution)/shard_map/ppermute | solution.py:24
  51.2 7.1 %collective-permute-start.3 = (f32[2,128]{1,0:T(2,128)S(1)}, f32[2,128]{1,0:T(2,128)S(1)}, u32[]{:S(2)}, u32[]{:S(2)}) collective-permute-start(f32[2,128]{1,0:T(2,128)S(1)} %fusion.61), channel_id=1, source_target_pairs={{0,2},{1,3},{2,0},{3,1},{4,6},{5,7},{6,4},{7,5},{8,10},{9,11},{10,... | collective-permute-start | bytes 3080 | tf_op jit(solution)/shard_map/ppermute | solution.py:24
  58.3 16.6 %collective-permute-start.4 = (f32[2,128]{1,0:T(2,128)S(1)}, f32[2,128]{1,0:T(2,128)S(1)}, u32[]{:S(2)}, u32[]{:S(2)}) collective-permute-start(f32[2,128]{1,0:T(2,128)S(1)} %fusion.93), channel_id=1, source_target_pairs={{0,384},{384,0},{1,385},{385,1},{2,386},{386,2},{3,387},{387,3},{4... | collective-permute-start | bytes 3080 | tf_op jit(solution)/shard_map/ppermute | solution.py:24
  73.4 10.4 %copy-start.1 = (bf16[2,2,512,512]{2,3,1,0:T(8,128)(2,1)S(1)}, bf16[2,2,512,512]{2,3,1,0:T(8,128)(2,1)}, u32[]{:S(2)}) copy-start(bf16[2,2,512,512]{2,3,1,0:T(8,128)(2,1)} %copy-done) | copy-start | bytes 6291460
  74.9 4.4 %collective-permute-start.5 = (f32[2,128]{1,0:T(2,128)S(1)}, f32[2,128]{1,0:T(2,128)S(1)}, u32[]{:S(2)}, u32[]{:S(2)}) collective-permute-start(f32[2,128]{1,0:T(2,128)S(1)} %add.212), channel_id=1, source_target_pairs={{0,4},{4,0},{8,12},{12,8},{16,20},{20,16},{24,28},{28,24},{32,36},... | collective-permute-start | bytes 3080 | tf_op jit(solution)/shard_map/ppermute | solution.py:24
  79.3 11.0 %copy-start.8 = (bf16[512,2,128]{0,2,1:T(8,128)(2,1)S(1)}, bf16[512,2,128]{0,2,1:T(8,128)(2,1)}, u32[]{:S(2)}) copy-start(bf16[512,2,128]{0,2,1:T(8,128)(2,1)} %get-tuple-element.19) | copy-start | bytes 786436
  79.3 21.7 %copy-start.7 = (bf16[512,2,128]{0,2,1:T(8,128)(2,1)S(1)}, bf16[512,2,128]{0,2,1:T(8,128)(2,1)}, u32[]{:S(2)}) copy-start(bf16[512,2,128]{0,2,1:T(8,128)(2,1)} %get-tuple-element.21) | copy-start | bytes 786436
  79.4 44.3 %copy-start.5 = (f32[512,2,2,128]{0,3,2,1:T(8,128)S(1)}, f32[512,2,2,128]{0,3,2,1:T(8,128)}, u32[]{:S(2)}) copy-start(f32[512,2,2,128]{0,3,2,1:T(8,128)} %get-tuple-element.26) | copy-start | bytes 3145732
  79.4 6.0 %collective-permute-start.6 = (f32[2,128]{1,0:T(2,128)S(1)}, f32[2,128]{1,0:T(2,128)S(1)}, u32[]{:S(2)}, u32[]{:S(2)}) collective-permute-start(f32[2,128]{1,0:T(2,128)S(1)} %add.213), channel_id=1, source_target_pairs={{0,8},{4,12},{8,0},{12,4},{16,24},{20,28},{24,16},{28,20},{32,40},... | collective-permute-start | bytes 3080 | tf_op jit(solution)/shard_map/ppermute | solution.py:24
  85.4 7.1 %collective-permute-start.7 = (f32[2,128]{1,0:T(2,128)S(1)}, f32[2,128]{1,0:T(2,128)S(1)}, u32[]{:S(2)}, u32[]{:S(2)}) collective-permute-start(f32[2,128]{1,0:T(2,128)S(1)} %add.214), channel_id=1, source_target_pairs={{0,16},{4,20},{8,24},{12,28},{16,0},{20,4},{24,8},{28,12},{32,48},... | collective-permute-start | bytes 3080 | tf_op jit(solution)/shard_map/ppermute | solution.py:24
  91.1 40.0 %collective-permute-start.13 = (bf16[512,2,256]{0,2,1:T(8,128)(2,1)}, bf16[512,2,256]{0,2,1:T(8,128)(2,1)}, u32[]{:S(2)}, u32[]{:S(2)}) collective-permute-start(bf16[512,2,256]{0,2,1:T(8,128)(2,1)} %pad_maximum_fusion.2), channel_id=1, source_target_pairs={{8,0},{12,4},{16,8},{20,12},{24,16},{28,20},{32,24},{36,28},{40,32... | collective-permute-start | bytes 1572872 | tf_op jit(solution)/shard_map/ppermute | solution.py:19
  92.4 10.8 %collective-permute-start.8 = (f32[2,128]{1,0:T(2,128)S(1)}, f32[2,128]{1,0:T(2,128)S(1)}, u32[]{:S(2)}, u32[]{:S(2)}) collective-permute-start(f32[2,128]{1,0:T(2,128)S(1)} %add.215), channel_id=1, source_target_pairs={{0,32},{4,36},{8,40},{12,44},{16,48},{20,52},{24,56},{28,60},{32,0... | collective-permute-start | bytes 3080 | tf_op jit(solution)/shard_map/ppermute | solution.py:24
  101.9 30.4 %collective-permute-start.12 = (bf16[512,2,256]{0,2,1:T(8,128)(2,1)}, bf16[512,2,256]{0,2,1:T(8,128)(2,1)}, u32[]{:S(2)}, u32[]{:S(2)}) collective-permute-start(bf16[512,2,256]{0,2,1:T(8,128)(2,1)} %pad_maximum_fusion.1), channel_id=1, source_target_pairs={{4,0},{8,4},{12,8},{16,12},{20,16},{24,20},{28,24},{32,28},{36,32}... | collective-permute-start | bytes 1572872 | tf_op jit(solution)/shard_map/ppermute | solution.py:19
  103.2 11.8 %collective-permute-start.9 = (f32[2,128]{1,0:T(2,128)S(1)}, f32[2,128]{1,0:T(2,128)S(1)}, u32[]{:S(2)}, u32[]{:S(2)}) collective-permute-start(f32[2,128]{1,0:T(2,128)S(1)} %add.216), channel_id=1, source_target_pairs={{0,64},{4,68},{8,72},{12,76},{16,80},{20,84},{24,88},{28,92},{32,9... | collective-permute-start | bytes 3080 | tf_op jit(solution)/shard_map/ppermute | solution.py:24
  115.0 12.0 %collective-permute-start.10 = (f32[2,128]{1,0:T(2,128)S(1)}, f32[2,128]{1,0:T(2,128)S(1)}, u32[]{:S(2)}, u32[]{:S(2)}) collective-permute-start(f32[2,128]{1,0:T(2,128)S(1)} %add.217), channel_id=1, source_target_pairs={{0,256},{4,260},{8,264},{12,268},{16,272},{20,276},{24,280},{28,28... | collective-permute-start | bytes 3080 | tf_op jit(solution)/shard_map/ppermute | solution.py:36
  121.8 9.4 %collective-permute-start.11 = (f32[2,128]{1,0:T(2,128)S(1)}, f32[2,128]{1,0:T(2,128)S(1)}, u32[]{:S(2)}, u32[]{:S(2)}) collective-permute-start(f32[2,128]{1,0:T(2,128)S(1)} %add.217), channel_id=1, source_target_pairs={{0,128},{4,132},{8,136},{12,140},{16,144},{20,148},{24,152},{28,15... | collective-permute-start | bytes 3080 | tf_op jit(solution)/shard_map/ppermute | solution.py:36
  124.8 8.7 %copy-start.3 = (bf16[2,2,512,512]{2,3,1,0:T(8,128)(2,1)S(1)}, bf16[2,2,512,512]{2,3,1,0:T(8,128)(2,1)}, u32[]{:S(2)}) copy-start(bf16[2,2,512,512]{2,3,1,0:T(8,128)(2,1)} %copy-done.2) | copy-start | bytes 6291460
  124.8 8.7 %copy-start.6 = (f32[512,2,128]{0,2,1:T(8,128)S(1)}, f32[512,2,128]{0,2,1:T(8,128)}, u32[]{:S(2)}) copy-start(f32[512,2,128]{0,2,1:T(8,128)} %get-tuple-element.28) | copy-start | bytes 1572868
  135.1 2.8 %copy-start.15 = (f32[2]{0:T(128)S(1)}, f32[2]{0:T(128)}, u32[]{:S(2)}) copy-start(f32[2]{0:T(128)} %constant.83) | copy-start | bytes 28

commit v6 on v4

--- a/solution.py
+++ b/solution.py
@@ -150,15 +150,15 @@
     returns = [
         passed_along(
             jnp.concatenate(pieces[distance], axis=-1).astype(jnp.bfloat16), "ctx", -distance
-        ).astype(jnp.float32)
+        )
         for distance in range(1, reach + 1)
     ]
     summed, *returns = lax.optimization_barrier((summed, *returns))
     dkey_n = pieces[0][0]
     dvalue_sum = pieces[0][1]
     for returned in returns:
-        dkey_n = dkey_n + returned[..., :HD]
-        dvalue_sum = dvalue_sum + returned[..., HD:]
+        dkey_n = dkey_n + returned[..., :HD].astype(jnp.float32)
+        dvalue_sum = dvalue_sum + returned[..., HD:].astype(jnp.float32)
     query_grad = (
         norm_backward(dquery_n, query_hat, query_inv, query_gain, factor)
         .astype(jnp.bfloat16)

time: 138 us -> 139 us (level)
    convert_element_type x3 -> x0, other arithmetic: 2.42 us -> none  [the longest x2 2.31 us: shards(): returns = [passed_along(jnp.concatenate(pieces[distance], axis=-1).astype...]
  transfers between devices with their start and end apart: 14 -> 14, of which waited for: 7 -> 7; matrix products, arithmetic and copies ran while one was open for 12% -> 11% of each run, Pallas kernels for 0% -> 0%
where the time goes in v6:
time: 139 us; the launch traced here: 138 us
  starting transfers between devices  67.7 us (49%)
  matrix products  23.5 us (17%)
  waiting for transfers between devices  22.3 us (16%)
  local copies, waits for them, and re-layouts  13.1 us (9%)
  other arithmetic  10.1 us (7%)
  between operations  1.41 us (1%)
    ppermute x8, starting transfers between devices, exchanged_sum(): lax.ppermute(value, axis, [(source, source ^ stride) for source in range(...  51.3 us
    ppermute x8, waiting for transfers between devices, exchanged_sum(): lax.ppermute(value, axis, [(source, source ^ stride) for source in range(...  14.4 us
    unnamed x58, local copies, waits for them, and re-layouts  12.9 us
    ppermute x2, starting transfers between devices, three_way_sum(): received.append(lax.ppermute(value, axis, pairs))  8.63 us
    ppermute x4, starting transfers between devices, passed_along(): lax.ppermute(value, axis, [(source, source + steps) for source in range(i...  7.68 us
    dot_general x3, matrix products, forward_block(): jnp.einsum('tkgd,ukd->kgtu', query_n, key_block, preferred_element_type=j...  6.43 us
    dot_general x3, matrix products, shards(): jnp.einsum('kgtu,tkgd->ukd', prob, grads_in, preferred_element_type=jnp.f...  6.13 us
    dot_general x3, matrix products, shards(): jnp.einsum('kgtu,tkgd->ukd', dscore, query_n, preferred_element_type=jnp....  4.66 us
  transfers between devices with their start and end apart: 14, of which 7 were waited for; matrix products, arithmetic and copies ran while one was open for 11% of the time, Pallas kernels for 0%

profile of v6, /device:TPU:2, one launch (start us, length us, event | category | flops | bytes accessed | tf_op | source)
XLA Modules:
  0.0 138.1 jit_solution(2581843602677652274)
XLA Ops:
  3.8 3.5 %collective-permute-start.1 = (bf16[512,2,256]{0,2,1:T(8,128)(2,1)}, bf16[512,2,256]{0,2,1:T(8,128)(2,1)S(1)}, u32[]{:S(2)}, u32[]{:S(2)}) collective-permute-start(bf16[512,2,256]{0,2,1:T(8,128)(2,1)} %pad_maximum_fusion), channel_id=1, source_target_pairs={{0,8},{4,12},{8,16},{12,20},{16,24},{20,28},{24,32},{28,36},{32,40... | collective-permute-start | bytes 1572872 | tf_op jit(solution)/shard_map/ppermute | solution.py:19
  7.3 1.5 %collective-permute-start = (bf16[512,2,256]{0,2,1:T(8,128)(2,1)}, bf16[512,2,256]{0,2,1:T(8,128)(2,1)S(1)}, u32[]{:S(2)}, u32[]{:S(2)}) collective-permute-start(bf16[512,2,256]{0,2,1:T(8,128)(2,1)} %pad_maximum_fusion), channel_id=1, source_target_pairs={{0,4},{4,8},{8,12},{12,16},{16,20},{20,24},{24,28},{28,32},{32,36}... | collective-permute-start | bytes 1572872 | tf_op jit(solution)/shard_map/ppermute | solution.py:19
  9.6 1.7 %fusion.19 = (pred[512,512]{0,1:T(8,128)(4,1)}, pred[512,512]{0,1:T(8,128)(4,1)}, pred[512,512]{0,1:T(8,128)(4,1)S(1)}) fusion(s32[512]{0:T(512)S(1)} %iota_add_fusion.2, s32[512]{0:T(512)S(1)} %bitcast.216, s32[512]{0:T(512)S(1)} %get-tuple-element.38, s32[512]{0:T(512)S(1)} %get-tuple-element.37), kind=kLoop, calls=%fused_computation.48 | loop fusion | flops 4718592 | bytes 794624 | tf_op jit(solution)/shard_map/and | solution.py:96
  12.0 3.0 %fusion.6 = (f32[2,2,512]{2,1,0:T(2,128)S(1)}, f32[2,512,512,2]{2,1,3,0:T(8,128)}) fusion(pred[512,512]{0,1:T(8,128)(4,1)S(1)} %get-tuple-element.27, bf16[512,2,2,128]{0,3,2,1:T(8,128)(2,1)S(1)} %multiply_convert_fusion.1, bf16[512,2,128]{0,2,1:T(8,128)(2,1)S(1)} %bitcast.202, f32[128]{0:T(128)S(1)} %copy-done.22, f32[512,2]{0,1:T(2,128)S(1)} %add_rsqrt_fusion.3), kind=kOutput, calls=%fused_computation.15 | convolution fusion | flops 271054848 | bytes 5255680 | tf_op jit(solution)/shard_map/tkgd,ukd->kgtu/dot_general | solution.py:103
  16.2 3.6 %collective-permute-done.1 = bf16[512,2,256]{0,2,1:T(8,128)(2,1)S(1)} collective-permute-done((bf16[512,2,256]{0,2,1:T(8,128)(2,1)}, bf16[512,2,256]{0,2,1:T(8,128)(2,1)S(1)}, u32[]{:S(2)}, u32[]{:S(2)}) %collective-permute-start.1) | collective-permute-done | bytes 524320 | tf_op jit(solution)/shard_map/ppermute | solution.py:19
  20.1 2.3 %fusion.8 = (f32[2,2,512]{2,1,0:T(2,128)S(1)}, f32[2,512,512,2]{2,1,3,0:T(8,128)S(1)}) fusion(pred[512,512]{0,1:T(8,128)(4,1)} %get-tuple-element.26, bf16[512,2,2,128]{0,3,2,1:T(8,128)(2,1)S(1)} %multiply_convert_fusion.1, f32[512,2]{0,1:T(2,128)S(1)} %add_rsqrt_fusion.1, f32[128]{0:T(128)S(1)} %copy-done.22, ...), kind=kOutput, calls=%fused_computation.17 | convolution fusion | flops 271054848 | bytes 5255680 | tf_op jit(solution)/shard_map/tkgd,ukd->kgtu/dot_general | solution.py:103
  24.7 2.2 %divide_convert_fusion.1 = (bf16[2,2,512,512]{2,3,1,0:T(8,128)(2,1)S(1)}, bf16[2,2,512,512]{2,3,1,0:T(8,128)(2,1)S(1)}, bf16[2,2,512,512]{2,3,1,0:T(8,128)(2,1)S(1)}) fusion(f32[2,512,512,2]{2,1,3,0:T(8,128)S(1)} %get-tuple-element.33, f32[2,2,512]{2,1,0:T(2,128)S(1)} %add_add_fusion, pred[512,512]{0,1:T(8,128)(4,1)S(1)} %copy-done.15, ...), kind=kLoop, calls=%fused_computation.13 | loop fusion | flops 9437184 | bytes 19668992 | tf_op jit(solution)/shard_map/convert_element_type | solution.py:112
  30.3 1.6 %fusion.34 = (f32[128]{0:T(128)S(1)}, f32[512,2,128]{0,2,1:T(8,128)}) fusion(bf16[512,2,128]{0,2,1:T(8,128)(2,1)S(1)} %bitcast.203, f32[512,2]{0,1:T(2,128)S(1)} %add_rsqrt_fusion.3, bf16[512,2,2,128]{0,3,2,1:T(8,128)(2,1)S(1)} %multiply_convert_fusion.1, bf16[2,2,512,512]{2,3,1,0:T(8,128)(2,1)S(1)} %fusion.5), kind=kOutput, calls=%fused_computation.69 | convolution fusion | flops 268959616 | bytes 3412480 | tf_op jit(solution)/shard_map/kgtu,tkgd->ukd/dot_general | solution.py:137
  35.2 1.6 %multiply_reduce_fusion = (f32[128]{0:T(128)S(1)}, f32[512,2,2]{0,2,1:T(2,128)S(1)}, f32[512,2,2,128]{0,3,2,1:T(8,128)}) fusion(f32[512,2,2,128]{0,3,2,1:T(8,128)S(1)} %bitcast.198, f32[512,2,2]{0,2,1:T(2,128)S(1)} %add_rsqrt_fusion, f32[128]{0:T(128)S(1)} %copy-done.23, f32[2,128,2,512]{3,1,2,0:T(8,128)S(1)} %convolution_add_fusion.1, ...), kind=kOutput, calls=%fused_computation.38 | convolution fusion | flops 271054720 | bytes 5527040 | tf_op jit(solution)/shard_map/kgtu,ukd->tkgd/dot_general | solution.py:134
  36.8 1.5 %fusion.56 = (bf16[512,2,128]{0,2,1:T(8,128)(2,1)}, f32[128]{0:T(128)S(1)}) fusion(f32[512,2]{0,1:T(2,128)S(1)} %add_rsqrt_fusion.1, bf16[512,2,256]{0,2,1:T(8,128)(2,1)S(1)} %copy-done.14, bf16[512,2,2,128]{0,3,2,1:T(8,128)(2,1)S(1)} %multiply_convert_fusion.1, bf16[2,2,512,512]{2,3,1,0:T(8,128)(2,1)S(1)} %fusion.1), kind=kOutput, calls=%fused_computation.107 | convolution fusion | flops 269090688 | bytes 3150336 | tf_op jit(solution)/shard_map/kgtu,tkgd->ukd/dot_general | solution.py:137
  38.3 1.5 %fusion.57 = (bf16[512,2,128]{0,2,1:T(8,128)(2,1)}, f32[128]{0:T(128)S(1)}) fusion(f32[512,2]{0,1:T(2,128)S(1)} %add_rsqrt_fusion.2, bf16[512,2,256]{0,2,1:T(8,128)(2,1)S(1)} %copy-done.12, bf16[512,2,2,128]{0,3,2,1:T(8,128)(2,1)S(1)} %multiply_convert_fusion.1, bf16[2,2,512,512]{2,3,1,0:T(8,128)(2,1)S(1)} %fusion.3), kind=kOutput, calls=%fused_computation.108 | convolution fusion | flops 269090688 | bytes 3150336 | tf_op jit(solution)/shard_map/kgtu,tkgd->ukd/dot_general | solution.py:137
  39.9 6.9 %collective-permute-start.2 = (f32[2,128]{1,0:T(2,128)S(1)}, f32[2,128]{1,0:T(2,128)S(1)}, u32[]{:S(2)}, u32[]{:S(2)}) collective-permute-start(f32[2,128]{1,0:T(2,128)S(1)} %pad_maximum_fusion.3), channel_id=1, source_target_pairs={{0,1},{1,0},{2,3},{3,2},{4,5},{5,4},{6,7},{7,6},{8,9},{9,8},{10,11... | collective-permute-start | bytes 3080 | tf_op jit(solution)/shard_map/ppermute | solution.py:24
  46.8 1.5 %collective-permute-done.2 = f32[2,128]{1,0:T(2,128)S(1)} collective-permute-done((f32[2,128]{1,0:T(2,128)S(1)}, f32[2,128]{1,0:T(2,128)S(1)}, u32[]{:S(2)}, u32[]{:S(2)}) %collective-permute-start.2) | collective-permute-done | bytes 1056 | tf_op jit(solution)/shard_map/ppermute | solution.py:24
  48.4 1.9 %collective-permute-start.3 = (f32[2,128]{1,0:T(2,128)S(1)}, f32[2,128]{1,0:T(2,128)S(1)}, u32[]{:S(2)}, u32[]{:S(2)}) collective-permute-start(f32[2,128]{1,0:T(2,128)S(1)} %fusion.55), channel_id=1, source_target_pairs={{0,2},{1,3},{2,0},{3,1},{4,6},{5,7},{6,4},{7,5},{8,10},{9,11},{10,... | collective-permute-start | bytes 3080 | tf_op jit(solution)/shard_map/ppermute | solution.py:24
  50.3 5.0 %collective-permute-done.3 = f32[2,128]{1,0:T(2,128)S(1)} collective-permute-done((f32[2,128]{1,0:T(2,128)S(1)}, f32[2,128]{1,0:T(2,128)S(1)}, u32[]{:S(2)}, u32[]{:S(2)}) %collective-permute-start.3) | collective-permute-done | bytes 1056 | tf_op jit(solution)/shard_map/ppermute | solution.py:24
  55.3 12.1 %collective-permute-start.4 = (f32[2,128]{1,0:T(2,128)S(1)}, f32[2,128]{1,0:T(2,128)S(1)}, u32[]{:S(2)}, u32[]{:S(2)}) collective-permute-start(f32[2,128]{1,0:T(2,128)S(1)} %fusion.84), channel_id=1, source_target_pairs={{0,384},{384,0},{1,385},{385,1},{2,386},{386,2},{3,387},{387,3},{4... | collective-permute-start | bytes 3080 | tf_op jit(solution)/shard_map/ppermute | solution.py:24
  67.5 1.5 %collective-permute-done.4 = f32[2,128]{1,0:T(2,128)S(1)} collective-permute-done((f32[2,128]{1,0:T(2,128)S(1)}, f32[2,128]{1,0:T(2,128)S(1)}, u32[]{:S(2)}, u32[]{:S(2)}) %collective-permute-start.4) | collective-permute-done | bytes 1056 | tf_op jit(solution)/shard_map/ppermute | solution.py:24
  69.0 3.3 %collective-permute-start.5 = (f32[2,128]{1,0:T(2,128)S(1)}, f32[2,128]{1,0:T(2,128)S(1)}, u32[]{:S(2)}, u32[]{:S(2)}) collective-permute-start(f32[2,128]{1,0:T(2,128)S(1)} %add.212), channel_id=1, source_target_pairs={{0,4},{4,0},{8,12},{12,8},{16,20},{20,16},{24,28},{28,24},{32,36},... | collective-permute-start | bytes 3080 | tf_op jit(solution)/shard_map/ppermute | solution.py:24
  72.4 2.4 %fusion.16 = bf16[512,2,128]{0,2,1:T(8,128)(2,1)S(1)} fusion(bf16[2,2,512,512]{2,3,1,0:T(8,128)(2,1)} %copy-done.2, bf16[512,2,2,128]{0,3,2,1:T(8,128)(2,1)S(1)} %bitcast.193), kind=kOutput, calls=%fused_computation.36 | convolution fusion | flops 268566528 | bytes 2883584 | tf_op jit(solution)/shard_map/kgtu,tkgd->ukd/dot_general | solution.py:140
  74.8 7.5 %collective-permute-start.6 = (f32[2,128]{1,0:T(2,128)S(1)}, f32[2,128]{1,0:T(2,128)S(1)}, u32[]{:S(2)}, u32[]{:S(2)}) collective-permute-start(f32[2,128]{1,0:T(2,128)S(1)} %add.213), channel_id=1, source_target_pairs={{0,8},{4,12},{8,0},{12,4},{16,24},{20,28},{24,16},{28,20},{32,40},... | collective-permute-start | bytes 3080 | tf_op jit(solution)/shard_map/ppermute | solution.py:24
  83.9 4.9 %collective-permute-start.7 = (f32[2,128]{1,0:T(2,128)S(1)}, f32[2,128]{1,0:T(2,128)S(1)}, u32[]{:S(2)}, u32[]{:S(2)}) collective-permute-start(f32[2,128]{1,0:T(2,128)S(1)} %add.214), channel_id=1, source_target_pairs={{0,16},{4,20},{8,24},{12,28},{16,0},{20,4},{24,8},{28,12},{32,48},... | collective-permute-start | bytes 3080 | tf_op jit(solution)/shard_map/ppermute | solution.py:24
  90.9 8.6 %collective-permute-start.8 = (f32[2,128]{1,0:T(2,128)S(1)}, f32[2,128]{1,0:T(2,128)S(1)}, u32[]{:S(2)}, u32[]{:S(2)}) collective-permute-start(f32[2,128]{1,0:T(2,128)S(1)} %add.215), channel_id=1, source_target_pairs={{0,32},{4,36},{8,40},{12,44},{16,48},{20,52},{24,56},{28,60},{32,0... | collective-permute-start | bytes 3080 | tf_op jit(solution)/shard_map/ppermute | solution.py:24
  100.4 1.4 %collective-permute-start.12 = (bf16[512,2,256]{0,2,1:T(8,128)(2,1)}, bf16[512,2,256]{0,2,1:T(8,128)(2,1)}, u32[]{:S(2)}, u32[]{:S(2)}) collective-permute-start(bf16[512,2,256]{0,2,1:T(8,128)(2,1)} %pad_maximum_fusion.1), channel_id=1, source_target_pairs={{4,0},{8,4},{12,8},{16,12},{20,16},{24,20},{28,24},{32,28},{36,32}... | collective-permute-start | bytes 1572872 | tf_op jit(solution)/shard_map/ppermute | solution.py:19
  101.9 6.0 %collective-permute-start.9 = (f32[2,128]{1,0:T(2,128)S(1)}, f32[2,128]{1,0:T(2,128)S(1)}, u32[]{:S(2)}, u32[]{:S(2)}) collective-permute-start(f32[2,128]{1,0:T(2,128)S(1)} %add.216), channel_id=1, source_target_pairs={{0,64},{4,68},{8,72},{12,76},{16,80},{20,84},{24,88},{28,92},{32,9... | collective-permute-start | bytes 3080 | tf_op jit(solution)/shard_map/ppermute | solution.py:24
  107.9 5.7 %collective-permute-done.9 = f32[2,128]{1,0:T(2,128)S(1)} collective-permute-done((f32[2,128]{1,0:T(2,128)S(1)}, f32[2,128]{1,0:T(2,128)S(1)}, u32[]{:S(2)}, u32[]{:S(2)}) %collective-permute-start.9) | collective-permute-done | bytes 1056 | tf_op jit(solution)/shard_map/ppermute | solution.py:24
  113.6 6.7 %collective-permute-start.10 = (f32[2,128]{1,0:T(2,128)S(1)}, f32[2,128]{1,0:T(2,128)S(1)}, u32[]{:S(2)}, u32[]{:S(2)}) collective-permute-start(f32[2,128]{1,0:T(2,128)S(1)} %add.217), channel_id=1, source_target_pairs={{0,256},{4,260},{8,264},{12,268},{16,272},{20,276},{24,280},{28,28... | collective-permute-start | bytes 3080 | tf_op jit(solution)/shard_map/ppermute | solution.py:36
  120.3 1.9 %collective-permute-start.11 = (f32[2,128]{1,0:T(2,128)S(1)}, f32[2,128]{1,0:T(2,128)S(1)}, u32[]{:S(2)}, u32[]{:S(2)}) collective-permute-start(f32[2,128]{1,0:T(2,128)S(1)} %add.217), channel_id=1, source_target_pairs={{0,128},{4,132},{8,136},{12,140},{16,144},{20,148},{24,152},{28,15... | collective-permute-start | bytes 3080 | tf_op jit(solution)/shard_map/ppermute | solution.py:36
  123.4 2.0 %copy.40 = bf16[1,512,512]{2,1,0:T(8,128)(2,1)} copy(bf16[1,512,512]{1,2,0:T(8,128)(2,1)} %bitcast.210) | data formatting | bytes 1048576
  125.4 4.2 %collective-permute-done.11 = f32[2,128]{1,0:T(2,128)S(1)} collective-permute-done((f32[2,128]{1,0:T(2,128)S(1)}, f32[2,128]{1,0:T(2,128)S(1)}, u32[]{:S(2)}, u32[]{:S(2)}) %collective-permute-start.11) | collective-permute-done | bytes 1056 | tf_op jit(solution)/shard_map/ppermute | solution.py:36
  130.9 2.9 %add_convert_fusion = (bf16[512,2,128]{0,2,1:T(8,128)(2,1)}, bf16[512,2,128]{0,2,1:T(8,128)(2,1)}) fusion(bf16[512,2,256]{0,2,1:T(8,128)(2,1)} %collective-permute-done.13, bf16[512,2,256]{0,2,1:T(8,128)(2,1)} %collective-permute-done.12, f32[512,2]{0,1:T(2,128)S(1)} %broadcast_multiply_fusion.1, f32[512,2]{0,1:T(2,128)S(1)} %add_rsqrt_fusion.3, ...), kind=kOutput, calls=%fused_computation.80 | convolution fusion | flops 270532608 | bytes 4989440 | tf_op jit(solution)/shard_map/kgtu,tkgd->ukd/dot_general | solution.py:140
  133.8 1.8 %copy.41 = bf16[1,512,256]{2,1,0:T(8,128)(2,1)} copy(bf16[1,512,256]{1,2,0:T(8,128)(2,1)} %bitcast.212) | data formatting | bytes 524288
  135.6 1.8 %copy.42 = bf16[1,512,256]{2,1,0:T(8,128)(2,1)} copy(bf16[1,512,256]{1,2,0:T(8,128)(2,1)} %bitcast.211) | data formatting | bytes 524288
  (107 shorter events, 22.3 us)
Async XLA Ops:
  0.6 8.2 %copy-start.21 = (bf16[1,512,512]{2,1,0:T(8,128)(2,1)S(1)}, bf16[1,512,512]{2,1,0:T(8,128)(2,1)}, u32[]{:S(2)}) copy-start(bf16[1,512,512]{2,1,0:T(8,128)(2,1)} %param.8) | copy-start | bytes 1572868
  2.9 6.6 %copy-start.8 = (bf16[1,512,256]{1,2,0:T(8,128)(2,1)}, bf16[1,512,256]{1,2,0:T(8,128)(2,1)S(1)}, u32[]{:S(2)}) copy-start(bf16[1,512,256]{1,2,0:T(8,128)(2,1)S(1)} %copy.16) | copy-start | bytes 786436
  2.9 6.4 %copy-start.23 = (f32[128]{0:T(128)S(1)}, f32[128]{0:T(128)}, u32[]{:S(2)}) copy-start(f32[128]{0:T(128)} %param.12) | copy-start | bytes 1540
  3.8 16.1 %collective-permute-start.1 = (bf16[512,2,256]{0,2,1:T(8,128)(2,1)}, bf16[512,2,256]{0,2,1:T(8,128)(2,1)S(1)}, u32[]{:S(2)}, u32[]{:S(2)}) collective-permute-start(bf16[512,2,256]{0,2,1:T(8,128)(2,1)} %pad_maximum_fusion), channel_id=1, source_target_pairs={{0,8},{4,12},{8,16},{12,20},{16,24},{20,28},{24,32},{28,36},{32,40... | collective-permute-start | bytes 1572872 | tf_op jit(solution)/shard_map/ppermute | solution.py:19
  7.3 12.7 %collective-permute-start = (bf16[512,2,256]{0,2,1:T(8,128)(2,1)}, bf16[512,2,256]{0,2,1:T(8,128)(2,1)S(1)}, u32[]{:S(2)}, u32[]{:S(2)}) collective-permute-start(bf16[512,2,256]{0,2,1:T(8,128)(2,1)} %pad_maximum_fusion), channel_id=1, source_target_pairs={{0,4},{4,8},{8,12},{12,16},{16,20},{20,24},{24,28},{28,32},{32,36}... | collective-permute-start | bytes 1572872 | tf_op jit(solution)/shard_map/ppermute | solution.py:19
  9.1 5.8 %copy-start.3 = (f32[1,512,512]{1,2,0:T(8,128)}, f32[1,512,512]{1,2,0:T(8,128)S(1)}, u32[]{:S(2)}) copy-start(f32[1,512,512]{1,2,0:T(8,128)S(1)} %copy.13) | copy-start | bytes 3145732
  9.1 2.9 %copy-start.22 = (f32[128]{0:T(128)S(1)}, f32[128]{0:T(128)}, u32[]{:S(2)}) copy-start(f32[128]{0:T(128)} %param.13) | copy-start | bytes 1540
  19.9 2.5 %copy-start.13 = (bf16[512,2,256]{0,2,1:T(8,128)(2,1)}, bf16[512,2,256]{0,2,1:T(8,128)(2,1)S(1)}, u32[]{:S(2)}) copy-start(bf16[512,2,256]{0,2,1:T(8,128)(2,1)S(1)} %collective-permute-done.1) | copy-start | bytes 1572868
  20.0 2.4 %copy-start.11 = (bf16[512,2,256]{0,2,1:T(8,128)(2,1)}, bf16[512,2,256]{0,2,1:T(8,128)(2,1)S(1)}, u32[]{:S(2)}) copy-start(bf16[512,2,256]{0,2,1:T(8,128)(2,1)S(1)} %collective-permute-done) | copy-start | bytes 1572868
  20.1 2.3 %copy-start.15 = (pred[512,512]{0,1:T(8,128)(4,1)S(1)}, pred[512,512]{0,1:T(8,128)(4,1)}, u32[]{:S(2)}) copy-start(pred[512,512]{0,1:T(8,128)(4,1)} %get-tuple-element.25) | copy-start | bytes 786436
  24.7 2.3 %copy-start.9 = (bf16[1,512,256]{1,2,0:T(8,128)(2,1)S(1)}, bf16[1,512,256]{1,2,0:T(8,128)(2,1)}, u32[]{:S(2)}) copy-start(bf16[1,512,256]{1,2,0:T(8,128)(2,1)} %copy-done.8) | copy-start | bytes 786436
  26.9 2.6 %copy-start = (bf16[2,2,512,512]{2,3,1,0:T(8,128)(2,1)}, bf16[2,2,512,512]{2,3,1,0:T(8,128)(2,1)S(1)}, u32[]{:S(2)}) copy-start(bf16[2,2,512,512]{2,3,1,0:T(8,128)(2,1)S(1)} %get-tuple-element.24) | copy-start | bytes 6291460
  27.0 5.5 %copy-start.2 = (bf16[2,2,512,512]{2,3,1,0:T(8,128)(2,1)}, bf16[2,2,512,512]{2,3,1,0:T(8,128)(2,1)S(1)}, u32[]{:S(2)}) copy-start(bf16[2,2,512,512]{2,3,1,0:T(8,128)(2,1)S(1)} %get-tuple-element.23) | copy-start | bytes 6291460
  39.9 8.5 %collective-permute-start.2 = (f32[2,128]{1,0:T(2,128)S(1)}, f32[2,128]{1,0:T(2,128)S(1)}, u32[]{:S(2)}, u32[]{:S(2)}) collective-permute-start(f32[2,128]{1,0:T(2,128)S(1)} %pad_maximum_fusion.3), channel_id=1, source_target_pairs={{0,1},{1,0},{2,3},{3,2},{4,5},{5,4},{6,7},{7,6},{8,9},{9,8},{10,11... | collective-permute-start | bytes 3080 | tf_op jit(solution)/shard_map/ppermute | solution.py:24
  48.4 7.0 %collective-permute-start.3 = (f32[2,128]{1,0:T(2,128)S(1)}, f32[2,128]{1,0:T(2,128)S(1)}, u32[]{:S(2)}, u32[]{:S(2)}) collective-permute-start(f32[2,128]{1,0:T(2,128)S(1)} %fusion.55), channel_id=1, source_target_pairs={{0,2},{1,3},{2,0},{3,1},{4,6},{5,7},{6,4},{7,5},{8,10},{9,11},{10,... | collective-permute-start | bytes 3080 | tf_op jit(solution)/shard_map/ppermute | solution.py:24
  55.3 13.7 %collective-permute-start.4 = (f32[2,128]{1,0:T(2,128)S(1)}, f32[2,128]{1,0:T(2,128)S(1)}, u32[]{:S(2)}, u32[]{:S(2)}) collective-permute-start(f32[2,128]{1,0:T(2,128)S(1)} %fusion.84), channel_id=1, source_target_pairs={{0,384},{384,0},{1,385},{385,1},{2,386},{386,2},{3,387},{387,3},{4... | collective-permute-start | bytes 3080 | tf_op jit(solution)/shard_map/ppermute | solution.py:24
  69.0 5.8 %collective-permute-start.5 = (f32[2,128]{1,0:T(2,128)S(1)}, f32[2,128]{1,0:T(2,128)S(1)}, u32[]{:S(2)}, u32[]{:S(2)}) collective-permute-start(f32[2,128]{1,0:T(2,128)S(1)} %add.212), channel_id=1, source_target_pairs={{0,4},{4,0},{8,12},{12,8},{16,20},{20,16},{24,28},{28,24},{32,36},... | collective-permute-start | bytes 3080 | tf_op jit(solution)/shard_map/ppermute | solution.py:24
  74.8 14.0 %copy-start.20 = (bf16[512,2,128]{0,2,1:T(8,128)(2,1)S(1)}, bf16[512,2,128]{0,2,1:T(8,128)(2,1)}, u32[]{:S(2)}) copy-start(bf16[512,2,128]{0,2,1:T(8,128)(2,1)} %get-tuple-element.18) | copy-start | bytes 786436
  74.8 24.8 %copy-start.19 = (bf16[512,2,128]{0,2,1:T(8,128)(2,1)S(1)}, bf16[512,2,128]{0,2,1:T(8,128)(2,1)}, u32[]{:S(2)}) copy-start(bf16[512,2,128]{0,2,1:T(8,128)(2,1)} %get-tuple-element.20) | copy-start | bytes 786436
  74.8 47.4 %copy-start.5 = (f32[1,512,512]{1,2,0:T(8,128)S(1)}, f32[1,512,512]{1,2,0:T(8,128)}, u32[]{:S(2)}) copy-start(f32[1,512,512]{1,2,0:T(8,128)} %copy-done.3) | copy-start | bytes 3145732
  74.8 47.4 %copy-start.7 = (f32[512,2,2,128]{0,3,2,1:T(8,128)S(1)}, f32[512,2,2,128]{0,3,2,1:T(8,128)}, u32[]{:S(2)}) copy-start(f32[512,2,2,128]{0,3,2,1:T(8,128)} %get-tuple-element.34) | copy-start | bytes 3145732
  74.8 9.0 %collective-permute-start.6 = (f32[2,128]{1,0:T(2,128)S(1)}, f32[2,128]{1,0:T(2,128)S(1)}, u32[]{:S(2)}, u32[]{:S(2)}) collective-permute-start(f32[2,128]{1,0:T(2,128)S(1)} %add.213), channel_id=1, source_target_pairs={{0,8},{4,12},{8,0},{12,4},{16,24},{20,28},{24,16},{28,20},{32,40},... | collective-permute-start | bytes 3080 | tf_op jit(solution)/shard_map/ppermute | solution.py:24
  83.9 7.1 %collective-permute-start.7 = (f32[2,128]{1,0:T(2,128)S(1)}, f32[2,128]{1,0:T(2,128)S(1)}, u32[]{:S(2)}, u32[]{:S(2)}) collective-permute-start(f32[2,128]{1,0:T(2,128)S(1)} %add.214), channel_id=1, source_target_pairs={{0,16},{4,20},{8,24},{12,28},{16,0},{20,4},{24,8},{28,12},{32,48},... | collective-permute-start | bytes 3080 | tf_op jit(solution)/shard_map/ppermute | solution.py:24
  89.6 40.0 %collective-permute-start.13 = (bf16[512,2,256]{0,2,1:T(8,128)(2,1)}, bf16[512,2,256]{0,2,1:T(8,128)(2,1)}, u32[]{:S(2)}, u32[]{:S(2)}) collective-permute-start(bf16[512,2,256]{0,2,1:T(8,128)(2,1)} %pad_maximum_fusion.2), channel_id=1, source_target_pairs={{8,0},{12,4},{16,8},{20,12},{24,16},{28,20},{32,24},{36,28},{40,32... | collective-permute-start | bytes 1572872 | tf_op jit(solution)/shard_map/ppermute | solution.py:19
  90.9 10.9 %collective-permute-start.8 = (f32[2,128]{1,0:T(2,128)S(1)}, f32[2,128]{1,0:T(2,128)S(1)}, u32[]{:S(2)}, u32[]{:S(2)}) collective-permute-start(f32[2,128]{1,0:T(2,128)S(1)} %add.215), channel_id=1, source_target_pairs={{0,32},{4,36},{8,40},{12,44},{16,48},{20,52},{24,56},{28,60},{32,0... | collective-permute-start | bytes 3080 | tf_op jit(solution)/shard_map/ppermute | solution.py:24
  100.4 29.2 %copy-start.6 = (f32[512,2,128]{0,2,1:T(8,128)S(1)}, f32[512,2,128]{0,2,1:T(8,128)}, u32[]{:S(2)}) copy-start(f32[512,2,128]{0,2,1:T(8,128)} %get-tuple-element.36) | copy-start | bytes 1572868
  100.4 29.2 %collective-permute-start.12 = (bf16[512,2,256]{0,2,1:T(8,128)(2,1)}, bf16[512,2,256]{0,2,1:T(8,128)(2,1)}, u32[]{:S(2)}, u32[]{:S(2)}) collective-permute-start(bf16[512,2,256]{0,2,1:T(8,128)(2,1)} %pad_maximum_fusion.1), channel_id=1, source_target_pairs={{4,0},{8,4},{12,8},{16,12},{20,16},{24,20},{28,24},{32,28},{36,32}... | collective-permute-start | bytes 1572872 | tf_op jit(solution)/shard_map/ppermute | solution.py:19
  101.9 11.7 %collective-permute-start.9 = (f32[2,128]{1,0:T(2,128)S(1)}, f32[2,128]{1,0:T(2,128)S(1)}, u32[]{:S(2)}, u32[]{:S(2)}) collective-permute-start(f32[2,128]{1,0:T(2,128)S(1)} %add.216), channel_id=1, source_target_pairs={{0,64},{4,68},{8,72},{12,76},{16,80},{20,84},{24,88},{28,92},{32,9... | collective-permute-start | bytes 3080 | tf_op jit(solution)/shard_map/ppermute | solution.py:24
  113.6 11.9 %collective-permute-start.10 = (f32[2,128]{1,0:T(2,128)S(1)}, f32[2,128]{1,0:T(2,128)S(1)}, u32[]{:S(2)}, u32[]{:S(2)}) collective-permute-start(f32[2,128]{1,0:T(2,128)S(1)} %add.217), channel_id=1, source_target_pairs={{0,256},{4,260},{8,264},{12,268},{16,272},{20,276},{24,280},{28,28... | collective-permute-start | bytes 3080 | tf_op jit(solution)/shard_map/ppermute | solution.py:36
  120.3 9.4 %collective-permute-start.11 = (f32[2,128]{1,0:T(2,128)S(1)}, f32[2,128]{1,0:T(2,128)S(1)}, u32[]{:S(2)}, u32[]{:S(2)}) collective-permute-start(f32[2,128]{1,0:T(2,128)S(1)} %add.217), channel_id=1, source_target_pairs={{0,128},{4,132},{8,136},{12,140},{16,144},{20,148},{24,152},{28,15... | collective-permute-start | bytes 3080 | tf_op jit(solution)/shard_map/ppermute | solution.py:36
  122.2 8.7 %copy-start.1 = (bf16[2,2,512,512]{2,3,1,0:T(8,128)(2,1)S(1)}, bf16[2,2,512,512]{2,3,1,0:T(8,128)(2,1)}, u32[]{:S(2)}) copy-start(bf16[2,2,512,512]{2,3,1,0:T(8,128)(2,1)} %copy-done) | copy-start | bytes 6291460
  130.9 6.5 %copy-start.25 = (f32[2]{0:T(128)S(1)}, f32[2]{0:T(128)}, u32[]{:S(2)}) copy-start(f32[2]{0:T(128)} %constant.83) | copy-start | bytes 28
  (8 other events, 12.3 us)

commit v7 on v6

--- a/solution.py
+++ b/solution.py
@@ -48,9 +48,12 @@
     value = exchanged_sum(value, "fsdp", 1)
     value = exchanged_sum(value, "fsdp", 2)
     value = exchanged_sum(value, "dp", 1)
-    for stride in (1, 2, 4, 8, 16):
+    for stride in (1, 2, 4, 8):
         value = exchanged_sum(value, "ctx", stride)
-    return three_way_sum(value, "ctx", 32)
+    value = three_way_sum(value, "ctx", 16)
+    count = lax.axis_size("ctx")
+    half = count // 2
+    return value + lax.ppermute(value, "ctx", [(source, (source + half) % count) for source in range(count)])
 
 
 def normalize(raw, gain, factor):

time: 139 us -> 136 us (0.978)
  the two profiles are of different devices: /device:TPU:2 before, /device:TPU:26 now
where the time goes in v7:
time: 136 us; the launch traced here: 135 us
  starting transfers between devices  60.9 us (45%)
  waiting for transfers between devices  26.5 us (19%)
  matrix products  23.5 us (17%)
  local copies, waits for them, and re-layouts  13.1 us (10%)
  other arithmetic  10.1 us (7%)
  between operations  1.37 us (1%)
    ppermute x7, starting transfers between devices, exchanged_sum(): lax.ppermute(value, axis, [(source, source ^ stride) for source in range(...  36.4 us
    ppermute x7, waiting for transfers between devices, exchanged_sum(): lax.ppermute(value, axis, [(source, source ^ stride) for source in range(...  17.2 us
    unnamed x58, local copies, waits for them, and re-layouts  12.9 us
    ppermute x4, starting transfers between devices, passed_along(): lax.ppermute(value, axis, [(source, source + steps) for source in range(i...  10.7 us
    ppermute x4, waiting for transfers between devices, passed_along(): lax.ppermute(value, axis, [(source, source + steps) for source in range(i...  7.24 us
    ppermute x1, starting transfers between devices, total_over_devices(): lax.ppermute(value, 'ctx', [(source, (source + half) % count) for source...  7.01 us
    ppermute x2, starting transfers between devices, three_way_sum(): received.append(lax.ppermute(value, axis, pairs))  6.73 us
    dot_general x3, matrix products, forward_block(): jnp.einsum('tkgd,ukd->kgtu', query_n, key_block, preferred_element_type=j...  6.37 us
  transfers between devices with their start and end apart: 14, of which 9 were waited for; matrix products, arithmetic and copies ran while one was open for 11% of the time, Pallas kernels for 0%

profile of v7, /device:TPU:26, one launch (start us, length us, event | category | flops | bytes accessed | tf_op | source)
XLA Modules:
  0.0 135.4 jit_solution(16431258078524659811)
XLA Ops:
  3.8 4.7 %collective-permute-start.1 = (bf16[512,2,256]{0,2,1:T(8,128)(2,1)}, bf16[512,2,256]{0,2,1:T(8,128)(2,1)S(1)}, u32[]{:S(2)}, u32[]{:S(2)}) collective-permute-start(bf16[512,2,256]{0,2,1:T(8,128)(2,1)} %pad_maximum_fusion), channel_id=1, source_target_pairs={{0,8},{4,12},{8,16},{12,20},{16,24},{20,28},{24,32},{28,36},{32,40... | collective-permute-start | bytes 1572872 | tf_op jit(solution)/shard_map/ppermute | solution.py:19
  8.5 1.9 %collective-permute-start = (bf16[512,2,256]{0,2,1:T(8,128)(2,1)}, bf16[512,2,256]{0,2,1:T(8,128)(2,1)S(1)}, u32[]{:S(2)}, u32[]{:S(2)}) collective-permute-start(bf16[512,2,256]{0,2,1:T(8,128)(2,1)} %pad_maximum_fusion), channel_id=1, source_target_pairs={{0,4},{4,8},{8,12},{12,16},{16,20},{20,24},{24,28},{28,32},{32,36}... | collective-permute-start | bytes 1572872 | tf_op jit(solution)/shard_map/ppermute | solution.py:19
  11.2 1.7 %fusion.19 = (pred[512,512]{0,1:T(8,128)(4,1)}, pred[512,512]{0,1:T(8,128)(4,1)}, pred[512,512]{0,1:T(8,128)(4,1)S(1)}) fusion(s32[512]{0:T(512)S(1)} %iota_add_fusion.2, s32[512]{0:T(512)S(1)} %bitcast.216, s32[512]{0:T(512)S(1)} %get-tuple-element.38, s32[512]{0:T(512)S(1)} %get-tuple-element.37), kind=kLoop, calls=%fused_computation.48 | loop fusion | flops 4718592 | bytes 794624 | tf_op jit(solution)/shard_map/and | solution.py:99
  13.6 3.0 %fusion.6 = (f32[2,2,512]{2,1,0:T(2,128)S(1)}, f32[2,512,512,2]{2,1,3,0:T(8,128)}) fusion(pred[512,512]{0,1:T(8,128)(4,1)S(1)} %get-tuple-element.27, bf16[512,2,2,128]{0,3,2,1:T(8,128)(2,1)S(1)} %multiply_convert_fusion.1, bf16[512,2,128]{0,2,1:T(8,128)(2,1)S(1)} %bitcast.202, f32[128]{0:T(128)S(1)} %copy-done.22, f32[512,2]{0,1:T(2,128)S(1)} %add_rsqrt_fusion.3), kind=kOutput, calls=%fused_computation.15 | convolution fusion | flops 271054848 | bytes 5255680 | tf_op jit(solution)/shard_map/tkgd,ukd->kgtu/dot_general | solution.py:106
  17.8 3.2 %collective-permute-done.1 = bf16[512,2,256]{0,2,1:T(8,128)(2,1)S(1)} collective-permute-done((bf16[512,2,256]{0,2,1:T(8,128)(2,1)}, bf16[512,2,256]{0,2,1:T(8,128)(2,1)S(1)}, u32[]{:S(2)}, u32[]{:S(2)}) %collective-permute-start.1) | collective-permute-done | bytes 524320 | tf_op jit(solution)/shard_map/ppermute | solution.py:19
  21.2 4.0 %collective-permute-done = bf16[512,2,256]{0,2,1:T(8,128)(2,1)S(1)} collective-permute-done((bf16[512,2,256]{0,2,1:T(8,128)(2,1)}, bf16[512,2,256]{0,2,1:T(8,128)(2,1)S(1)}, u32[]{:S(2)}, u32[]{:S(2)}) %collective-permute-start) | collective-permute-done | bytes 524320 | tf_op jit(solution)/shard_map/ppermute | solution.py:19
  25.2 2.2 %fusion.8 = (f32[2,2,512]{2,1,0:T(2,128)S(1)}, f32[2,512,512,2]{2,1,3,0:T(8,128)S(1)}) fusion(pred[512,512]{0,1:T(8,128)(4,1)} %get-tuple-element.26, bf16[512,2,2,128]{0,3,2,1:T(8,128)(2,1)S(1)} %multiply_convert_fusion.1, f32[512,2]{0,1:T(2,128)S(1)} %add_rsqrt_fusion.1, f32[128]{0:T(128)S(1)} %copy-done.22, ...), kind=kOutput, calls=%fused_computation.17 | convolution fusion | flops 271054848 | bytes 5255680 | tf_op jit(solution)/shard_map/tkgd,ukd->kgtu/dot_general | solution.py:106
  29.8 2.2 %divide_convert_fusion.1 = (bf16[2,2,512,512]{2,3,1,0:T(8,128)(2,1)S(1)}, bf16[2,2,512,512]{2,3,1,0:T(8,128)(2,1)S(1)}, bf16[2,2,512,512]{2,3,1,0:T(8,128)(2,1)S(1)}) fusion(f32[2,512,512,2]{2,1,3,0:T(8,128)S(1)} %get-tuple-element.33, f32[2,2,512]{2,1,0:T(2,128)S(1)} %add_add_fusion, pred[512,512]{0,1:T(8,128)(4,1)S(1)} %copy-done.15, ...), kind=kLoop, calls=%fused_computation.13 | loop fusion | flops 9437184 | bytes 19668992 | tf_op jit(solution)/shard_map/convert_element_type | solution.py:115
  35.4 1.6 %fusion.34 = (f32[128]{0:T(128)S(1)}, f32[512,2,128]{0,2,1:T(8,128)}) fusion(bf16[512,2,128]{0,2,1:T(8,128)(2,1)S(1)} %bitcast.203, f32[512,2]{0,1:T(2,128)S(1)} %add_rsqrt_fusion.3, bf16[512,2,2,128]{0,3,2,1:T(8,128)(2,1)S(1)} %multiply_convert_fusion.1, bf16[2,2,512,512]{2,3,1,0:T(8,128)(2,1)S(1)} %fusion.5), kind=kOutput, calls=%fused_computation.69 | convolution fusion | flops 268959616 | bytes 3412480 | tf_op jit(solution)/shard_map/kgtu,tkgd->ukd/dot_general | solution.py:140
  40.3 1.6 %multiply_reduce_fusion = (f32[128]{0:T(128)S(1)}, f32[512,2,2]{0,2,1:T(2,128)S(1)}, f32[512,2,2,128]{0,3,2,1:T(8,128)}) fusion(f32[512,2,2,128]{0,3,2,1:T(8,128)S(1)} %bitcast.198, f32[512,2,2]{0,2,1:T(2,128)S(1)} %add_rsqrt_fusion, f32[128]{0:T(128)S(1)} %copy-done.23, f32[2,128,2,512]{3,1,2,0:T(8,128)S(1)} %convolution_add_fusion.1, ...), kind=kOutput, calls=%fused_computation.38 | convolution fusion | flops 271054720 | bytes 5527040 | tf_op jit(solution)/shard_map/kgtu,ukd->tkgd/dot_general | solution.py:137
  45.0 2.4 %collective-permute-start.2 = (f32[2,128]{1,0:T(2,128)S(1)}, f32[2,128]{1,0:T(2,128)S(1)}, u32[]{:S(2)}, u32[]{:S(2)}) collective-permute-start(f32[2,128]{1,0:T(2,128)S(1)} %pad_maximum_fusion.3), channel_id=1, source_target_pairs={{0,1},{1,0},{2,3},{3,2},{4,5},{5,4},{6,7},{7,6},{8,9},{9,8},{10,11... | collective-permute-start | bytes 3080 | tf_op jit(solution)/shard_map/ppermute | solution.py:24
  47.4 3.0 %collective-permute-done.2 = f32[2,128]{1,0:T(2,128)S(1)} collective-permute-done((f32[2,128]{1,0:T(2,128)S(1)}, f32[2,128]{1,0:T(2,128)S(1)}, u32[]{:S(2)}, u32[]{:S(2)}) %collective-permute-start.2) | collective-permute-done | bytes 1056 | tf_op jit(solution)/shard_map/ppermute | solution.py:24
  50.5 4.0 %collective-permute-start.3 = (f32[2,128]{1,0:T(2,128)S(1)}, f32[2,128]{1,0:T(2,128)S(1)}, u32[]{:S(2)}, u32[]{:S(2)}) collective-permute-start(f32[2,128]{1,0:T(2,128)S(1)} %fusion.55), channel_id=1, source_target_pairs={{0,2},{1,3},{2,0},{3,1},{4,6},{5,7},{6,4},{7,5},{8,10},{9,11},{10,... | collective-permute-start | bytes 3080 | tf_op jit(solution)/shard_map/ppermute | solution.py:24
  54.5 2.9 %collective-permute-done.3 = f32[2,128]{1,0:T(2,128)S(1)} collective-permute-done((f32[2,128]{1,0:T(2,128)S(1)}, f32[2,128]{1,0:T(2,128)S(1)}, u32[]{:S(2)}, u32[]{:S(2)}) %collective-permute-start.3) | collective-permute-done | bytes 1056 | tf_op jit(solution)/shard_map/ppermute | solution.py:24
  57.4 15.1 %collective-permute-start.4 = (f32[2,128]{1,0:T(2,128)S(1)}, f32[2,128]{1,0:T(2,128)S(1)}, u32[]{:S(2)}, u32[]{:S(2)}) collective-permute-start(f32[2,128]{1,0:T(2,128)S(1)} %fusion.84), channel_id=1, source_target_pairs={{0,384},{384,0},{1,385},{385,1},{2,386},{386,2},{3,387},{387,3},{4... | collective-permute-start | bytes 3080 | tf_op jit(solution)/shard_map/ppermute | solution.py:24
  74.1 2.1 %collective-permute-start.5 = (f32[2,128]{1,0:T(2,128)S(1)}, f32[2,128]{1,0:T(2,128)S(1)}, u32[]{:S(2)}, u32[]{:S(2)}) collective-permute-start(f32[2,128]{1,0:T(2,128)S(1)} %add.212), channel_id=1, source_target_pairs={{0,4},{4,0},{8,12},{12,8},{16,20},{20,16},{24,28},{28,24},{32,36},... | collective-permute-start | bytes 3080 | tf_op jit(solution)/shard_map/ppermute | solution.py:24
  76.2 2.4 %fusion.16 = bf16[512,2,128]{0,2,1:T(8,128)(2,1)S(1)} fusion(bf16[2,2,512,512]{2,3,1,0:T(8,128)(2,1)} %copy-done.2, bf16[512,2,2,128]{0,3,2,1:T(8,128)(2,1)S(1)} %bitcast.193), kind=kOutput, calls=%fused_computation.36 | convolution fusion | flops 268566528 | bytes 2883584 | tf_op jit(solution)/shard_map/kgtu,tkgd->ukd/dot_general | solution.py:143
  78.7 2.5 %collective-permute-start.6 = (f32[2,128]{1,0:T(2,128)S(1)}, f32[2,128]{1,0:T(2,128)S(1)}, u32[]{:S(2)}, u32[]{:S(2)}) collective-permute-start(f32[2,128]{1,0:T(2,128)S(1)} %add.213), channel_id=1, source_target_pairs={{0,8},{4,12},{8,0},{12,4},{16,24},{20,28},{24,16},{28,20},{32,40},... | collective-permute-start | bytes 3080 | tf_op jit(solution)/shard_map/ppermute | solution.py:24
  82.0 2.3 %collective-permute-done.6 = f32[2,128]{1,0:T(2,128)S(1)} collective-permute-done((f32[2,128]{1,0:T(2,128)S(1)}, f32[2,128]{1,0:T(2,128)S(1)}, u32[]{:S(2)}, u32[]{:S(2)}) %collective-permute-start.6) | collective-permute-done | bytes 1056 | tf_op jit(solution)/shard_map/ppermute | solution.py:24
  84.3 2.2 %collective-permute-start.7 = (f32[2,128]{1,0:T(2,128)S(1)}, f32[2,128]{1,0:T(2,128)S(1)}, u32[]{:S(2)}, u32[]{:S(2)}) collective-permute-start(f32[2,128]{1,0:T(2,128)S(1)} %add.214), channel_id=1, source_target_pairs={{0,16},{4,20},{8,24},{12,28},{16,0},{20,4},{24,8},{28,12},{32,48},... | collective-permute-start | bytes 3080 | tf_op jit(solution)/shard_map/ppermute | solution.py:24
  87.4 2.0 %collective-permute-start.13 = (bf16[512,2,256]{0,2,1:T(8,128)(2,1)}, bf16[512,2,256]{0,2,1:T(8,128)(2,1)}, u32[]{:S(2)}, u32[]{:S(2)}) collective-permute-start(bf16[512,2,256]{0,2,1:T(8,128)(2,1)} %pad_maximum_fusion.2), channel_id=1, source_target_pairs={{8,0},{12,4},{16,8},{20,12},{24,16},{28,20},{32,24},{36,28},{40,32... | collective-permute-start | bytes 1572872 | tf_op jit(solution)/shard_map/ppermute | solution.py:19
  90.7 8.0 %collective-permute-start.8 = (f32[2,128]{1,0:T(2,128)S(1)}, f32[2,128]{1,0:T(2,128)S(1)}, u32[]{:S(2)}, u32[]{:S(2)}) collective-permute-start(f32[2,128]{1,0:T(2,128)S(1)} %add.215), channel_id=1, source_target_pairs={{0,32},{4,36},{8,40},{12,44},{16,48},{20,52},{24,56},{28,60},{32,0... | collective-permute-start | bytes 3080 | tf_op jit(solution)/shard_map/ppermute | solution.py:24
  99.5 2.0 %collective-permute-start.12 = (bf16[512,2,256]{0,2,1:T(8,128)(2,1)}, bf16[512,2,256]{0,2,1:T(8,128)(2,1)}, u32[]{:S(2)}, u32[]{:S(2)}) collective-permute-start(bf16[512,2,256]{0,2,1:T(8,128)(2,1)} %pad_maximum_fusion.1), channel_id=1, source_target_pairs={{4,0},{8,4},{12,8},{16,12},{20,16},{24,20},{28,24},{32,28},{36,32}... | collective-permute-start | bytes 1572872 | tf_op jit(solution)/shard_map/ppermute | solution.py:19
  101.6 6.3 %collective-permute-done.8 = f32[2,128]{1,0:T(2,128)S(1)} collective-permute-done((f32[2,128]{1,0:T(2,128)S(1)}, f32[2,128]{1,0:T(2,128)S(1)}, u32[]{:S(2)}, u32[]{:S(2)}) %collective-permute-start.8) | collective-permute-done | bytes 1056 | tf_op jit(solution)/shard_map/ppermute | solution.py:24
  107.9 3.4 %collective-permute-start.10 = (f32[2,128]{1,0:T(2,128)S(1)}, f32[2,128]{1,0:T(2,128)S(1)}, u32[]{:S(2)}, u32[]{:S(2)}) collective-permute-start(f32[2,128]{1,0:T(2,128)S(1)} %add.216), channel_id=1, source_target_pairs={{0,64},{4,68},{8,72},{12,76},{16,80},{20,84},{24,88},{28,92},{32,9... | collective-permute-start | bytes 3080 | tf_op jit(solution)/shard_map/ppermute | solution.py:36
  111.3 3.4 %collective-permute-start.9 = (f32[2,128]{1,0:T(2,128)S(1)}, f32[2,128]{1,0:T(2,128)S(1)}, u32[]{:S(2)}, u32[]{:S(2)}) collective-permute-start(f32[2,128]{1,0:T(2,128)S(1)} %add.216), channel_id=1, source_target_pairs={{0,128},{4,132},{8,136},{12,140},{16,144},{20,148},{24,152},{28,15... | collective-permute-start | bytes 3080 | tf_op jit(solution)/shard_map/ppermute | solution.py:36
  114.7 2.1 %collective-permute-done.9 = f32[2,128]{1,0:T(2,128)S(1)} collective-permute-done((f32[2,128]{1,0:T(2,128)S(1)}, f32[2,128]{1,0:T(2,128)S(1)}, u32[]{:S(2)}, u32[]{:S(2)}) %collective-permute-start.9) | collective-permute-done | bytes 1056 | tf_op jit(solution)/shard_map/ppermute | solution.py:36
  116.7 7.0 %collective-permute-start.11 = (f32[2,128]{1,0:T(2,128)S(1)}, f32[2,128]{1,0:T(2,128)S(1)}, u32[]{:S(2)}, u32[]{:S(2)}) collective-permute-start(f32[2,128]{1,0:T(2,128)S(1)} %select_add_fusion), channel_id=1, source_target_pairs={{0,192},{4,196},{8,200},{12,204},{16,208},{20,212},{24,216},{28,22... | collective-permute-start | bytes 3080 | tf_op jit(solution)/shard_map/ppermute | solution.py:56
  124.9 2.0 %copy.40 = bf16[1,512,512]{2,1,0:T(8,128)(2,1)} copy(bf16[1,512,512]{1,2,0:T(8,128)(2,1)} %bitcast.210) | data formatting | bytes 1048576
  128.2 2.9 %add_convert_fusion = (bf16[512,2,128]{0,2,1:T(8,128)(2,1)}, bf16[512,2,128]{0,2,1:T(8,128)(2,1)}) fusion(bf16[512,2,256]{0,2,1:T(8,128)(2,1)} %collective-permute-done.13, bf16[512,2,256]{0,2,1:T(8,128)(2,1)} %collective-permute-done.12, f32[512,2]{0,1:T(2,128)S(1)} %broadcast_multiply_fusion.1, f32[512,2]{0,1:T(2,128)S(1)} %add_rsqrt_fusion.3, ...), kind=kOutput, calls=%fused_computation.80 | convolution fusion | flops 270532608 | bytes 4989440 | tf_op jit(solution)/shard_map/kgtu,tkgd->ukd/dot_general | solution.py:143
  131.2 1.8 %copy.41 = bf16[1,512,256]{2,1,0:T(8,128)(2,1)} copy(bf16[1,512,256]{1,2,0:T(8,128)(2,1)} %bitcast.212) | data formatting | bytes 524288
  133.0 1.8 %copy.42 = bf16[1,512,256]{2,1,0:T(8,128)(2,1)} copy(bf16[1,512,256]{1,2,0:T(8,128)(2,1)} %bitcast.211) | data formatting | bytes 524288
  (107 shorter events, 26.0 us)
Async XLA Ops:
  0.6 9.9 %copy-start.21 = (bf16[1,512,512]{2,1,0:T(8,128)(2,1)S(1)}, bf16[1,512,512]{2,1,0:T(8,128)(2,1)}, u32[]{:S(2)}) copy-start(bf16[1,512,512]{2,1,0:T(8,128)(2,1)} %param.8) | copy-start | bytes 1572868
  2.9 8.2 %copy-start.8 = (bf16[1,512,256]{1,2,0:T(8,128)(2,1)}, bf16[1,512,256]{1,2,0:T(8,128)(2,1)S(1)}, u32[]{:S(2)}) copy-start(bf16[1,512,256]{1,2,0:T(8,128)(2,1)S(1)} %copy.16) | copy-start | bytes 786436
  2.9 8.0 %copy-start.23 = (f32[128]{0:T(128)S(1)}, f32[128]{0:T(128)}, u32[]{:S(2)}) copy-start(f32[128]{0:T(128)} %param.12) | copy-start | bytes 1540
  3.8 17.3 %collective-permute-start.1 = (bf16[512,2,256]{0,2,1:T(8,128)(2,1)}, bf16[512,2,256]{0,2,1:T(8,128)(2,1)S(1)}, u32[]{:S(2)}, u32[]{:S(2)}) collective-permute-start(bf16[512,2,256]{0,2,1:T(8,128)(2,1)} %pad_maximum_fusion), channel_id=1, source_target_pairs={{0,8},{4,12},{8,16},{12,20},{16,24},{20,28},{24,32},{28,36},{32,40... | collective-permute-start | bytes 1572872 | tf_op jit(solution)/shard_map/ppermute | solution.py:19
  8.5 16.7 %collective-permute-start = (bf16[512,2,256]{0,2,1:T(8,128)(2,1)}, bf16[512,2,256]{0,2,1:T(8,128)(2,1)S(1)}, u32[]{:S(2)}, u32[]{:S(2)}) collective-permute-start(bf16[512,2,256]{0,2,1:T(8,128)(2,1)} %pad_maximum_fusion), channel_id=1, source_target_pairs={{0,4},{4,8},{8,12},{12,16},{16,20},{20,24},{24,28},{28,32},{32,36}... | collective-permute-start | bytes 1572872 | tf_op jit(solution)/shard_map/ppermute | solution.py:19
  10.7 5.8 %copy-start.3 = (f32[1,512,512]{1,2,0:T(8,128)}, f32[1,512,512]{1,2,0:T(8,128)S(1)}, u32[]{:S(2)}) copy-start(f32[1,512,512]{1,2,0:T(8,128)S(1)} %copy.13) | copy-start | bytes 3145732
  10.7 2.9 %copy-start.22 = (f32[128]{0:T(128)S(1)}, f32[128]{0:T(128)}, u32[]{:S(2)}) copy-start(f32[128]{0:T(128)} %param.13) | copy-start | bytes 1540
  21.1 6.4 %copy-start.13 = (bf16[512,2,256]{0,2,1:T(8,128)(2,1)}, bf16[512,2,256]{0,2,1:T(8,128)(2,1)S(1)}, u32[]{:S(2)}) copy-start(bf16[512,2,256]{0,2,1:T(8,128)(2,1)S(1)} %collective-permute-done.1) | copy-start | bytes 1572868
  25.1 2.4 %copy-start.11 = (bf16[512,2,256]{0,2,1:T(8,128)(2,1)}, bf16[512,2,256]{0,2,1:T(8,128)(2,1)S(1)}, u32[]{:S(2)}) copy-start(bf16[512,2,256]{0,2,1:T(8,128)(2,1)S(1)} %collective-permute-done) | copy-start | bytes 1572868
  25.2 2.3 %copy-start.15 = (pred[512,512]{0,1:T(8,128)(4,1)S(1)}, pred[512,512]{0,1:T(8,128)(4,1)}, u32[]{:S(2)}) copy-start(pred[512,512]{0,1:T(8,128)(4,1)} %get-tuple-element.25) | copy-start | bytes 786436
  29.8 2.3 %copy-start.9 = (bf16[1,512,256]{1,2,0:T(8,128)(2,1)S(1)}, bf16[1,512,256]{1,2,0:T(8,128)(2,1)}, u32[]{:S(2)}) copy-start(bf16[1,512,256]{1,2,0:T(8,128)(2,1)} %copy-done.8) | copy-start | bytes 786436
  32.1 2.6 %copy-start = (bf16[2,2,512,512]{2,3,1,0:T(8,128)(2,1)}, bf16[2,2,512,512]{2,3,1,0:T(8,128)(2,1)S(1)}, u32[]{:S(2)}) copy-start(bf16[2,2,512,512]{2,3,1,0:T(8,128)(2,1)S(1)} %get-tuple-element.24) | copy-start | bytes 6291460
  32.1 5.5 %copy-start.2 = (bf16[2,2,512,512]{2,3,1,0:T(8,128)(2,1)}, bf16[2,2,512,512]{2,3,1,0:T(8,128)(2,1)S(1)}, u32[]{:S(2)}) copy-start(bf16[2,2,512,512]{2,3,1,0:T(8,128)(2,1)S(1)} %get-tuple-element.23) | copy-start | bytes 6291460
  45.0 5.5 %collective-permute-start.2 = (f32[2,128]{1,0:T(2,128)S(1)}, f32[2,128]{1,0:T(2,128)S(1)}, u32[]{:S(2)}, u32[]{:S(2)}) collective-permute-start(f32[2,128]{1,0:T(2,128)S(1)} %pad_maximum_fusion.3), channel_id=1, source_target_pairs={{0,1},{1,0},{2,3},{3,2},{4,5},{5,4},{6,7},{7,6},{8,9},{9,8},{10,11... | collective-permute-start | bytes 3080 | tf_op jit(solution)/shard_map/ppermute | solution.py:24
  50.5 7.0 %collective-permute-start.3 = (f32[2,128]{1,0:T(2,128)S(1)}, f32[2,128]{1,0:T(2,128)S(1)}, u32[]{:S(2)}, u32[]{:S(2)}) collective-permute-start(f32[2,128]{1,0:T(2,128)S(1)} %fusion.55), channel_id=1, source_target_pairs={{0,2},{1,3},{2,0},{3,1},{4,6},{5,7},{6,4},{7,5},{8,10},{9,11},{10,... | collective-permute-start | bytes 3080 | tf_op jit(solution)/shard_map/ppermute | solution.py:24
  57.4 16.7 %collective-permute-start.4 = (f32[2,128]{1,0:T(2,128)S(1)}, f32[2,128]{1,0:T(2,128)S(1)}, u32[]{:S(2)}, u32[]{:S(2)}) collective-permute-start(f32[2,128]{1,0:T(2,128)S(1)} %fusion.84), channel_id=1, source_target_pairs={{0,384},{384,0},{1,385},{385,1},{2,386},{386,2},{3,387},{387,3},{4... | collective-permute-start | bytes 3080 | tf_op jit(solution)/shard_map/ppermute | solution.py:24
  74.1 4.5 %collective-permute-start.5 = (f32[2,128]{1,0:T(2,128)S(1)}, f32[2,128]{1,0:T(2,128)S(1)}, u32[]{:S(2)}, u32[]{:S(2)}) collective-permute-start(f32[2,128]{1,0:T(2,128)S(1)} %add.212), channel_id=1, source_target_pairs={{0,4},{4,0},{8,12},{12,8},{16,20},{20,16},{24,28},{28,24},{32,36},... | collective-permute-start | bytes 3080 | tf_op jit(solution)/shard_map/ppermute | solution.py:24
  78.6 7.9 %copy-start.20 = (bf16[512,2,128]{0,2,1:T(8,128)(2,1)S(1)}, bf16[512,2,128]{0,2,1:T(8,128)(2,1)}, u32[]{:S(2)}) copy-start(bf16[512,2,128]{0,2,1:T(8,128)(2,1)} %get-tuple-element.18) | copy-start | bytes 786436
  78.6 20.1 %copy-start.19 = (bf16[512,2,128]{0,2,1:T(8,128)(2,1)S(1)}, bf16[512,2,128]{0,2,1:T(8,128)(2,1)}, u32[]{:S(2)}) copy-start(bf16[512,2,128]{0,2,1:T(8,128)(2,1)} %get-tuple-element.20) | copy-start | bytes 786436
  78.7 45.1 %copy-start.5 = (f32[1,512,512]{1,2,0:T(8,128)S(1)}, f32[1,512,512]{1,2,0:T(8,128)}, u32[]{:S(2)}) copy-start(f32[1,512,512]{1,2,0:T(8,128)} %copy-done.3) | copy-start | bytes 3145732
  78.7 45.1 %copy-start.7 = (f32[512,2,2,128]{0,3,2,1:T(8,128)S(1)}, f32[512,2,2,128]{0,3,2,1:T(8,128)}, u32[]{:S(2)}) copy-start(f32[512,2,2,128]{0,3,2,1:T(8,128)} %get-tuple-element.34) | copy-start | bytes 3145732
  78.7 5.6 %collective-permute-start.6 = (f32[2,128]{1,0:T(2,128)S(1)}, f32[2,128]{1,0:T(2,128)S(1)}, u32[]{:S(2)}, u32[]{:S(2)}) collective-permute-start(f32[2,128]{1,0:T(2,128)S(1)} %add.213), channel_id=1, source_target_pairs={{0,8},{4,12},{8,0},{12,4},{16,24},{20,28},{24,16},{28,20},{32,40},... | collective-permute-start | bytes 3080 | tf_op jit(solution)/shard_map/ppermute | solution.py:24
  84.3 6.4 %collective-permute-start.7 = (f32[2,128]{1,0:T(2,128)S(1)}, f32[2,128]{1,0:T(2,128)S(1)}, u32[]{:S(2)}, u32[]{:S(2)}) collective-permute-start(f32[2,128]{1,0:T(2,128)S(1)} %add.214), channel_id=1, source_target_pairs={{0,16},{4,20},{8,24},{12,28},{16,0},{20,4},{24,8},{28,12},{32,48},... | collective-permute-start | bytes 3080 | tf_op jit(solution)/shard_map/ppermute | solution.py:24
  87.4 39.6 %collective-permute-start.13 = (bf16[512,2,256]{0,2,1:T(8,128)(2,1)}, bf16[512,2,256]{0,2,1:T(8,128)(2,1)}, u32[]{:S(2)}, u32[]{:S(2)}) collective-permute-start(bf16[512,2,256]{0,2,1:T(8,128)(2,1)} %pad_maximum_fusion.2), channel_id=1, source_target_pairs={{8,0},{12,4},{16,8},{20,12},{24,16},{28,20},{32,24},{36,28},{40,32... | collective-permute-start | bytes 1572872 | tf_op jit(solution)/shard_map/ppermute | solution.py:19
  90.7 17.2 %collective-permute-start.8 = (f32[2,128]{1,0:T(2,128)S(1)}, f32[2,128]{1,0:T(2,128)S(1)}, u32[]{:S(2)}, u32[]{:S(2)}) collective-permute-start(f32[2,128]{1,0:T(2,128)S(1)} %add.215), channel_id=1, source_target_pairs={{0,32},{4,36},{8,40},{12,44},{16,48},{20,52},{24,56},{28,60},{32,0... | collective-permute-start | bytes 3080 | tf_op jit(solution)/shard_map/ppermute | solution.py:24
  99.5 27.4 %copy-start.6 = (f32[512,2,128]{0,2,1:T(8,128)S(1)}, f32[512,2,128]{0,2,1:T(8,128)}, u32[]{:S(2)}) copy-start(f32[512,2,128]{0,2,1:T(8,128)} %get-tuple-element.36) | copy-start | bytes 1572868
  99.5 27.4 %collective-permute-start.12 = (bf16[512,2,256]{0,2,1:T(8,128)(2,1)}, bf16[512,2,256]{0,2,1:T(8,128)(2,1)}, u32[]{:S(2)}, u32[]{:S(2)}) collective-permute-start(bf16[512,2,256]{0,2,1:T(8,128)(2,1)} %pad_maximum_fusion.1), channel_id=1, source_target_pairs={{4,0},{8,4},{12,8},{16,12},{20,16},{24,20},{28,24},{32,28},{36,32}... | collective-permute-start | bytes 1572872 | tf_op jit(solution)/shard_map/ppermute | solution.py:19
  107.9 6.8 %collective-permute-start.10 = (f32[2,128]{1,0:T(2,128)S(1)}, f32[2,128]{1,0:T(2,128)S(1)}, u32[]{:S(2)}, u32[]{:S(2)}) collective-permute-start(f32[2,128]{1,0:T(2,128)S(1)} %add.216), channel_id=1, source_target_pairs={{0,64},{4,68},{8,72},{12,76},{16,80},{20,84},{24,88},{28,92},{32,9... | collective-permute-start | bytes 3080 | tf_op jit(solution)/shard_map/ppermute | solution.py:36
  111.3 5.5 %collective-permute-start.9 = (f32[2,128]{1,0:T(2,128)S(1)}, f32[2,128]{1,0:T(2,128)S(1)}, u32[]{:S(2)}, u32[]{:S(2)}) collective-permute-start(f32[2,128]{1,0:T(2,128)S(1)} %add.216), channel_id=1, source_target_pairs={{0,128},{4,132},{8,136},{12,140},{16,144},{20,148},{24,152},{28,15... | collective-permute-start | bytes 3080 | tf_op jit(solution)/shard_map/ppermute | solution.py:36
  116.7 10.2 %collective-permute-start.11 = (f32[2,128]{1,0:T(2,128)S(1)}, f32[2,128]{1,0:T(2,128)S(1)}, u32[]{:S(2)}, u32[]{:S(2)}) collective-permute-start(f32[2,128]{1,0:T(2,128)S(1)} %select_add_fusion), channel_id=1, source_target_pairs={{0,192},{4,196},{8,200},{12,204},{16,208},{20,212},{24,216},{28,22... | collective-permute-start | bytes 3080 | tf_op jit(solution)/shard_map/ppermute | solution.py:56
  123.8 4.4 %copy-start.1 = (bf16[2,2,512,512]{2,3,1,0:T(8,128)(2,1)S(1)}, bf16[2,2,512,512]{2,3,1,0:T(8,128)(2,1)}, u32[]{:S(2)}) copy-start(bf16[2,2,512,512]{2,3,1,0:T(8,128)(2,1)} %copy-done) | copy-start | bytes 6291460
  128.2 6.5 %copy-start.25 = (f32[2]{0:T(128)S(1)}, f32[2]{0:T(128)}, u32[]{:S(2)}) copy-start(f32[2]{0:T(128)} %constant.83) | copy-start | bytes 28
  (8 other events, 12.3 us)

commit v8 on v7

--- a/solution.py
+++ b/solution.py
@@ -44,13 +44,22 @@
     return ordered[0] + ordered[1] + ordered[2]
 
 
-def total_over_devices(value):
+def first_rounds(value):
     value = exchanged_sum(value, "fsdp", 1)
     value = exchanged_sum(value, "fsdp", 2)
     value = exchanged_sum(value, "dp", 1)
-    for stride in (1, 2, 4, 8):
+    for stride in (1, 2):
         value = exchanged_sum(value, "ctx", stride)
-    value = three_way_sum(value, "ctx", 16)
+    return value
+
+
+def middle_rounds(value):
+    for stride in (4, 8):
+        value = exchanged_sum(value, "ctx", stride)
+    return three_way_sum(value, "ctx", 16)
+
+
+def last_round(value):
     count = lax.axis_size("ctx")
     half = count // 2
     return value + lax.ppermute(value, "ctx", [(source, (source + half) % count) for source in range(count)])
@@ -149,13 +158,13 @@
     for distance in range(1, reach + 1):
         key_term = key_term + jnp.sum(pieces[distance][0] * block_hats[distance], axis=(0, 1))
     partial_sums = jnp.stack([jnp.sum(dquery_n * query_hat, axis=(0, 1, 2)) * factor, key_term])
-    summed = total_over_devices(partial_sums)
     returns = [
         passed_along(
             jnp.concatenate(pieces[distance], axis=-1).astype(jnp.bfloat16), "ctx", -distance
         )
         for distance in range(1, reach + 1)
     ]
+    summed = first_rounds(partial_sums)
     summed, *returns = lax.optimization_barrier((summed, *returns))
     dkey_n = pieces[0][0]
     dvalue_sum = pieces[0][1]
@@ -173,6 +182,11 @@
         .reshape(1, tokens, -1)
     )
     value_grad = dvalue_sum.astype(jnp.bfloat16).reshape(1, tokens, -1)
+    summed = middle_rounds(summed)
+    summed, query_grad, key_grad, value_grad = lax.optimization_barrier(
+        (summed, query_grad, key_grad, value_grad)
+    )
+    summed = last_round(summed)
     counted = lax.axis_size("dp") * lax.axis_size("ctx") * tokens
     normalizers = jnp.array([[(counted * HQ) ** (-0.5)], [(counted * HK) ** (-0.5)]], jnp.float32)
     return (query_grad, key_grad, value_grad, summed * normalizers)

time: 136 us -> 132 us (0.971)
  the two profiles are of different devices: /device:TPU:26 before, /device:TPU:4 now
where the time goes in v8:
time: 132 us; the launch traced here: 131 us
  starting transfers between devices  76.9 us (58%)
  matrix products  20.6 us (16%)
  local copies, waits for them, and re-layouts  12.5 us (9%)
  other arithmetic  11.6 us (9%)
  waiting for transfers between devices  8.6 us (7%)
    ppermute x7, starting transfers between devices, exchanged_sum(): lax.ppermute(value, axis, [(source, source ^ stride) for source in range(...  48.6 us
    unnamed x44, local copies, waits for them, and re-layouts  12.3 us
    ppermute x2, starting transfers between devices, three_way_sum(): received.append(lax.ppermute(value, axis, pairs))  11.8 us
    ppermute x1, starting transfers between devices, last_round(): lax.ppermute(value, 'ctx', [(source, (source + half) % count) for source...  8.77 us
    ppermute x4, starting transfers between devices, passed_along(): lax.ppermute(value, axis, [(source, source + steps) for source in range(i...  7.68 us
    dot_general x3, matrix products, forward_block(): jnp.einsum('tkgd,ukd->kgtu', query_n, key_block, preferred_element_type=j...  6.43 us
    dot_general x3, matrix products, shards(): jnp.einsum('kgtu,tkgd->ukd', prob, grads_in, preferred_element_type=jnp.f...  4.52 us
    ppermute x4, waiting for transfers between devices, passed_along(): lax.ppermute(value, axis, [(source, source + steps) for source in range(i...  4.33 us
  transfers between devices with their start and end apart: 14, of which 7 were waited for; matrix products, arithmetic and copies ran while one was open for 16% of the time, Pallas kernels for 0%

profile of v8, /device:TPU:4, one launch (start us, length us, event | category | flops | bytes accessed | tf_op | source)
XLA Modules:
  0.0 131.5 jit_solution(16289950373803955605)
XLA Ops:
  0.6 1.1 copy.12
  3.8 3.5 %collective-permute-start.1 = (bf16[512,2,256]{0,2,1:T(8,128)(2,1)}, bf16[512,2,256]{0,2,1:T(8,128)(2,1)S(1)}, u32[]{:S(2)}, u32[]{:S(2)}) collective-permute-start(bf16[512,2,256]{0,2,1:T(8,128)(2,1)} %pad_maximum_fusion), channel_id=1, source_target_pairs={{0,8},{4,12},{8,16},{12,20},{16,24},{20,28},{24,32},{28,36},{32,40... | collective-permute-start | bytes 1572872 | tf_op jit(solution)/shard_map/ppermute | solution.py:19
  7.3 1.5 %collective-permute-start = (bf16[512,2,256]{0,2,1:T(8,128)(2,1)}, bf16[512,2,256]{0,2,1:T(8,128)(2,1)S(1)}, u32[]{:S(2)}, u32[]{:S(2)}) collective-permute-start(bf16[512,2,256]{0,2,1:T(8,128)(2,1)} %pad_maximum_fusion), channel_id=1, source_target_pairs={{0,4},{4,8},{8,12},{12,16},{16,20},{20,24},{24,28},{28,32},{32,36}... | collective-permute-start | bytes 1572872 | tf_op jit(solution)/shard_map/ppermute | solution.py:19
  9.6 1.7 %fusion.19 = (pred[512,512]{0,1:T(8,128)(4,1)}, pred[512,512]{0,1:T(8,128)(4,1)}, pred[512,512]{0,1:T(8,128)(4,1)S(1)}) fusion(s32[512]{0:T(512)S(1)} %iota_add_fusion.2, s32[512]{0:T(512)S(1)} %bitcast.216, s32[512]{0:T(512)S(1)} %get-tuple-element.46, s32[512]{0:T(512)S(1)} %get-tuple-element.45), kind=kLoop, calls=%fused_computation.48 | loop fusion | flops 4718592 | bytes 794624 | tf_op jit(solution)/shard_map/and | solution.py:108
  11.3 3.0 %fusion.6 = (f32[2,2,512]{2,1,0:T(2,128)S(1)}, f32[2,512,512,2]{2,1,3,0:T(8,128)}) fusion(pred[512,512]{0,1:T(8,128)(4,1)S(1)} %get-tuple-element.35, bf16[512,2,2,128]{0,3,2,1:T(8,128)(2,1)S(1)} %multiply_convert_fusion.1, bf16[512,2,128]{0,2,1:T(8,128)(2,1)S(1)} %bitcast.202, f32[128]{0:T(128)S(1)} %copy-done.15, f32[512,2]{0,1:T(2,128)S(1)} %add_rsqrt_fusion.3), kind=kOutput, calls=%fused_computation.15 | convolution fusion | flops 271054848 | bytes 5255680 | tf_op jit(solution)/shard_map/tkgd,ukd->kgtu/dot_general | solution.py:115
  14.3 1.3 copy.21
  15.5 4.3 %collective-permute-done.1 = bf16[512,2,256]{0,2,1:T(8,128)(2,1)S(1)} collective-permute-done((bf16[512,2,256]{0,2,1:T(8,128)(2,1)}, bf16[512,2,256]{0,2,1:T(8,128)(2,1)S(1)}, u32[]{:S(2)}, u32[]{:S(2)}) %collective-permute-start.1) | collective-permute-done | bytes 524320 | tf_op jit(solution)/shard_map/ppermute | solution.py:19
  20.1 2.3 %fusion.8 = (f32[2,2,512]{2,1,0:T(2,128)S(1)}, f32[2,512,512,2]{2,1,3,0:T(8,128)S(1)}) fusion(pred[512,512]{0,1:T(8,128)(4,1)} %get-tuple-element.34, bf16[512,2,2,128]{0,3,2,1:T(8,128)(2,1)S(1)} %multiply_convert_fusion.1, f32[512,2]{0,1:T(2,128)S(1)} %add_rsqrt_fusion.1, f32[128]{0:T(128)S(1)} %copy-done.15, ...), kind=kOutput, calls=%fused_computation.17 | convolution fusion | flops 271054848 | bytes 5255680 | tf_op jit(solution)/shard_map/tkgd,ukd->kgtu/dot_general | solution.py:115
  22.4 1.2 fusion.7
  24.7 2.2 %divide_convert_fusion.1 = (bf16[2,2,512,512]{2,3,1,0:T(8,128)(2,1)S(1)}, bf16[2,2,512,512]{2,3,1,0:T(8,128)(2,1)S(1)}, bf16[2,2,512,512]{2,3,1,0:T(8,128)(2,1)S(1)}) fusion(f32[2,512,512,2]{2,1,3,0:T(8,128)S(1)} %get-tuple-element.41, f32[2,2,512]{2,1,0:T(2,128)S(1)} %add_add_fusion, pred[512,512]{0,1:T(8,128)(4,1)S(1)} %copy-done.10, ...), kind=kLoop, calls=%fused_computation.13 | loop fusion | flops 9437184 | bytes 19668992 | tf_op jit(solution)/shard_map/convert_element_type | solution.py:124
  32.5 1.6 %fusion.34 = (f32[128]{0:T(128)S(1)}, f32[512,2,128]{0,2,1:T(8,128)}) fusion(bf16[512,2,128]{0,2,1:T(8,128)(2,1)S(1)} %bitcast.204, f32[512,2]{0,1:T(2,128)S(1)} %add_rsqrt_fusion.3, bf16[512,2,2,128]{0,3,2,1:T(8,128)(2,1)S(1)} %multiply_convert_fusion.1, bf16[2,2,512,512]{2,3,1,0:T(8,128)(2,1)S(1)} %fusion.5), kind=kOutput, calls=%fused_computation.69 | convolution fusion | flops 268959616 | bytes 3412480 | tf_op jit(solution)/shard_map/kgtu,tkgd->ukd/dot_general | solution.py:149
  36.8 1.6 %multiply_reduce_fusion = (f32[512,2,2]{0,2,1:T(2,128)S(1)}, f32[128]{0:T(128)S(1)}, f32[512,2,2,128]{0,3,2,1:T(8,128)}) fusion(f32[512,2,2,128]{0,3,2,1:T(8,128)S(1)} %bitcast.199, f32[128]{0:T(128)S(1)} %copy-done.16, f32[512,2,2]{0,2,1:T(2,128)S(1)} %add_rsqrt_fusion, f32[2,128,2,512]{3,1,2,0:T(8,128)S(1)} %convolution_add_fusion.1, ...), kind=kOutput, calls=%fused_computation.39 | convolution fusion | flops 271054720 | bytes 5527040 | tf_op jit(solution)/shard_map/kgtu,ukd->tkgd/dot_general | solution.py:146
  40.3 3.1 %collective-permute-start.2 = (f32[2,128]{1,0:T(2,128)S(1)}, f32[2,128]{1,0:T(2,128)S(1)}, u32[]{:S(2)}, u32[]{:S(2)}) collective-permute-start(f32[2,128]{1,0:T(2,128)S(1)} %pad_maximum_fusion.3), channel_id=1, source_target_pairs={{0,1},{1,0},{2,3},{3,2},{4,5},{5,4},{6,7},{7,6},{8,9},{9,8},{10,11... | collective-permute-start | bytes 3080 | tf_op jit(solution)/shard_map/ppermute | solution.py:24
  44.2 1.4 %collective-permute-start.8 = (bf16[512,2,256]{0,2,1:T(8,128)(2,1)}, bf16[512,2,256]{0,2,1:T(8,128)(2,1)}, u32[]{:S(2)}, u32[]{:S(2)}) collective-permute-start(bf16[512,2,256]{0,2,1:T(8,128)(2,1)} %pad_maximum_fusion.2), channel_id=1, source_target_pairs={{8,0},{12,4},{16,8},{20,12},{24,16},{28,20},{32,24},{36,28},{40,32... | collective-permute-start | bytes 1572872 | tf_op jit(solution)/shard_map/ppermute | solution.py:19
  45.8 6.9 %collective-permute-start.3 = (f32[2,128]{1,0:T(2,128)S(1)}, f32[2,128]{1,0:T(2,128)S(1)}, u32[]{:S(2)}, u32[]{:S(2)}) collective-permute-start(f32[2,128]{1,0:T(2,128)S(1)} %fusion.55), channel_id=1, source_target_pairs={{0,2},{1,3},{2,0},{3,1},{4,6},{5,7},{6,4},{7,5},{8,10},{9,11},{10,... | collective-permute-start | bytes 3080 | tf_op jit(solution)/shard_map/ppermute | solution.py:24
  53.5 1.3 collective-permute-start.7
  54.8 13.1 %collective-permute-start.4 = (f32[2,128]{1,0:T(2,128)S(1)}, f32[2,128]{1,0:T(2,128)S(1)}, u32[]{:S(2)}, u32[]{:S(2)}) collective-permute-start(f32[2,128]{1,0:T(2,128)S(1)} %fusion.84), channel_id=1, source_target_pairs={{0,384},{384,0},{1,385},{385,1},{2,386},{386,2},{3,387},{387,3},{4... | collective-permute-start | bytes 3080 | tf_op jit(solution)/shard_map/ppermute | solution.py:24
  67.9 1.5 %collective-permute-done.4 = f32[2,128]{1,0:T(2,128)S(1)} collective-permute-done((f32[2,128]{1,0:T(2,128)S(1)}, f32[2,128]{1,0:T(2,128)S(1)}, u32[]{:S(2)}, u32[]{:S(2)}) %collective-permute-start.4) | collective-permute-done | bytes 1056 | tf_op jit(solution)/shard_map/ppermute | solution.py:24
  69.4 3.9 %collective-permute-start.5 = (f32[2,128]{1,0:T(2,128)S(1)}, f32[2,128]{1,0:T(2,128)S(1)}, u32[]{:S(2)}, u32[]{:S(2)}) collective-permute-start(f32[2,128]{1,0:T(2,128)S(1)} %add.212), channel_id=1, source_target_pairs={{0,4},{4,0},{8,12},{12,8},{16,20},{20,16},{24,28},{28,24},{32,36},... | collective-permute-start | bytes 3080 | tf_op jit(solution)/shard_map/ppermute | solution.py:24
  74.2 7.4 %collective-permute-start.6 = (f32[2,128]{1,0:T(2,128)S(1)}, f32[2,128]{1,0:T(2,128)S(1)}, u32[]{:S(2)}, u32[]{:S(2)}) collective-permute-start(f32[2,128]{1,0:T(2,128)S(1)} %add.213), channel_id=1, source_target_pairs={{0,8},{4,12},{8,0},{12,4},{16,24},{20,28},{24,16},{28,20},{32,40},... | collective-permute-start | bytes 3080 | tf_op jit(solution)/shard_map/ppermute | solution.py:24
  81.6 2.6 %multiply_convert_fusion = bf16[512,2,2,128]{0,3,2,1:T(8,128)(2,1)} fusion(f32[512,2,2,128]{0,3,2,1:T(8,128)} %get-tuple-element.44, f32[512,2,2,128]{0,3,2,1:T(8,128)} %bitcast.198, f32[512,2,2]{0,2,1:T(2,128)S(1)} %broadcast_multiply_fusion, f32[128]{0:T(128)S(1)} %copy-done.16, f32[512,2,2]{0,2,1:T(2,128)S(1)} %add_rsqrt_fusion), kind=kLoop, calls=%fused_computation.38 | loop fusion | flops 1835008 | bytes 2638336 | tf_op jit(solution)/shard_map/convert_element_type | solution.py:176
  84.3 4.9 %collective-permute-start.9 = (f32[2,128]{1,0:T(2,128)S(1)}, f32[2,128]{1,0:T(2,128)S(1)}, u32[]{:S(2)}, u32[]{:S(2)}) collective-permute-start(f32[2,128]{1,0:T(2,128)S(1)} %add.214), channel_id=1, source_target_pairs={{0,16},{4,20},{8,24},{12,28},{16,0},{20,4},{24,8},{28,12},{32,48},... | collective-permute-start | bytes 3080 | tf_op jit(solution)/shard_map/ppermute | solution.py:24
  89.2 1.2 fusion.35
  90.8 9.3 %collective-permute-start.10 = (f32[2,128]{1,0:T(2,128)S(1)}, f32[2,128]{1,0:T(2,128)S(1)}, u32[]{:S(2)}, u32[]{:S(2)}) collective-permute-start(f32[2,128]{1,0:T(2,128)S(1)} %add.215), channel_id=1, source_target_pairs={{0,32},{4,36},{8,40},{12,44},{16,48},{20,52},{24,56},{28,60},{32,0... | collective-permute-start | bytes 3080 | tf_op jit(solution)/shard_map/ppermute | solution.py:24
  100.0 1.5 %collective-permute-done.10 = f32[2,128]{1,0:T(2,128)S(1)} collective-permute-done((f32[2,128]{1,0:T(2,128)S(1)}, f32[2,128]{1,0:T(2,128)S(1)}, u32[]{:S(2)}, u32[]{:S(2)}) %collective-permute-start.10) | collective-permute-done | bytes 1056 | tf_op jit(solution)/shard_map/ppermute | solution.py:24
  101.6 6.1 %collective-permute-start.11 = (f32[2,128]{1,0:T(2,128)S(1)}, f32[2,128]{1,0:T(2,128)S(1)}, u32[]{:S(2)}, u32[]{:S(2)}) collective-permute-start(f32[2,128]{1,0:T(2,128)S(1)} %add.216), channel_id=1, source_target_pairs={{0,128},{4,132},{8,136},{12,140},{16,144},{20,148},{24,152},{28,15... | collective-permute-start | bytes 3080 | tf_op jit(solution)/shard_map/ppermute | solution.py:36
  107.7 5.7 %collective-permute-start.12 = (f32[2,128]{1,0:T(2,128)S(1)}, f32[2,128]{1,0:T(2,128)S(1)}, u32[]{:S(2)}, u32[]{:S(2)}) collective-permute-start(f32[2,128]{1,0:T(2,128)S(1)} %add.216), channel_id=1, source_target_pairs={{0,64},{4,68},{8,72},{12,76},{16,80},{20,84},{24,88},{28,92},{32,9... | collective-permute-start | bytes 3080 | tf_op jit(solution)/shard_map/ppermute | solution.py:36
  113.4 2.9 %add_convert_fusion = (bf16[512,2,128]{0,2,1:T(8,128)(2,1)}, bf16[512,2,128]{0,2,1:T(8,128)(2,1)}) fusion(bf16[512,2,256]{0,2,1:T(8,128)(2,1)} %collective-permute-done.8, bf16[512,2,256]{0,2,1:T(8,128)(2,1)} %collective-permute-done.7, f32[512,2]{0,1:T(2,128)S(1)} %broadcast_multiply_fusion.1, f32[512,2]{0,1:T(2,128)S(1)} %add_rsqrt_fusion.3, ...), kind=kOutput, calls=%fused_computation.80 | convolution fusion | flops 270532608 | bytes 4989440 | tf_op jit(solution)/shard_map/kgtu,tkgd->ukd/dot_general | solution.py:152
  116.4 8.8 %collective-permute-start.13 = (f32[2,128]{1,0:T(2,128)S(1)}, f32[2,128]{1,0:T(2,128)S(1)}, u32[]{:S(2)}, u32[]{:S(2)}) collective-permute-start(f32[2,128]{1,0:T(2,128)S(1)} %select_add_fusion), channel_id=1, source_target_pairs={{0,192},{4,196},{8,200},{12,204},{16,208},{20,212},{24,216},{28,22... | collective-permute-start | bytes 3080 | tf_op jit(solution)/shard_map/ppermute | solution.py:65
  125.2 2.0 %copy.40 = bf16[1,512,512]{2,1,0:T(8,128)(2,1)} copy(bf16[1,512,512]{1,2,0:T(8,128)(2,1)} %bitcast.210) | data formatting | bytes 1048576
  127.2 1.8 %copy.41 = bf16[1,512,256]{2,1,0:T(8,128)(2,1)} copy(bf16[1,512,256]{1,2,0:T(8,128)(2,1)} %bitcast.212) | data formatting | bytes 524288
  129.0 1.8 %copy.42 = bf16[1,512,256]{2,1,0:T(8,128)(2,1)} copy(bf16[1,512,256]{1,2,0:T(8,128)(2,1)} %bitcast.211) | data formatting | bytes 524288
  (92 shorter events, 17.6 us)
Async XLA Ops:
  0.6 8.3 %copy-start.14 = (bf16[1,512,512]{2,1,0:T(8,128)(2,1)S(1)}, bf16[1,512,512]{2,1,0:T(8,128)(2,1)}, u32[]{:S(2)}) copy-start(bf16[1,512,512]{2,1,0:T(8,128)(2,1)} %param.8) | copy-start | bytes 1572868
  2.9 6.0 %copy-start.3 = (bf16[1,512,256]{1,2,0:T(8,128)(2,1)}, bf16[1,512,256]{1,2,0:T(8,128)(2,1)S(1)}, u32[]{:S(2)}) copy-start(bf16[1,512,256]{1,2,0:T(8,128)(2,1)S(1)} %copy.16) | copy-start | bytes 786436
  2.9 6.4 %copy-start.16 = (f32[128]{0:T(128)S(1)}, f32[128]{0:T(128)}, u32[]{:S(2)}) copy-start(f32[128]{0:T(128)} %param.12) | copy-start | bytes 1540
  3.8 16.1 %collective-permute-start.1 = (bf16[512,2,256]{0,2,1:T(8,128)(2,1)}, bf16[512,2,256]{0,2,1:T(8,128)(2,1)S(1)}, u32[]{:S(2)}, u32[]{:S(2)}) collective-permute-start(bf16[512,2,256]{0,2,1:T(8,128)(2,1)} %pad_maximum_fusion), channel_id=1, source_target_pairs={{0,8},{4,12},{8,16},{12,20},{16,24},{20,28},{24,32},{28,36},{32,40... | collective-permute-start | bytes 1572872 | tf_op jit(solution)/shard_map/ppermute | solution.py:19
  7.3 12.7 %collective-permute-start = (bf16[512,2,256]{0,2,1:T(8,128)(2,1)}, bf16[512,2,256]{0,2,1:T(8,128)(2,1)S(1)}, u32[]{:S(2)}, u32[]{:S(2)}) collective-permute-start(bf16[512,2,256]{0,2,1:T(8,128)(2,1)} %pad_maximum_fusion), channel_id=1, source_target_pairs={{0,4},{4,8},{8,12},{12,16},{16,20},{20,24},{24,28},{28,32},{32,36}... | collective-permute-start | bytes 1572872 | tf_op jit(solution)/shard_map/ppermute | solution.py:19
  9.1 5.2 %copy-start = (f32[1,512,512]{1,2,0:T(8,128)}, f32[1,512,512]{1,2,0:T(8,128)S(1)}, u32[]{:S(2)}) copy-start(f32[1,512,512]{1,2,0:T(8,128)S(1)} %copy.13) | copy-start | bytes 3145732
  9.1 2.2 %copy-start.15 = (f32[128]{0:T(128)S(1)}, f32[128]{0:T(128)}, u32[]{:S(2)}) copy-start(f32[128]{0:T(128)} %param.13) | copy-start | bytes 1540
  11.3 3.0 %copy-start.12 = (pred[512,512]{0,1:T(8,128)(4,1)}, pred[512,512]{0,1:T(8,128)(4,1)S(1)}, u32[]{:S(2)}) copy-start(pred[512,512]{0,1:T(8,128)(4,1)S(1)} %get-tuple-element.35) | copy-start | bytes 786436
  19.9 2.5 %copy-start.8 = (bf16[512,2,256]{0,2,1:T(8,128)(2,1)}, bf16[512,2,256]{0,2,1:T(8,128)(2,1)S(1)}, u32[]{:S(2)}) copy-start(bf16[512,2,256]{0,2,1:T(8,128)(2,1)S(1)} %collective-permute-done.1) | copy-start | bytes 1572868
  20.0 2.4 %copy-start.6 = (bf16[512,2,256]{0,2,1:T(8,128)(2,1)}, bf16[512,2,256]{0,2,1:T(8,128)(2,1)S(1)}, u32[]{:S(2)}) copy-start(bf16[512,2,256]{0,2,1:T(8,128)(2,1)S(1)} %collective-permute-done) | copy-start | bytes 1572868
  20.1 2.3 %copy-start.10 = (pred[512,512]{0,1:T(8,128)(4,1)S(1)}, pred[512,512]{0,1:T(8,128)(4,1)}, u32[]{:S(2)}) copy-start(pred[512,512]{0,1:T(8,128)(4,1)} %get-tuple-element.33) | copy-start | bytes 786436
  22.4 2.2 %copy-start.5 = (f32[2,512,512,2]{2,1,3,0:T(8,128)S(1)}, f32[2,512,512,2]{2,1,3,0:T(8,128)}, u32[]{:S(2)}) copy-start(f32[2,512,512,2]{2,1,3,0:T(8,128)} %get-tuple-element.39) | copy-start | bytes 12582916
  22.4 2.2 %copy-start.11 = (pred[512,512]{0,1:T(8,128)(4,1)S(1)}, pred[512,512]{0,1:T(8,128)(4,1)}, u32[]{:S(2)}) copy-start(pred[512,512]{0,1:T(8,128)(4,1)} %get-tuple-element.34) | copy-start | bytes 786436
  22.4 2.3 %copy-start.13 = (pred[512,512]{0,1:T(8,128)(4,1)S(1)}, pred[512,512]{0,1:T(8,128)(4,1)}, u32[]{:S(2)}) copy-start(pred[512,512]{0,1:T(8,128)(4,1)} %copy-done.12) | copy-start | bytes 786436
  27.7 1.0 copy-start.4
  28.6 1.1 copy-start.9
  29.6 1.0 copy-start.7
  35.6 1.2 copy-start.1
  40.3 5.5 %collective-permute-start.2 = (f32[2,128]{1,0:T(2,128)S(1)}, f32[2,128]{1,0:T(2,128)S(1)}, u32[]{:S(2)}, u32[]{:S(2)}) collective-permute-start(f32[2,128]{1,0:T(2,128)S(1)} %pad_maximum_fusion.3), channel_id=1, source_target_pairs={{0,1},{1,0},{2,3},{3,2},{4,5},{5,4},{6,7},{7,6},{8,9},{9,8},{10,11... | collective-permute-start | bytes 3080 | tf_op jit(solution)/shard_map/ppermute | solution.py:24
  44.2 45.0 %copy-start.2 = (f32[512,2,128]{0,2,1:T(8,128)S(1)}, f32[512,2,128]{0,2,1:T(8,128)}, u32[]{:S(2)}) copy-start(f32[512,2,128]{0,2,1:T(8,128)} %get-tuple-element.43) | copy-start | bytes 1572868
  44.2 40.0 %collective-permute-start.8 = (bf16[512,2,256]{0,2,1:T(8,128)(2,1)}, bf16[512,2,256]{0,2,1:T(8,128)(2,1)}, u32[]{:S(2)}, u32[]{:S(2)}) collective-permute-start(bf16[512,2,256]{0,2,1:T(8,128)(2,1)} %pad_maximum_fusion.2), channel_id=1, source_target_pairs={{8,0},{12,4},{16,8},{20,12},{24,16},{28,20},{32,24},{36,28},{40,32... | collective-permute-start | bytes 1572872 | tf_op jit(solution)/shard_map/ppermute | solution.py:19
  45.8 9.0 %collective-permute-start.3 = (f32[2,128]{1,0:T(2,128)S(1)}, f32[2,128]{1,0:T(2,128)S(1)}, u32[]{:S(2)}, u32[]{:S(2)}) collective-permute-start(f32[2,128]{1,0:T(2,128)S(1)} %fusion.55), channel_id=1, source_target_pairs={{0,2},{1,3},{2,0},{3,1},{4,6},{5,7},{6,4},{7,5},{8,10},{9,11},{10,... | collective-permute-start | bytes 3080 | tf_op jit(solution)/shard_map/ppermute | solution.py:24
  53.5 30.8 %collective-permute-start.7 = (bf16[512,2,256]{0,2,1:T(8,128)(2,1)}, bf16[512,2,256]{0,2,1:T(8,128)(2,1)}, u32[]{:S(2)}, u32[]{:S(2)}) collective-permute-start(bf16[512,2,256]{0,2,1:T(8,128)(2,1)} %pad_maximum_fusion.1), channel_id=1, source_target_pairs={{4,0},{8,4},{12,8},{16,12},{20,16},{24,20},{28,24},{32,28},{36,32}... | collective-permute-start | bytes 1572872 | tf_op jit(solution)/shard_map/ppermute | solution.py:19
  54.8 14.6 %collective-permute-start.4 = (f32[2,128]{1,0:T(2,128)S(1)}, f32[2,128]{1,0:T(2,128)S(1)}, u32[]{:S(2)}, u32[]{:S(2)}) collective-permute-start(f32[2,128]{1,0:T(2,128)S(1)} %fusion.84), channel_id=1, source_target_pairs={{0,384},{384,0},{1,385},{385,1},{2,386},{386,2},{3,387},{387,3},{4... | collective-permute-start | bytes 3080 | tf_op jit(solution)/shard_map/ppermute | solution.py:24
  69.4 4.7 %collective-permute-start.5 = (f32[2,128]{1,0:T(2,128)S(1)}, f32[2,128]{1,0:T(2,128)S(1)}, u32[]{:S(2)}, u32[]{:S(2)}) collective-permute-start(f32[2,128]{1,0:T(2,128)S(1)} %add.212), channel_id=1, source_target_pairs={{0,4},{4,0},{8,12},{12,8},{16,20},{20,16},{24,28},{28,24},{32,36},... | collective-permute-start | bytes 3080 | tf_op jit(solution)/shard_map/ppermute | solution.py:24
  74.2 10.1 %collective-permute-start.6 = (f32[2,128]{1,0:T(2,128)S(1)}, f32[2,128]{1,0:T(2,128)S(1)}, u32[]{:S(2)}, u32[]{:S(2)}) collective-permute-start(f32[2,128]{1,0:T(2,128)S(1)} %add.213), channel_id=1, source_target_pairs={{0,8},{4,12},{8,0},{12,4},{16,24},{20,28},{24,16},{28,20},{32,40},... | collective-permute-start | bytes 3080 | tf_op jit(solution)/shard_map/ppermute | solution.py:24
  84.3 6.5 %collective-permute-start.9 = (f32[2,128]{1,0:T(2,128)S(1)}, f32[2,128]{1,0:T(2,128)S(1)}, u32[]{:S(2)}, u32[]{:S(2)}) collective-permute-start(f32[2,128]{1,0:T(2,128)S(1)} %add.214), channel_id=1, source_target_pairs={{0,16},{4,20},{8,24},{12,28},{16,0},{20,4},{24,8},{28,12},{32,48},... | collective-permute-start | bytes 3080 | tf_op jit(solution)/shard_map/ppermute | solution.py:24
  90.8 10.8 %collective-permute-start.10 = (f32[2,128]{1,0:T(2,128)S(1)}, f32[2,128]{1,0:T(2,128)S(1)}, u32[]{:S(2)}, u32[]{:S(2)}) collective-permute-start(f32[2,128]{1,0:T(2,128)S(1)} %add.215), channel_id=1, source_target_pairs={{0,32},{4,36},{8,40},{12,44},{16,48},{20,52},{24,56},{28,60},{32,0... | collective-permute-start | bytes 3080 | tf_op jit(solution)/shard_map/ppermute | solution.py:24
  101.6 14.8 %collective-permute-start.11 = (f32[2,128]{1,0:T(2,128)S(1)}, f32[2,128]{1,0:T(2,128)S(1)}, u32[]{:S(2)}, u32[]{:S(2)}) collective-permute-start(f32[2,128]{1,0:T(2,128)S(1)} %add.216), channel_id=1, source_target_pairs={{0,128},{4,132},{8,136},{12,140},{16,144},{20,148},{24,152},{28,15... | collective-permute-start | bytes 3080 | tf_op jit(solution)/shard_map/ppermute | solution.py:36
  107.7 8.7 %collective-permute-start.12 = (f32[2,128]{1,0:T(2,128)S(1)}, f32[2,128]{1,0:T(2,128)S(1)}, u32[]{:S(2)}, u32[]{:S(2)}) collective-permute-start(f32[2,128]{1,0:T(2,128)S(1)} %add.216), channel_id=1, source_target_pairs={{0,64},{4,68},{8,72},{12,76},{16,80},{20,84},{24,88},{28,92},{32,9... | collective-permute-start | bytes 3080 | tf_op jit(solution)/shard_map/ppermute | solution.py:36
  116.3 14.5 %copy-start.18 = (f32[2]{0:T(128)S(1)}, f32[2]{0:T(128)}, u32[]{:S(2)}) copy-start(f32[2]{0:T(128)} %constant.83) | copy-start | bytes 28
  116.4 14.4 %collective-permute-start.13 = (f32[2,128]{1,0:T(2,128)S(1)}, f32[2,128]{1,0:T(2,128)S(1)}, u32[]{:S(2)}, u32[]{:S(2)}) collective-permute-start(f32[2,128]{1,0:T(2,128)S(1)} %select_add_fusion), channel_id=1, source_target_pairs={{0,192},{4,196},{8,200},{12,204},{16,208},{20,212},{24,216},{28,22... | collective-permute-start | bytes 3080 | tf_op jit(solution)/shard_map/ppermute | solution.py:65
  (1 other events, 0.7 us)

commit v9 on v8

--- a/solution.py
+++ b/solution.py
@@ -56,10 +56,11 @@
 def middle_rounds(value):
     for stride in (4, 8):
         value = exchanged_sum(value, "ctx", stride)
-    return three_way_sum(value, "ctx", 16)
+    return value
 
 
 def last_round(value):
+    value = three_way_sum(value, "ctx", 16)
     count = lax.axis_size("ctx")
     half = count // 2
     return value + lax.ppermute(value, "ctx", [(source, (source + half) % count) for source in range(count)])

time: 132 us -> 132 us (level)
  starting transfers between devices: 76.9 us -> 75.5 us
  waiting for transfers between devices: 8.6 us -> 9.95 us
    ppermute x2, waiting for transfers between devices: 0.05 us -> 2.94 us  [three_way_sum(): received.append(lax.ppermute(value, axis, pairs))]
    ppermute x7, waiting for transfers between devices: 4.22 us -> 2.69 us  [exchanged_sum(): lax.ppermute(value, axis, [(source, source ^ stride) for source in range(...]
    ppermute x2, starting transfers between devices: 11.8 us -> 10.4 us  [three_way_sum(): received.append(lax.ppermute(value, axis, pairs))]
  transfers between devices with their start and end apart: 14 -> 14, of which waited for: 7 -> 6; matrix products, arithmetic and copies ran while one was open for 16% -> 16% of each run, Pallas kernels for 0% -> 0%
where the time goes in v9:
time: 132 us; the launch traced here: 131 us
  starting transfers between devices  75.5 us (57%)
  matrix products  20.6 us (16%)
  local copies, waits for them, and re-layouts  12.5 us (9%)
  other arithmetic  11.6 us (9%)
  waiting for transfers between devices  9.95 us (8%)
    ppermute x7, starting transfers between devices, exchanged_sum(): lax.ppermute(value, axis, [(source, source ^ stride) for source in range(...  48.6 us
    unnamed x44, local copies, waits for them, and re-layouts  12.3 us
    ppermute x2, starting transfers between devices, three_way_sum(): received.append(lax.ppermute(value, axis, pairs))  10.4 us
    ppermute x1, starting transfers between devices, last_round(): lax.ppermute(value, 'ctx', [(source, (source + half) % count) for source...  8.77 us
    ppermute x4, starting transfers between devices, passed_along(): lax.ppermute(value, axis, [(source, source + steps) for source in range(i...  7.68 us
    dot_general x3, matrix products, forward_block(): jnp.einsum('tkgd,ukd->kgtu', query_n, key_block, preferred_element_type=j...  6.43 us
    dot_general x3, matrix products, shards(): jnp.einsum('kgtu,tkgd->ukd', prob, grads_in, preferred_element_type=jnp.f...  4.52 us
    ppermute x4, waiting for transfers between devices, passed_along(): lax.ppermute(value, axis, [(source, source + steps) for source in range(i...  4.32 us
  transfers between devices with their start and end apart: 14, of which 6 were waited for; matrix products, arithmetic and copies ran while one was open for 16% of the time, Pallas kernels for 0%

profile of v9, /device:TPU:4, one launch (start us, length us, event | category | flops | bytes accessed | tf_op | source)
XLA Modules:
  0.0 131.5 jit_solution(16078426616793247909)
XLA Ops:
  0.6 1.1 copy.12
  3.8 3.5 %collective-permute-start.1 = (bf16[512,2,256]{0,2,1:T(8,128)(2,1)}, bf16[512,2,256]{0,2,1:T(8,128)(2,1)S(1)}, u32[]{:S(2)}, u32[]{:S(2)}) collective-permute-start(bf16[512,2,256]{0,2,1:T(8,128)(2,1)} %pad_maximum_fusion), channel_id=1, source_target_pairs={{0,8},{4,12},{8,16},{12,20},{16,24},{20,28},{24,32},{28,36},{32,40... | collective-permute-start | bytes 1572872 | tf_op jit(solution)/shard_map/ppermute | solution.py:19
  7.3 1.5 %collective-permute-start = (bf16[512,2,256]{0,2,1:T(8,128)(2,1)}, bf16[512,2,256]{0,2,1:T(8,128)(2,1)S(1)}, u32[]{:S(2)}, u32[]{:S(2)}) collective-permute-start(bf16[512,2,256]{0,2,1:T(8,128)(2,1)} %pad_maximum_fusion), channel_id=1, source_target_pairs={{0,4},{4,8},{8,12},{12,16},{16,20},{20,24},{24,28},{28,32},{32,36}... | collective-permute-start | bytes 1572872 | tf_op jit(solution)/shard_map/ppermute | solution.py:19
  9.6 1.7 %fusion.19 = (pred[512,512]{0,1:T(8,128)(4,1)}, pred[512,512]{0,1:T(8,128)(4,1)}, pred[512,512]{0,1:T(8,128)(4,1)S(1)}) fusion(s32[512]{0:T(512)S(1)} %iota_add_fusion.2, s32[512]{0:T(512)S(1)} %bitcast.216, s32[512]{0:T(512)S(1)} %get-tuple-element.46, s32[512]{0:T(512)S(1)} %get-tuple-element.45), kind=kLoop, calls=%fused_computation.48 | loop fusion | flops 4718592 | bytes 794624 | tf_op jit(solution)/shard_map/and | solution.py:109
  11.3 3.0 %fusion.6 = (f32[2,2,512]{2,1,0:T(2,128)S(1)}, f32[2,512,512,2]{2,1,3,0:T(8,128)}) fusion(pred[512,512]{0,1:T(8,128)(4,1)S(1)} %get-tuple-element.35, bf16[512,2,2,128]{0,3,2,1:T(8,128)(2,1)S(1)} %multiply_convert_fusion.1, bf16[512,2,128]{0,2,1:T(8,128)(2,1)S(1)} %bitcast.202, f32[128]{0:T(128)S(1)} %copy-done.15, f32[512,2]{0,1:T(2,128)S(1)} %add_rsqrt_fusion.3), kind=kOutput, calls=%fused_computation.15 | convolution fusion | flops 271054848 | bytes 5255680 | tf_op jit(solution)/shard_map/tkgd,ukd->kgtu/dot_general | solution.py:116
  14.3 1.3 copy.21
  15.5 4.3 %collective-permute-done.1 = bf16[512,2,256]{0,2,1:T(8,128)(2,1)S(1)} collective-permute-done((bf16[512,2,256]{0,2,1:T(8,128)(2,1)}, bf16[512,2,256]{0,2,1:T(8,128)(2,1)S(1)}, u32[]{:S(2)}, u32[]{:S(2)}) %collective-permute-start.1) | collective-permute-done | bytes 524320 | tf_op jit(solution)/shard_map/ppermute | solution.py:19
  20.1 2.3 %fusion.8 = (f32[2,2,512]{2,1,0:T(2,128)S(1)}, f32[2,512,512,2]{2,1,3,0:T(8,128)S(1)}) fusion(pred[512,512]{0,1:T(8,128)(4,1)} %get-tuple-element.34, bf16[512,2,2,128]{0,3,2,1:T(8,128)(2,1)S(1)} %multiply_convert_fusion.1, f32[512,2]{0,1:T(2,128)S(1)} %add_rsqrt_fusion.1, f32[128]{0:T(128)S(1)} %copy-done.15, ...), kind=kOutput, calls=%fused_computation.17 | convolution fusion | flops 271054848 | bytes 5255680 | tf_op jit(solution)/shard_map/tkgd,ukd->kgtu/dot_general | solution.py:116
  22.4 1.2 fusion.7
  24.7 2.2 %divide_convert_fusion.1 = (bf16[2,2,512,512]{2,3,1,0:T(8,128)(2,1)S(1)}, bf16[2,2,512,512]{2,3,1,0:T(8,128)(2,1)S(1)}, bf16[2,2,512,512]{2,3,1,0:T(8,128)(2,1)S(1)}) fusion(f32[2,512,512,2]{2,1,3,0:T(8,128)S(1)} %get-tuple-element.41, f32[2,2,512]{2,1,0:T(2,128)S(1)} %add_add_fusion, pred[512,512]{0,1:T(8,128)(4,1)S(1)} %copy-done.10, ...), kind=kLoop, calls=%fused_computation.13 | loop fusion | flops 9437184 | bytes 19668992 | tf_op jit(solution)/shard_map/convert_element_type | solution.py:125
  32.5 1.6 %fusion.34 = (f32[128]{0:T(128)S(1)}, f32[512,2,128]{0,2,1:T(8,128)}) fusion(bf16[512,2,128]{0,2,1:T(8,128)(2,1)S(1)} %bitcast.204, f32[512,2]{0,1:T(2,128)S(1)} %add_rsqrt_fusion.3, bf16[512,2,2,128]{0,3,2,1:T(8,128)(2,1)S(1)} %multiply_convert_fusion.1, bf16[2,2,512,512]{2,3,1,0:T(8,128)(2,1)S(1)} %fusion.5), kind=kOutput, calls=%fused_computation.69 | convolution fusion | flops 268959616 | bytes 3412480 | tf_op jit(solution)/shard_map/kgtu,tkgd->ukd/dot_general | solution.py:150
  36.8 1.6 %multiply_reduce_fusion = (f32[512,2,2]{0,2,1:T(2,128)S(1)}, f32[128]{0:T(128)S(1)}, f32[512,2,2,128]{0,3,2,1:T(8,128)}) fusion(f32[512,2,2,128]{0,3,2,1:T(8,128)S(1)} %bitcast.199, f32[128]{0:T(128)S(1)} %copy-done.16, f32[512,2,2]{0,2,1:T(2,128)S(1)} %add_rsqrt_fusion, f32[2,128,2,512]{3,1,2,0:T(8,128)S(1)} %convolution_add_fusion.1, ...), kind=kOutput, calls=%fused_computation.39 | convolution fusion | flops 271054720 | bytes 5527040 | tf_op jit(solution)/shard_map/kgtu,ukd->tkgd/dot_general | solution.py:147
  40.3 3.1 %collective-permute-start.2 = (f32[2,128]{1,0:T(2,128)S(1)}, f32[2,128]{1,0:T(2,128)S(1)}, u32[]{:S(2)}, u32[]{:S(2)}) collective-permute-start(f32[2,128]{1,0:T(2,128)S(1)} %pad_maximum_fusion.3), channel_id=1, source_target_pairs={{0,1},{1,0},{2,3},{3,2},{4,5},{5,4},{6,7},{7,6},{8,9},{9,8},{10,11... | collective-permute-start | bytes 3080 | tf_op jit(solution)/shard_map/ppermute | solution.py:24
  44.2 1.4 %collective-permute-start.8 = (bf16[512,2,256]{0,2,1:T(8,128)(2,1)}, bf16[512,2,256]{0,2,1:T(8,128)(2,1)}, u32[]{:S(2)}, u32[]{:S(2)}) collective-permute-start(bf16[512,2,256]{0,2,1:T(8,128)(2,1)} %pad_maximum_fusion.2), channel_id=1, source_target_pairs={{8,0},{12,4},{16,8},{20,12},{24,16},{28,20},{32,24},{36,28},{40,32... | collective-permute-start | bytes 1572872 | tf_op jit(solution)/shard_map/ppermute | solution.py:19
  45.8 6.9 %collective-permute-start.3 = (f32[2,128]{1,0:T(2,128)S(1)}, f32[2,128]{1,0:T(2,128)S(1)}, u32[]{:S(2)}, u32[]{:S(2)}) collective-permute-start(f32[2,128]{1,0:T(2,128)S(1)} %fusion.55), channel_id=1, source_target_pairs={{0,2},{1,3},{2,0},{3,1},{4,6},{5,7},{6,4},{7,5},{8,10},{9,11},{10,... | collective-permute-start | bytes 3080 | tf_op jit(solution)/shard_map/ppermute | solution.py:24
  53.5 1.3 collective-permute-start.7
  54.8 13.1 %collective-permute-start.4 = (f32[2,128]{1,0:T(2,128)S(1)}, f32[2,128]{1,0:T(2,128)S(1)}, u32[]{:S(2)}, u32[]{:S(2)}) collective-permute-start(f32[2,128]{1,0:T(2,128)S(1)} %fusion.84), channel_id=1, source_target_pairs={{0,384},{384,0},{1,385},{385,1},{2,386},{386,2},{3,387},{387,3},{4... | collective-permute-start | bytes 3080 | tf_op jit(solution)/shard_map/ppermute | solution.py:24
  67.9 1.5 %collective-permute-done.4 = f32[2,128]{1,0:T(2,128)S(1)} collective-permute-done((f32[2,128]{1,0:T(2,128)S(1)}, f32[2,128]{1,0:T(2,128)S(1)}, u32[]{:S(2)}, u32[]{:S(2)}) %collective-permute-start.4) | collective-permute-done | bytes 1056 | tf_op jit(solution)/shard_map/ppermute | solution.py:24
  69.4 3.9 %collective-permute-start.5 = (f32[2,128]{1,0:T(2,128)S(1)}, f32[2,128]{1,0:T(2,128)S(1)}, u32[]{:S(2)}, u32[]{:S(2)}) collective-permute-start(f32[2,128]{1,0:T(2,128)S(1)} %add.211), channel_id=1, source_target_pairs={{0,4},{4,0},{8,12},{12,8},{16,20},{20,16},{24,28},{28,24},{32,36},... | collective-permute-start | bytes 3080 | tf_op jit(solution)/shard_map/ppermute | solution.py:24
  74.2 7.4 %collective-permute-start.6 = (f32[2,128]{1,0:T(2,128)S(1)}, f32[2,128]{1,0:T(2,128)S(1)}, u32[]{:S(2)}, u32[]{:S(2)}) collective-permute-start(f32[2,128]{1,0:T(2,128)S(1)} %add.212), channel_id=1, source_target_pairs={{0,8},{4,12},{8,0},{12,4},{16,24},{20,28},{24,16},{28,20},{32,40},... | collective-permute-start | bytes 3080 | tf_op jit(solution)/shard_map/ppermute | solution.py:24
  81.6 2.6 %multiply_convert_fusion = bf16[512,2,2,128]{0,3,2,1:T(8,128)(2,1)} fusion(f32[512,2,2,128]{0,3,2,1:T(8,128)} %get-tuple-element.44, f32[512,2,2,128]{0,3,2,1:T(8,128)} %bitcast.198, f32[512,2,2]{0,2,1:T(2,128)S(1)} %broadcast_multiply_fusion, f32[128]{0:T(128)S(1)} %copy-done.16, f32[512,2,2]{0,2,1:T(2,128)S(1)} %add_rsqrt_fusion), kind=kLoop, calls=%fused_computation.38 | loop fusion | flops 1835008 | bytes 2638336 | tf_op jit(solution)/shard_map/convert_element_type | solution.py:177
  84.3 4.9 %collective-permute-start.9 = (f32[2,128]{1,0:T(2,128)S(1)}, f32[2,128]{1,0:T(2,128)S(1)}, u32[]{:S(2)}, u32[]{:S(2)}) collective-permute-start(f32[2,128]{1,0:T(2,128)S(1)} %add.213), channel_id=1, source_target_pairs={{0,16},{4,20},{8,24},{12,28},{16,0},{20,4},{24,8},{28,12},{32,48},... | collective-permute-start | bytes 3080 | tf_op jit(solution)/shard_map/ppermute | solution.py:24
  89.2 1.2 fusion.35
  90.8 9.3 %collective-permute-start.10 = (f32[2,128]{1,0:T(2,128)S(1)}, f32[2,128]{1,0:T(2,128)S(1)}, u32[]{:S(2)}, u32[]{:S(2)}) collective-permute-start(f32[2,128]{1,0:T(2,128)S(1)} %add.214), channel_id=1, source_target_pairs={{0,32},{4,36},{8,40},{12,44},{16,48},{20,52},{24,56},{28,60},{32,0... | collective-permute-start | bytes 3080 | tf_op jit(solution)/shard_map/ppermute | solution.py:24
  100.0 2.9 %add_convert_fusion = (bf16[512,2,128]{0,2,1:T(8,128)(2,1)}, bf16[512,2,128]{0,2,1:T(8,128)(2,1)}) fusion(bf16[512,2,256]{0,2,1:T(8,128)(2,1)} %collective-permute-done.8, bf16[512,2,256]{0,2,1:T(8,128)(2,1)} %collective-permute-done.7, f32[512,2]{0,1:T(2,128)S(1)} %broadcast_multiply_fusion.1, f32[512,2]{0,1:T(2,128)S(1)} %add_rsqrt_fusion.3, ...), kind=kOutput, calls=%fused_computation.80 | convolution fusion | flops 270532608 | bytes 4989440 | tf_op jit(solution)/shard_map/kgtu,tkgd->ukd/dot_general | solution.py:153
  103.0 4.7 %collective-permute-start.11 = (f32[2,128]{1,0:T(2,128)S(1)}, f32[2,128]{1,0:T(2,128)S(1)}, u32[]{:S(2)}, u32[]{:S(2)}) collective-permute-start(f32[2,128]{1,0:T(2,128)S(1)} %add.215), channel_id=1, source_target_pairs={{0,128},{4,132},{8,136},{12,140},{16,144},{20,148},{24,152},{28,15... | collective-permute-start | bytes 3080 | tf_op jit(solution)/shard_map/ppermute | solution.py:36
  107.7 5.7 %collective-permute-start.12 = (f32[2,128]{1,0:T(2,128)S(1)}, f32[2,128]{1,0:T(2,128)S(1)}, u32[]{:S(2)}, u32[]{:S(2)}) collective-permute-start(f32[2,128]{1,0:T(2,128)S(1)} %add.215), channel_id=1, source_target_pairs={{0,64},{4,68},{8,72},{12,76},{16,80},{20,84},{24,88},{28,92},{32,9... | collective-permute-start | bytes 3080 | tf_op jit(solution)/shard_map/ppermute | solution.py:36
  113.5 2.9 %collective-permute-done.12 = f32[2,128]{1,0:T(2,128)S(1)} collective-permute-done((f32[2,128]{1,0:T(2,128)S(1)}, f32[2,128]{1,0:T(2,128)S(1)}, u32[]{:S(2)}, u32[]{:S(2)}) %collective-permute-start.12) | collective-permute-done | bytes 1056 | tf_op jit(solution)/shard_map/ppermute | solution.py:36
  116.4 8.8 %collective-permute-start.13 = (f32[2,128]{1,0:T(2,128)S(1)}, f32[2,128]{1,0:T(2,128)S(1)}, u32[]{:S(2)}, u32[]{:S(2)}) collective-permute-start(f32[2,128]{1,0:T(2,128)S(1)} %select_add_fusion), channel_id=1, source_target_pairs={{0,192},{4,196},{8,200},{12,204},{16,208},{20,212},{24,216},{28,22... | collective-permute-start | bytes 3080 | tf_op jit(solution)/shard_map/ppermute | solution.py:66
  125.2 2.0 %copy.40 = bf16[1,512,512]{2,1,0:T(8,128)(2,1)} copy(bf16[1,512,512]{1,2,0:T(8,128)(2,1)} %bitcast.210) | data formatting | bytes 1048576
  127.2 1.8 %copy.41 = bf16[1,512,256]{2,1,0:T(8,128)(2,1)} copy(bf16[1,512,256]{1,2,0:T(8,128)(2,1)} %bitcast.212) | data formatting | bytes 524288
  129.0 1.8 %copy.42 = bf16[1,512,256]{2,1,0:T(8,128)(2,1)} copy(bf16[1,512,256]{1,2,0:T(8,128)(2,1)} %bitcast.211) | data formatting | bytes 524288
  (92 shorter events, 17.5 us)
Async XLA Ops:
  0.6 8.3 %copy-start.14 = (bf16[1,512,512]{2,1,0:T(8,128)(2,1)S(1)}, bf16[1,512,512]{2,1,0:T(8,128)(2,1)}, u32[]{:S(2)}) copy-start(bf16[1,512,512]{2,1,0:T(8,128)(2,1)} %param.8) | copy-start | bytes 1572868
  2.9 6.0 %copy-start.3 = (bf16[1,512,256]{1,2,0:T(8,128)(2,1)}, bf16[1,512,256]{1,2,0:T(8,128)(2,1)S(1)}, u32[]{:S(2)}) copy-start(bf16[1,512,256]{1,2,0:T(8,128)(2,1)S(1)} %copy.16) | copy-start | bytes 786436
  2.9 6.4 %copy-start.16 = (f32[128]{0:T(128)S(1)}, f32[128]{0:T(128)}, u32[]{:S(2)}) copy-start(f32[128]{0:T(128)} %param.12) | copy-start | bytes 1540
  3.8 16.1 %collective-permute-start.1 = (bf16[512,2,256]{0,2,1:T(8,128)(2,1)}, bf16[512,2,256]{0,2,1:T(8,128)(2,1)S(1)}, u32[]{:S(2)}, u32[]{:S(2)}) collective-permute-start(bf16[512,2,256]{0,2,1:T(8,128)(2,1)} %pad_maximum_fusion), channel_id=1, source_target_pairs={{0,8},{4,12},{8,16},{12,20},{16,24},{20,28},{24,32},{28,36},{32,40... | collective-permute-start | bytes 1572872 | tf_op jit(solution)/shard_map/ppermute | solution.py:19
  7.3 12.7 %collective-permute-start = (bf16[512,2,256]{0,2,1:T(8,128)(2,1)}, bf16[512,2,256]{0,2,1:T(8,128)(2,1)S(1)}, u32[]{:S(2)}, u32[]{:S(2)}) collective-permute-start(bf16[512,2,256]{0,2,1:T(8,128)(2,1)} %pad_maximum_fusion), channel_id=1, source_target_pairs={{0,4},{4,8},{8,12},{12,16},{16,20},{20,24},{24,28},{28,32},{32,36}... | collective-permute-start | bytes 1572872 | tf_op jit(solution)/shard_map/ppermute | solution.py:19
  9.1 5.2 %copy-start = (f32[1,512,512]{1,2,0:T(8,128)}, f32[1,512,512]{1,2,0:T(8,128)S(1)}, u32[]{:S(2)}) copy-start(f32[1,512,512]{1,2,0:T(8,128)S(1)} %copy.13) | copy-start | bytes 3145732
  9.1 2.2 %copy-start.15 = (f32[128]{0:T(128)S(1)}, f32[128]{0:T(128)}, u32[]{:S(2)}) copy-start(f32[128]{0:T(128)} %param.13) | copy-start | bytes 1540
  11.3 3.0 %copy-start.12 = (pred[512,512]{0,1:T(8,128)(4,1)}, pred[512,512]{0,1:T(8,128)(4,1)S(1)}, u32[]{:S(2)}) copy-start(pred[512,512]{0,1:T(8,128)(4,1)S(1)} %get-tuple-element.35) | copy-start | bytes 786436
  19.9 2.5 %copy-start.8 = (bf16[512,2,256]{0,2,1:T(8,128)(2,1)}, bf16[512,2,256]{0,2,1:T(8,128)(2,1)S(1)}, u32[]{:S(2)}) copy-start(bf16[512,2,256]{0,2,1:T(8,128)(2,1)S(1)} %collective-permute-done.1) | copy-start | bytes 1572868
  20.0 2.4 %copy-start.6 = (bf16[512,2,256]{0,2,1:T(8,128)(2,1)}, bf16[512,2,256]{0,2,1:T(8,128)(2,1)S(1)}, u32[]{:S(2)}) copy-start(bf16[512,2,256]{0,2,1:T(8,128)(2,1)S(1)} %collective-permute-done) | copy-start | bytes 1572868
  20.1 2.3 %copy-start.10 = (pred[512,512]{0,1:T(8,128)(4,1)S(1)}, pred[512,512]{0,1:T(8,128)(4,1)}, u32[]{:S(2)}) copy-start(pred[512,512]{0,1:T(8,128)(4,1)} %get-tuple-element.33) | copy-start | bytes 786436
  22.4 2.2 %copy-start.5 = (f32[2,512,512,2]{2,1,3,0:T(8,128)S(1)}, f32[2,512,512,2]{2,1,3,0:T(8,128)}, u32[]{:S(2)}) copy-start(f32[2,512,512,2]{2,1,3,0:T(8,128)} %get-tuple-element.39) | copy-start | bytes 12582916
  22.4 2.2 %copy-start.11 = (pred[512,512]{0,1:T(8,128)(4,1)S(1)}, pred[512,512]{0,1:T(8,128)(4,1)}, u32[]{:S(2)}) copy-start(pred[512,512]{0,1:T(8,128)(4,1)} %get-tuple-element.34) | copy-start | bytes 786436
  22.4 2.3 %copy-start.13 = (pred[512,512]{0,1:T(8,128)(4,1)S(1)}, pred[512,512]{0,1:T(8,128)(4,1)}, u32[]{:S(2)}) copy-start(pred[512,512]{0,1:T(8,128)(4,1)} %copy-done.12) | copy-start | bytes 786436
  27.7 1.0 copy-start.4
  28.6 1.1 copy-start.9
  29.6 1.0 copy-start.7
  35.6 1.2 copy-start.1
  40.3 5.5 %collective-permute-start.2 = (f32[2,128]{1,0:T(2,128)S(1)}, f32[2,128]{1,0:T(2,128)S(1)}, u32[]{:S(2)}, u32[]{:S(2)}) collective-permute-start(f32[2,128]{1,0:T(2,128)S(1)} %pad_maximum_fusion.3), channel_id=1, source_target_pairs={{0,1},{1,0},{2,3},{3,2},{4,5},{5,4},{6,7},{7,6},{8,9},{9,8},{10,11... | collective-permute-start | bytes 3080 | tf_op jit(solution)/shard_map/ppermute | solution.py:24
  44.2 45.0 %copy-start.2 = (f32[512,2,128]{0,2,1:T(8,128)S(1)}, f32[512,2,128]{0,2,1:T(8,128)}, u32[]{:S(2)}) copy-start(f32[512,2,128]{0,2,1:T(8,128)} %get-tuple-element.43) | copy-start | bytes 1572868
  44.2 40.0 %collective-permute-start.8 = (bf16[512,2,256]{0,2,1:T(8,128)(2,1)}, bf16[512,2,256]{0,2,1:T(8,128)(2,1)}, u32[]{:S(2)}, u32[]{:S(2)}) collective-permute-start(bf16[512,2,256]{0,2,1:T(8,128)(2,1)} %pad_maximum_fusion.2), channel_id=1, source_target_pairs={{8,0},{12,4},{16,8},{20,12},{24,16},{28,20},{32,24},{36,28},{40,32... | collective-permute-start | bytes 1572872 | tf_op jit(solution)/shard_map/ppermute | solution.py:19
  45.8 9.0 %collective-permute-start.3 = (f32[2,128]{1,0:T(2,128)S(1)}, f32[2,128]{1,0:T(2,128)S(1)}, u32[]{:S(2)}, u32[]{:S(2)}) collective-permute-start(f32[2,128]{1,0:T(2,128)S(1)} %fusion.55), channel_id=1, source_target_pairs={{0,2},{1,3},{2,0},{3,1},{4,6},{5,7},{6,4},{7,5},{8,10},{9,11},{10,... | collective-permute-start | bytes 3080 | tf_op jit(solution)/shard_map/ppermute | solution.py:24
  53.5 30.8 %collective-permute-start.7 = (bf16[512,2,256]{0,2,1:T(8,128)(2,1)}, bf16[512,2,256]{0,2,1:T(8,128)(2,1)}, u32[]{:S(2)}, u32[]{:S(2)}) collective-permute-start(bf16[512,2,256]{0,2,1:T(8,128)(2,1)} %pad_maximum_fusion.1), channel_id=1, source_target_pairs={{4,0},{8,4},{12,8},{16,12},{20,16},{24,20},{28,24},{32,28},{36,32}... | collective-permute-start | bytes 1572872 | tf_op jit(solution)/shard_map/ppermute | solution.py:19
  54.8 14.6 %collective-permute-start.4 = (f32[2,128]{1,0:T(2,128)S(1)}, f32[2,128]{1,0:T(2,128)S(1)}, u32[]{:S(2)}, u32[]{:S(2)}) collective-permute-start(f32[2,128]{1,0:T(2,128)S(1)} %fusion.84), channel_id=1, source_target_pairs={{0,384},{384,0},{1,385},{385,1},{2,386},{386,2},{3,387},{387,3},{4... | collective-permute-start | bytes 3080 | tf_op jit(solution)/shard_map/ppermute | solution.py:24
  69.4 4.7 %collective-permute-start.5 = (f32[2,128]{1,0:T(2,128)S(1)}, f32[2,128]{1,0:T(2,128)S(1)}, u32[]{:S(2)}, u32[]{:S(2)}) collective-permute-start(f32[2,128]{1,0:T(2,128)S(1)} %add.211), channel_id=1, source_target_pairs={{0,4},{4,0},{8,12},{12,8},{16,20},{20,16},{24,28},{28,24},{32,36},... | collective-permute-start | bytes 3080 | tf_op jit(solution)/shard_map/ppermute | solution.py:24
  74.2 10.1 %collective-permute-start.6 = (f32[2,128]{1,0:T(2,128)S(1)}, f32[2,128]{1,0:T(2,128)S(1)}, u32[]{:S(2)}, u32[]{:S(2)}) collective-permute-start(f32[2,128]{1,0:T(2,128)S(1)} %add.212), channel_id=1, source_target_pairs={{0,8},{4,12},{8,0},{12,4},{16,24},{20,28},{24,16},{28,20},{32,40},... | collective-permute-start | bytes 3080 | tf_op jit(solution)/shard_map/ppermute | solution.py:24
  84.3 6.5 %collective-permute-start.9 = (f32[2,128]{1,0:T(2,128)S(1)}, f32[2,128]{1,0:T(2,128)S(1)}, u32[]{:S(2)}, u32[]{:S(2)}) collective-permute-start(f32[2,128]{1,0:T(2,128)S(1)} %add.213), channel_id=1, source_target_pairs={{0,16},{4,20},{8,24},{12,28},{16,0},{20,4},{24,8},{28,12},{32,48},... | collective-permute-start | bytes 3080 | tf_op jit(solution)/shard_map/ppermute | solution.py:24
  90.8 12.2 %collective-permute-start.10 = (f32[2,128]{1,0:T(2,128)S(1)}, f32[2,128]{1,0:T(2,128)S(1)}, u32[]{:S(2)}, u32[]{:S(2)}) collective-permute-start(f32[2,128]{1,0:T(2,128)S(1)} %add.214), channel_id=1, source_target_pairs={{0,32},{4,36},{8,40},{12,44},{16,48},{20,52},{24,56},{28,60},{32,0... | collective-permute-start | bytes 3080 | tf_op jit(solution)/shard_map/ppermute | solution.py:24
  102.9 27.9 %copy-start.18 = (f32[2]{0:T(128)S(1)}, f32[2]{0:T(128)}, u32[]{:S(2)}) copy-start(f32[2]{0:T(128)} %constant.83) | copy-start | bytes 28
  103.0 10.5 %collective-permute-start.11 = (f32[2,128]{1,0:T(2,128)S(1)}, f32[2,128]{1,0:T(2,128)S(1)}, u32[]{:S(2)}, u32[]{:S(2)}) collective-permute-start(f32[2,128]{1,0:T(2,128)S(1)} %add.215), channel_id=1, source_target_pairs={{0,128},{4,132},{8,136},{12,140},{16,144},{20,148},{24,152},{28,15... | collective-permute-start | bytes 3080 | tf_op jit(solution)/shard_map/ppermute | solution.py:36
  107.7 8.7 %collective-permute-start.12 = (f32[2,128]{1,0:T(2,128)S(1)}, f32[2,128]{1,0:T(2,128)S(1)}, u32[]{:S(2)}, u32[]{:S(2)}) collective-permute-start(f32[2,128]{1,0:T(2,128)S(1)} %add.215), channel_id=1, source_target_pairs={{0,64},{4,68},{8,72},{12,76},{16,80},{20,84},{24,88},{28,92},{32,9... | collective-permute-start | bytes 3080 | tf_op jit(solution)/shard_map/ppermute | solution.py:36
  116.4 14.4 %collective-permute-start.13 = (f32[2,128]{1,0:T(2,128)S(1)}, f32[2,128]{1,0:T(2,128)S(1)}, u32[]{:S(2)}, u32[]{:S(2)}) collective-permute-start(f32[2,128]{1,0:T(2,128)S(1)} %select_add_fusion), channel_id=1, source_target_pairs={{0,192},{4,196},{8,200},{12,204},{16,208},{20,212},{24,216},{28,22... | collective-permute-start | bytes 3080 | tf_op jit(solution)/shard_map/ppermute | solution.py:66
  (1 other events, 0.7 us)

commit v10 on v9

--- a/solution.py
+++ b/solution.py
@@ -48,22 +48,20 @@
     value = exchanged_sum(value, "fsdp", 1)
     value = exchanged_sum(value, "fsdp", 2)
     value = exchanged_sum(value, "dp", 1)
-    for stride in (1, 2):
-        value = exchanged_sum(value, "ctx", stride)
-    return value
-
-
-def middle_rounds(value):
-    for stride in (4, 8):
-        value = exchanged_sum(value, "ctx", stride)
-    return value
-
-
-def last_round(value):
     value = three_way_sum(value, "ctx", 16)
     count = lax.axis_size("ctx")
     half = count // 2
     return value + lax.ppermute(value, "ctx", [(source, (source + half) % count) for source in range(count)])
+
+
+def middle_rounds(value):
+    for stride in (1, 2, 4):
+        value = exchanged_sum(value, "ctx", stride)
+    return value
+
+
+def last_round(value):
+    return exchanged_sum(value, "ctx", 8)
 
 
 def normalize(raw, gain, factor):

time: 132 us -> 126 us (0.955)
  the two profiles are of different devices: /device:TPU:4 before, /device:TPU:2 now
where the time goes in v10:
time: 126 us; the launch traced here: 125 us
  starting transfers between devices  63.3 us (50%)
  waiting for transfers between devices  25 us (20%)
  matrix products  20.8 us (17%)
  local copies, waits for them, and re-layouts  7.61 us (6%)
  other arithmetic  7.5 us (6%)
    ppermute x7, starting transfers between devices, exchanged_sum(): lax.ppermute(value, axis, [(source, source ^ stride) for source in range(...  28.8 us
    ppermute x2, starting transfers between devices, three_way_sum(): received.append(lax.ppermute(value, axis, pairs))  17.4 us
    ppermute x7, waiting for transfers between devices, exchanged_sum(): lax.ppermute(value, axis, [(source, source ^ stride) for source in range(...  17.1 us
    ppermute x1, starting transfers between devices, first_rounds(): lax.ppermute(value, 'ctx', [(source, (source + half) % count) for source...  8.79 us
    ppermute x4, starting transfers between devices, passed_along(): lax.ppermute(value, axis, [(source, source + steps) for source in range(i...  8.33 us
    unnamed x24, local copies, waits for them, and re-layouts  7.4 us
    dot_general x3, matrix products, forward_block(): jnp.einsum('tkgd,ukd->kgtu', query_n, key_block, preferred_element_type=j...  6.3 us
    ppermute x4, waiting for transfers between devices, passed_along(): lax.ppermute(value, axis, [(source, source + steps) for source in range(i...  3.69 us
  transfers between devices with their start and end apart: 14, of which 10 were waited for; matrix products, arithmetic and copies ran while one was open for 10% of the time, Pallas kernels for 0%

profile of v10, /device:TPU:2, one launch (start us, length us, event | category | flops | bytes accessed | tf_op | source)
XLA Modules:
  0.0 125.2 jit_solution(2423209756124994176)
XLA Ops:
  0.6 1.1 copy.12
  3.7 4.3 %collective-permute-start.1 = (bf16[512,2,256]{0,2,1:T(8,128)(2,1)}, bf16[512,2,256]{0,2,1:T(8,128)(2,1)}, u32[]{:S(2)}, u32[]{:S(2)}) collective-permute-start(bf16[512,2,256]{0,2,1:T(8,128)(2,1)} %pad_maximum_fusion), channel_id=1, source_target_pairs={{0,8},{4,12},{8,16},{12,20},{16,24},{20,28},{24,32},{28,36},{32,40... | collective-permute-start | bytes 1572872 | tf_op jit(solution)/shard_map/ppermute | solution.py:19
  8.0 1.5 %collective-permute-start = (bf16[512,2,256]{0,2,1:T(8,128)(2,1)}, bf16[512,2,256]{0,2,1:T(8,128)(2,1)S(1)}, u32[]{:S(2)}, u32[]{:S(2)}) collective-permute-start(bf16[512,2,256]{0,2,1:T(8,128)(2,1)} %pad_maximum_fusion), channel_id=1, source_target_pairs={{0,4},{4,8},{8,12},{12,16},{16,20},{20,24},{24,28},{28,32},{32,36}... | collective-permute-start | bytes 1572872 | tf_op jit(solution)/shard_map/ppermute | solution.py:19
  10.3 1.6 %fusion.19 = (pred[512,512]{0,1:T(8,128)(4,1)S(1)}, pred[512,512]{0,1:T(8,128)(4,1)}, pred[512,512]{0,1:T(8,128)(4,1)S(1)}) fusion(s32[512]{0:T(512)S(1)} %iota_add_fusion.2, s32[512]{0:T(512)S(1)} %bitcast.216, s32[512]{0:T(512)S(1)} %get-tuple-element.46, s32[512]{0:T(512)S(1)} %get-tuple-element.45), kind=kLoop, calls=%fused_computation.48 | loop fusion | flops 4718592 | bytes 794624 | tf_op jit(solution)/shard_map/and | solution.py:107
  11.9 3.0 %fusion.6 = (f32[2,2,512]{2,1,0:T(2,128)S(1)}, f32[2,512,512,2]{2,1,3,0:T(8,128)}) fusion(pred[512,512]{0,1:T(8,128)(4,1)S(1)} %get-tuple-element.35, bf16[512,2,2,128]{0,3,2,1:T(8,128)(2,1)S(1)} %multiply_convert_fusion.1, bf16[512,2,128]{0,2,1:T(8,128)(2,1)S(1)} %bitcast.202, f32[128]{0:T(128)S(1)} %copy-done.5, f32[512,2]{0,1:T(2,128)S(1)} %add_rsqrt_fusion.3), kind=kOutput, calls=%fused_computation.15 | convolution fusion | flops 271054848 | bytes 5255680 | tf_op jit(solution)/shard_map/tkgd,ukd->kgtu/dot_general | solution.py:114
  14.9 1.3 %copy.21 = bf16[1,512,512]{1,2,0:T(8,128)(2,1)S(1)} copy(bf16[1,512,512]{2,1,0:T(8,128)(2,1)} %param.11) | data formatting | bytes 1048576 | tf_op args[3]
  16.1 3.7 %collective-permute-done.1 = bf16[512,2,256]{0,2,1:T(8,128)(2,1)} collective-permute-done((bf16[512,2,256]{0,2,1:T(8,128)(2,1)}, bf16[512,2,256]{0,2,1:T(8,128)(2,1)}, u32[]{:S(2)}, u32[]{:S(2)}) %collective-permute-start.1) | collective-permute-done | bytes 524320 | tf_op jit(solution)/shard_map/ppermute | solution.py:19
  21.0 2.2 %fusion.8 = (f32[2,2,512]{2,1,0:T(2,128)S(1)}, f32[2,512,512,2]{2,1,3,0:T(8,128)S(1)}) fusion(pred[512,512]{0,1:T(8,128)(4,1)} %get-tuple-element.34, bf16[512,2,2,128]{0,3,2,1:T(8,128)(2,1)S(1)} %multiply_convert_fusion.1, f32[512,2]{0,1:T(2,128)S(1)} %add_rsqrt_fusion.1, f32[128]{0:T(128)S(1)} %copy-done.5, bf16[512,2,256]{0,2,1:T(8,128)(2,1)} %collective-permute-done.1), kind=kOutput, calls=%fused_computation.17 | convolution fusion | flops 271054848 | bytes 5255680 | tf_op jit(solution)/shard_map/tkgd,ukd->kgtu/dot_general | solution.py:114
  23.2 1.2 fusion.7
  25.4 2.2 %divide_convert_fusion.1 = (bf16[2,2,512,512]{2,3,1,0:T(8,128)(2,1)S(1)}, bf16[2,2,512,512]{2,3,1,0:T(8,128)(2,1)S(1)}, bf16[2,2,512,512]{2,3,1,0:T(8,128)(2,1)S(1)}) fusion(f32[2,512,512,2]{2,1,3,0:T(8,128)S(1)} %get-tuple-element.41, f32[2,2,512]{2,1,0:T(2,128)S(1)} %add_add_fusion, pred[512,512]{0,1:T(8,128)(4,1)S(1)} %get-tuple-element.33, ...), kind=kLoop, calls=%fused_computation.13 | loop fusion | flops 9437184 | bytes 19668992 | tf_op jit(solution)/shard_map/convert_element_type | solution.py:123
  28.9 1.4 %convolution_bitcast_fusion.1 = f32[512,2,2,128]{0,3,2,1:T(8,128)S(1)} fusion(bf16[2,2,512,512]{2,3,1,0:T(8,128)(2,1)S(1)} %get-tuple-element.31, bf16[512,2,256]{0,2,1:T(8,128)(2,1)} %collective-permute-done.1), kind=kOutput, calls=%fused_computation.19 | convolution fusion | flops 268435456 | bytes 3407872 | tf_op jit(solution)/shard_map/kgtu,ukd->tkgd/dot_general | solution.py:129
  33.1 1.7 %fusion.1 = bf16[2,2,512,512]{2,3,1,0:T(8,128)(2,1)S(1)} fusion(bf16[2,2,512,512]{2,3,1,0:T(8,128)(2,1)S(1)} %get-tuple-element.31, bf16[512,2,2,128]{0,3,2,1:T(8,128)(2,1)S(1)} %bitcast.192, f32[2,2,512]{2,1,0:T(2,128)S(1)} %bitcast.214, bf16[512,2,256]{0,2,1:T(8,128)(2,1)} %collective-permute-done.1), kind=kOutput, calls=%fused_computation.2 | convolution fusion | flops 272629760 | bytes 4988928 | tf_op jit(solution)/shard_map/tkgd,ukd->kgtu/dot_general | solution.py:141
  36.0 1.7 %multiply_reduce_fusion = (f32[512,2,2]{0,2,1:T(2,128)S(1)}, f32[128]{0:T(128)S(1)}, f32[512,2,2,128]{0,3,2,1:T(8,128)S(1)}) fusion(f32[512,2,2,128]{0,3,2,1:T(8,128)S(1)} %bitcast.198, f32[128]{0:T(128)S(1)} %copy-done.6, f32[512,2,2]{0,2,1:T(2,128)S(1)} %add_rsqrt_fusion, f32[2,128,2,512]{3,1,2,0:T(8,128)S(1)} %convolution_add_fusion.1, ...), kind=kOutput, calls=%fused_computation.39 | convolution fusion | flops 271054720 | bytes 5527040 | tf_op jit(solution)/shard_map/kgtu,ukd->tkgd/dot_general | solution.py:145
  37.7 1.8 %fusion.56 = (bf16[512,2,128]{0,2,1:T(8,128)(2,1)S(1)}, f32[128]{0:T(128)S(1)}) fusion(f32[512,2]{0,1:T(2,128)S(1)} %add_rsqrt_fusion.1, bf16[512,2,256]{0,2,1:T(8,128)(2,1)} %collective-permute-done.1, bf16[512,2,2,128]{0,3,2,1:T(8,128)(2,1)S(1)} %multiply_convert_fusion.1, bf16[2,2,512,512]{2,3,1,0:T(8,128)(2,1)S(1)} %fusion.1), kind=kOutput, calls=%fused_computation.107 | convolution fusion | flops 269090688 | bytes 3150336 | tf_op jit(solution)/shard_map/kgtu,tkgd->ukd/dot_general | solution.py:148
  40.5 7.1 %collective-permute-start.2 = (f32[2,128]{1,0:T(2,128)S(1)}, f32[2,128]{1,0:T(2,128)S(1)}, u32[]{:S(2)}, u32[]{:S(2)}) collective-permute-start(f32[2,128]{1,0:T(2,128)S(1)} %pad_maximum_fusion.3), channel_id=1, source_target_pairs={{0,1},{1,0},{2,3},{3,2},{4,5},{5,4},{6,7},{7,6},{8,9},{9,8},{10,11... | collective-permute-start | bytes 3080 | tf_op jit(solution)/shard_map/ppermute | solution.py:24
  49.0 1.9 %collective-permute-start.3 = (f32[2,128]{1,0:T(2,128)S(1)}, f32[2,128]{1,0:T(2,128)S(1)}, u32[]{:S(2)}, u32[]{:S(2)}) collective-permute-start(f32[2,128]{1,0:T(2,128)S(1)} %fusion.55), channel_id=1, source_target_pairs={{0,2},{1,3},{2,0},{3,1},{4,6},{5,7},{6,4},{7,5},{8,10},{9,11},{10,... | collective-permute-start | bytes 3080 | tf_op jit(solution)/shard_map/ppermute | solution.py:24
  50.9 1.3 %collective-permute-start.9 = (bf16[512,2,256]{0,2,1:T(8,128)(2,1)S(1)}, bf16[512,2,256]{0,2,1:T(8,128)(2,1)S(1)}, u32[]{:S(2)}, u32[]{:S(2)}) collective-permute-start(bf16[512,2,256]{0,2,1:T(8,128)(2,1)S(1)} %pad_maximum_fusion.2), channel_id=1, source_target_pairs={{8,0},{12,4},{16,8},{20,12},{24,16},{28,20},{32,24},{36,28},{40,32... | collective-permute-start | bytes 1572872 | tf_op jit(solution)/shard_map/ppermute | solution.py:19
  52.2 3.7 %collective-permute-done.3 = f32[2,128]{1,0:T(2,128)S(1)} collective-permute-done((f32[2,128]{1,0:T(2,128)S(1)}, f32[2,128]{1,0:T(2,128)S(1)}, u32[]{:S(2)}, u32[]{:S(2)}) %collective-permute-start.3) | collective-permute-done | bytes 1056 | tf_op jit(solution)/shard_map/ppermute | solution.py:24
  55.9 12.1 %collective-permute-start.4 = (f32[2,128]{1,0:T(2,128)S(1)}, f32[2,128]{1,0:T(2,128)S(1)}, u32[]{:S(2)}, u32[]{:S(2)}) collective-permute-start(f32[2,128]{1,0:T(2,128)S(1)} %fusion.84), channel_id=1, source_target_pairs={{0,384},{384,0},{1,385},{385,1},{2,386},{386,2},{3,387},{387,3},{4... | collective-permute-start | bytes 3080 | tf_op jit(solution)/shard_map/ppermute | solution.py:24
  68.1 1.3 %collective-permute-start.8 = (bf16[512,2,256]{0,2,1:T(8,128)(2,1)S(1)}, bf16[512,2,256]{0,2,1:T(8,128)(2,1)S(1)}, u32[]{:S(2)}, u32[]{:S(2)}) collective-permute-start(bf16[512,2,256]{0,2,1:T(8,128)(2,1)S(1)} %pad_maximum_fusion.1), channel_id=1, source_target_pairs={{4,0},{8,4},{12,8},{16,12},{20,16},{24,20},{28,24},{32,28},{36,32}... | collective-permute-start | bytes 1572872 | tf_op jit(solution)/shard_map/ppermute | solution.py:19
  69.6 12.1 %collective-permute-start.5 = (f32[2,128]{1,0:T(2,128)S(1)}, f32[2,128]{1,0:T(2,128)S(1)}, u32[]{:S(2)}, u32[]{:S(2)}) collective-permute-start(f32[2,128]{1,0:T(2,128)S(1)} %add.212), channel_id=1, source_target_pairs={{0,128},{4,132},{8,136},{12,140},{16,144},{20,148},{24,152},{28,15... | collective-permute-start | bytes 3080 | tf_op jit(solution)/shard_map/ppermute | solution.py:36
  81.7 5.3 %collective-permute-start.6 = (f32[2,128]{1,0:T(2,128)S(1)}, f32[2,128]{1,0:T(2,128)S(1)}, u32[]{:S(2)}, u32[]{:S(2)}) collective-permute-start(f32[2,128]{1,0:T(2,128)S(1)} %add.212), channel_id=1, source_target_pairs={{0,64},{4,68},{8,72},{12,76},{16,80},{20,84},{24,88},{28,92},{32,9... | collective-permute-start | bytes 3080 | tf_op jit(solution)/shard_map/ppermute | solution.py:36
  87.0 3.0 %collective-permute-done.6 = f32[2,128]{1,0:T(2,128)S(1)} collective-permute-done((f32[2,128]{1,0:T(2,128)S(1)}, f32[2,128]{1,0:T(2,128)S(1)}, u32[]{:S(2)}, u32[]{:S(2)}) %collective-permute-start.6) | collective-permute-done | bytes 1056 | tf_op jit(solution)/shard_map/ppermute | solution.py:36
  90.0 8.8 %collective-permute-start.7 = (f32[2,128]{1,0:T(2,128)S(1)}, f32[2,128]{1,0:T(2,128)S(1)}, u32[]{:S(2)}, u32[]{:S(2)}) collective-permute-start(f32[2,128]{1,0:T(2,128)S(1)} %select_add_fusion), channel_id=1, source_target_pairs={{0,192},{4,196},{8,200},{12,204},{16,208},{20,212},{24,216},{28,22... | collective-permute-start | bytes 3080 | tf_op jit(solution)/shard_map/ppermute | solution.py:54
  99.1 1.2 collective-permute-done.7
  100.3 1.9 %collective-permute-start.10 = (f32[2,128]{1,0:T(2,128)S(1)}, f32[2,128]{1,0:T(2,128)S(1)}, u32[]{:S(2)}, u32[]{:S(2)}) collective-permute-start(f32[2,128]{1,0:T(2,128)S(1)} %add.217), channel_id=1, source_target_pairs={{0,4},{4,0},{8,12},{12,8},{16,20},{20,16},{24,28},{28,24},{32,36},... | collective-permute-start | bytes 3080 | tf_op jit(solution)/shard_map/ppermute | solution.py:24
  103.4 1.9 %collective-permute-start.11 = (f32[2,128]{1,0:T(2,128)S(1)}, f32[2,128]{1,0:T(2,128)S(1)}, u32[]{:S(2)}, u32[]{:S(2)}) collective-permute-start(f32[2,128]{1,0:T(2,128)S(1)} %add.218), channel_id=1, source_target_pairs={{0,8},{4,12},{8,0},{12,4},{16,24},{20,28},{24,16},{28,20},{32,40},... | collective-permute-start | bytes 3080 | tf_op jit(solution)/shard_map/ppermute | solution.py:24
  105.3 3.5 %collective-permute-done.11 = f32[2,128]{1,0:T(2,128)S(1)} collective-permute-done((f32[2,128]{1,0:T(2,128)S(1)}, f32[2,128]{1,0:T(2,128)S(1)}, u32[]{:S(2)}, u32[]{:S(2)}) %collective-permute-start.11) | collective-permute-done | bytes 1056 | tf_op jit(solution)/shard_map/ppermute | solution.py:24
  108.9 1.9 %collective-permute-start.12 = (f32[2,128]{1,0:T(2,128)S(1)}, f32[2,128]{1,0:T(2,128)S(1)}, u32[]{:S(2)}, u32[]{:S(2)}) collective-permute-start(f32[2,128]{1,0:T(2,128)S(1)} %add.219), channel_id=1, source_target_pairs={{0,16},{4,20},{8,24},{12,28},{16,0},{20,4},{24,8},{28,12},{32,48},... | collective-permute-start | bytes 3080 | tf_op jit(solution)/shard_map/ppermute | solution.py:24
  111.8 3.5 %collective-permute-done.12 = f32[2,128]{1,0:T(2,128)S(1)} collective-permute-done((f32[2,128]{1,0:T(2,128)S(1)}, f32[2,128]{1,0:T(2,128)S(1)}, u32[]{:S(2)}, u32[]{:S(2)}) %collective-permute-start.12) | collective-permute-done | bytes 1056 | tf_op jit(solution)/shard_map/ppermute | solution.py:24
  115.2 1.9 %collective-permute-start.13 = (f32[2,128]{1,0:T(2,128)S(1)}, f32[2,128]{1,0:T(2,128)S(1)}, u32[]{:S(2)}, u32[]{:S(2)}) collective-permute-start(f32[2,128]{1,0:T(2,128)S(1)} %add.220), channel_id=1, source_target_pairs={{0,32},{4,36},{8,40},{12,44},{16,48},{20,52},{24,56},{28,60},{32,0... | collective-permute-start | bytes 3080 | tf_op jit(solution)/shard_map/ppermute | solution.py:24
  119.8 4.8 %collective-permute-done.13 = f32[2,128]{1,0:T(2,128)S(1)} collective-permute-done((f32[2,128]{1,0:T(2,128)S(1)}, f32[2,128]{1,0:T(2,128)S(1)}, u32[]{:S(2)}, u32[]{:S(2)}) %collective-permute-start.13) | collective-permute-done | bytes 1056 | tf_op jit(solution)/shard_map/ppermute | solution.py:24
  (72 shorter events, 18.4 us)
Async XLA Ops:
  0.6 9.0 %copy-start.4 = (bf16[1,512,512]{2,1,0:T(8,128)(2,1)S(1)}, bf16[1,512,512]{2,1,0:T(8,128)(2,1)}, u32[]{:S(2)}) copy-start(bf16[1,512,512]{2,1,0:T(8,128)(2,1)} %param.8) | copy-start | bytes 1572868
  2.9 7.1 %copy-start.6 = (f32[128]{0:T(128)S(1)}, f32[128]{0:T(128)}, u32[]{:S(2)}) copy-start(f32[128]{0:T(128)} %param.12) | copy-start | bytes 1540
  3.7 16.1 %collective-permute-start.1 = (bf16[512,2,256]{0,2,1:T(8,128)(2,1)}, bf16[512,2,256]{0,2,1:T(8,128)(2,1)}, u32[]{:S(2)}, u32[]{:S(2)}) collective-permute-start(bf16[512,2,256]{0,2,1:T(8,128)(2,1)} %pad_maximum_fusion), channel_id=1, source_target_pairs={{0,8},{4,12},{8,16},{12,20},{16,24},{20,28},{24,32},{28,36},{32,40... | collective-permute-start | bytes 1572872 | tf_op jit(solution)/shard_map/ppermute | solution.py:19
  8.0 12.9 %collective-permute-start = (bf16[512,2,256]{0,2,1:T(8,128)(2,1)}, bf16[512,2,256]{0,2,1:T(8,128)(2,1)S(1)}, u32[]{:S(2)}, u32[]{:S(2)}) collective-permute-start(bf16[512,2,256]{0,2,1:T(8,128)(2,1)} %pad_maximum_fusion), channel_id=1, source_target_pairs={{0,4},{4,8},{8,12},{12,16},{16,20},{20,24},{24,28},{28,32},{32,36}... | collective-permute-start | bytes 1572872 | tf_op jit(solution)/shard_map/ppermute | solution.py:19
  9.6 0.7 copy-start.7
  9.8 2.1 %copy-start.5 = (f32[128]{0:T(128)S(1)}, f32[128]{0:T(128)}, u32[]{:S(2)}) copy-start(f32[128]{0:T(128)} %param.13) | copy-start | bytes 1540
  11.9 3.0 %copy-start.2 = (pred[512,512]{0,1:T(8,128)(4,1)}, pred[512,512]{0,1:T(8,128)(4,1)S(1)}, u32[]{:S(2)}) copy-start(pred[512,512]{0,1:T(8,128)(4,1)S(1)} %get-tuple-element.35) | copy-start | bytes 786436
  23.1 2.2 %copy-start = (f32[2,512,512,2]{2,1,3,0:T(8,128)S(1)}, f32[2,512,512,2]{2,1,3,0:T(8,128)}, u32[]{:S(2)}) copy-start(f32[2,512,512,2]{2,1,3,0:T(8,128)} %get-tuple-element.39) | copy-start | bytes 12582916
  23.2 2.2 %copy-start.1 = (pred[512,512]{0,1:T(8,128)(4,1)S(1)}, pred[512,512]{0,1:T(8,128)(4,1)}, u32[]{:S(2)}) copy-start(pred[512,512]{0,1:T(8,128)(4,1)} %get-tuple-element.34) | copy-start | bytes 786436
  23.2 2.3 %copy-start.3 = (pred[512,512]{0,1:T(8,128)(4,1)S(1)}, pred[512,512]{0,1:T(8,128)(4,1)}, u32[]{:S(2)}) copy-start(pred[512,512]{0,1:T(8,128)(4,1)} %copy-done.2) | copy-start | bytes 786436
  40.5 8.5 %collective-permute-start.2 = (f32[2,128]{1,0:T(2,128)S(1)}, f32[2,128]{1,0:T(2,128)S(1)}, u32[]{:S(2)}, u32[]{:S(2)}) collective-permute-start(f32[2,128]{1,0:T(2,128)S(1)} %pad_maximum_fusion.3), channel_id=1, source_target_pairs={{0,1},{1,0},{2,3},{3,2},{4,5},{5,4},{6,7},{7,6},{8,9},{9,8},{10,11... | collective-permute-start | bytes 3080 | tf_op jit(solution)/shard_map/ppermute | solution.py:24
  49.0 7.0 %collective-permute-start.3 = (f32[2,128]{1,0:T(2,128)S(1)}, f32[2,128]{1,0:T(2,128)S(1)}, u32[]{:S(2)}, u32[]{:S(2)}) collective-permute-start(f32[2,128]{1,0:T(2,128)S(1)} %fusion.55), channel_id=1, source_target_pairs={{0,2},{1,3},{2,0},{3,1},{4,6},{5,7},{6,4},{7,5},{8,10},{9,11},{10,... | collective-permute-start | bytes 3080 | tf_op jit(solution)/shard_map/ppermute | solution.py:24
  50.9 49.4 %collective-permute-start.9 = (bf16[512,2,256]{0,2,1:T(8,128)(2,1)S(1)}, bf16[512,2,256]{0,2,1:T(8,128)(2,1)S(1)}, u32[]{:S(2)}, u32[]{:S(2)}) collective-permute-start(bf16[512,2,256]{0,2,1:T(8,128)(2,1)S(1)} %pad_maximum_fusion.2), channel_id=1, source_target_pairs={{8,0},{12,4},{16,8},{20,12},{24,16},{28,20},{32,24},{36,28},{40,32... | collective-permute-start | bytes 1572872 | tf_op jit(solution)/shard_map/ppermute | solution.py:19
  55.9 13.7 %collective-permute-start.4 = (f32[2,128]{1,0:T(2,128)S(1)}, f32[2,128]{1,0:T(2,128)S(1)}, u32[]{:S(2)}, u32[]{:S(2)}) collective-permute-start(f32[2,128]{1,0:T(2,128)S(1)} %fusion.84), channel_id=1, source_target_pairs={{0,384},{384,0},{1,385},{385,1},{2,386},{386,2},{3,387},{387,3},{4... | collective-permute-start | bytes 3080 | tf_op jit(solution)/shard_map/ppermute | solution.py:24
  68.1 32.2 %collective-permute-start.8 = (bf16[512,2,256]{0,2,1:T(8,128)(2,1)S(1)}, bf16[512,2,256]{0,2,1:T(8,128)(2,1)S(1)}, u32[]{:S(2)}, u32[]{:S(2)}) collective-permute-start(bf16[512,2,256]{0,2,1:T(8,128)(2,1)S(1)} %pad_maximum_fusion.1), channel_id=1, source_target_pairs={{4,0},{8,4},{12,8},{16,12},{20,16},{24,20},{28,24},{32,28},{36,32}... | collective-permute-start | bytes 1572872 | tf_op jit(solution)/shard_map/ppermute | solution.py:19
  69.6 17.4 %collective-permute-start.5 = (f32[2,128]{1,0:T(2,128)S(1)}, f32[2,128]{1,0:T(2,128)S(1)}, u32[]{:S(2)}, u32[]{:S(2)}) collective-permute-start(f32[2,128]{1,0:T(2,128)S(1)} %add.212), channel_id=1, source_target_pairs={{0,128},{4,132},{8,136},{12,140},{16,144},{20,148},{24,152},{28,15... | collective-permute-start | bytes 3080 | tf_op jit(solution)/shard_map/ppermute | solution.py:36
  81.7 8.3 %collective-permute-start.6 = (f32[2,128]{1,0:T(2,128)S(1)}, f32[2,128]{1,0:T(2,128)S(1)}, u32[]{:S(2)}, u32[]{:S(2)}) collective-permute-start(f32[2,128]{1,0:T(2,128)S(1)} %add.212), channel_id=1, source_target_pairs={{0,64},{4,68},{8,72},{12,76},{16,80},{20,84},{24,88},{28,92},{32,9... | collective-permute-start | bytes 3080 | tf_op jit(solution)/shard_map/ppermute | solution.py:36
  90.0 10.3 %collective-permute-start.7 = (f32[2,128]{1,0:T(2,128)S(1)}, f32[2,128]{1,0:T(2,128)S(1)}, u32[]{:S(2)}, u32[]{:S(2)}) collective-permute-start(f32[2,128]{1,0:T(2,128)S(1)} %select_add_fusion), channel_id=1, source_target_pairs={{0,192},{4,196},{8,200},{12,204},{16,208},{20,212},{24,216},{28,22... | collective-permute-start | bytes 3080 | tf_op jit(solution)/shard_map/ppermute | solution.py:54
  100.3 3.1 %collective-permute-start.10 = (f32[2,128]{1,0:T(2,128)S(1)}, f32[2,128]{1,0:T(2,128)S(1)}, u32[]{:S(2)}, u32[]{:S(2)}) collective-permute-start(f32[2,128]{1,0:T(2,128)S(1)} %add.217), channel_id=1, source_target_pairs={{0,4},{4,0},{8,12},{12,8},{16,20},{20,16},{24,28},{28,24},{32,36},... | collective-permute-start | bytes 3080 | tf_op jit(solution)/shard_map/ppermute | solution.py:24
  103.4 5.5 %collective-permute-start.11 = (f32[2,128]{1,0:T(2,128)S(1)}, f32[2,128]{1,0:T(2,128)S(1)}, u32[]{:S(2)}, u32[]{:S(2)}) collective-permute-start(f32[2,128]{1,0:T(2,128)S(1)} %add.218), channel_id=1, source_target_pairs={{0,8},{4,12},{8,0},{12,4},{16,24},{20,28},{24,16},{28,20},{32,40},... | collective-permute-start | bytes 3080 | tf_op jit(solution)/shard_map/ppermute | solution.py:24
  108.9 6.4 %collective-permute-start.12 = (f32[2,128]{1,0:T(2,128)S(1)}, f32[2,128]{1,0:T(2,128)S(1)}, u32[]{:S(2)}, u32[]{:S(2)}) collective-permute-start(f32[2,128]{1,0:T(2,128)S(1)} %add.219), channel_id=1, source_target_pairs={{0,16},{4,20},{8,24},{12,28},{16,0},{20,4},{24,8},{28,12},{32,48},... | collective-permute-start | bytes 3080 | tf_op jit(solution)/shard_map/ppermute | solution.py:24
  111.7 12.8 %copy-start.8 = (f32[2]{0:T(128)S(1)}, f32[2]{0:T(128)}, u32[]{:S(2)}) copy-start(f32[2]{0:T(128)} %constant.83) | copy-start | bytes 28
  115.2 9.4 %collective-permute-start.13 = (f32[2,128]{1,0:T(2,128)S(1)}, f32[2,128]{1,0:T(2,128)S(1)}, u32[]{:S(2)}, u32[]{:S(2)}) collective-permute-start(f32[2,128]{1,0:T(2,128)S(1)} %add.220), channel_id=1, source_target_pairs={{0,32},{4,36},{8,40},{12,44},{16,48},{20,52},{24,56},{28,60},{32,0... | collective-permute-start | bytes 3080 | tf_op jit(solution)/shard_map/ppermute | solution.py:24

commit v11 on v10

--- a/solution.py
+++ b/solution.py
@@ -55,13 +55,13 @@
 
 
 def middle_rounds(value):
-    for stride in (1, 2, 4):
+    return exchanged_sum(value, "ctx", 1)
+
+
+def last_round(value):
+    for stride in (2, 4, 8):
         value = exchanged_sum(value, "ctx", stride)
     return value
-
-
-def last_round(value):
-    return exchanged_sum(value, "ctx", 8)
 
 
 def normalize(raw, gain, factor):

time: 126 us -> 126 us (level)
  no operation moved by 1% of the time
where the time goes in v11:
time: 126 us; the launch traced here: 125 us
  starting transfers between devices  63.3 us (50%)
  waiting for transfers between devices  25.2 us (20%)
  matrix products  20.8 us (17%)
  local copies, waits for them, and re-layouts  7.61 us (6%)
  other arithmetic  7.5 us (6%)
    ppermute x7, starting transfers between devices, exchanged_sum(): lax.ppermute(value, axis, [(source, source ^ stride) for source in range(...  28.8 us
    ppermute x2, starting transfers between devices, three_way_sum(): received.append(lax.ppermute(value, axis, pairs))  17.4 us
    ppermute x7, waiting for transfers between devices, exchanged_sum(): lax.ppermute(value, axis, [(source, source ^ stride) for source in range(...  17.3 us
    ppermute x1, starting transfers between devices, first_rounds(): lax.ppermute(value, 'ctx', [(source, (source + half) % count) for source...  8.79 us
    ppermute x4, starting transfers between devices, passed_along(): lax.ppermute(value, axis, [(source, source + steps) for source in range(i...  8.33 us
    unnamed x24, local copies, waits for them, and re-layouts  7.4 us
    dot_general x3, matrix products, forward_block(): jnp.einsum('tkgd,ukd->kgtu', query_n, key_block, preferred_element_type=j...  6.3 us
    ppermute x4, waiting for transfers between devices, passed_along(): lax.ppermute(value, axis, [(source, source + steps) for source in range(i...  3.69 us
  transfers between devices with their start and end apart: 14, of which 10 were waited for; matrix products, arithmetic and copies ran while one was open for 10% of the time, Pallas kernels for 0%

profile of v11, /device:TPU:2, one launch (start us, length us, event | category | flops | bytes accessed | tf_op | source)
XLA Modules:
  0.0 125.4 jit_solution(11060174815961569002)
XLA Ops:
  0.6 1.1 copy.12
  3.7 4.3 %collective-permute-start.1 = (bf16[512,2,256]{0,2,1:T(8,128)(2,1)}, bf16[512,2,256]{0,2,1:T(8,128)(2,1)}, u32[]{:S(2)}, u32[]{:S(2)}) collective-permute-start(bf16[512,2,256]{0,2,1:T(8,128)(2,1)} %pad_maximum_fusion), channel_id=1, source_target_pairs={{0,8},{4,12},{8,16},{12,20},{16,24},{20,28},{24,32},{28,36},{32,40... | collective-permute-start | bytes 1572872 | tf_op jit(solution)/shard_map/ppermute | solution.py:19
  8.0 1.5 %collective-permute-start = (bf16[512,2,256]{0,2,1:T(8,128)(2,1)}, bf16[512,2,256]{0,2,1:T(8,128)(2,1)S(1)}, u32[]{:S(2)}, u32[]{:S(2)}) collective-permute-start(bf16[512,2,256]{0,2,1:T(8,128)(2,1)} %pad_maximum_fusion), channel_id=1, source_target_pairs={{0,4},{4,8},{8,12},{12,16},{16,20},{20,24},{24,28},{28,32},{32,36}... | collective-permute-start | bytes 1572872 | tf_op jit(solution)/shard_map/ppermute | solution.py:19
  10.3 1.6 %fusion.19 = (pred[512,512]{0,1:T(8,128)(4,1)S(1)}, pred[512,512]{0,1:T(8,128)(4,1)}, pred[512,512]{0,1:T(8,128)(4,1)S(1)}) fusion(s32[512]{0:T(512)S(1)} %iota_add_fusion.2, s32[512]{0:T(512)S(1)} %bitcast.216, s32[512]{0:T(512)S(1)} %get-tuple-element.46, s32[512]{0:T(512)S(1)} %get-tuple-element.45), kind=kLoop, calls=%fused_computation.48 | loop fusion | flops 4718592 | bytes 794624 | tf_op jit(solution)/shard_map/and | solution.py:107
  11.9 3.0 %fusion.6 = (f32[2,2,512]{2,1,0:T(2,128)S(1)}, f32[2,512,512,2]{2,1,3,0:T(8,128)}) fusion(pred[512,512]{0,1:T(8,128)(4,1)S(1)} %get-tuple-element.35, bf16[512,2,2,128]{0,3,2,1:T(8,128)(2,1)S(1)} %multiply_convert_fusion.1, bf16[512,2,128]{0,2,1:T(8,128)(2,1)S(1)} %bitcast.202, f32[128]{0:T(128)S(1)} %copy-done.5, f32[512,2]{0,1:T(2,128)S(1)} %add_rsqrt_fusion.3), kind=kOutput, calls=%fused_computation.15 | convolution fusion | flops 271054848 | bytes 5255680 | tf_op jit(solution)/shard_map/tkgd,ukd->kgtu/dot_general | solution.py:114
  14.9 1.3 copy.21
  16.1 3.7 %collective-permute-done.1 = bf16[512,2,256]{0,2,1:T(8,128)(2,1)} collective-permute-done((bf16[512,2,256]{0,2,1:T(8,128)(2,1)}, bf16[512,2,256]{0,2,1:T(8,128)(2,1)}, u32[]{:S(2)}, u32[]{:S(2)}) %collective-permute-start.1) | collective-permute-done | bytes 524320 | tf_op jit(solution)/shard_map/ppermute | solution.py:19
  21.0 2.2 %fusion.8 = (f32[2,2,512]{2,1,0:T(2,128)S(1)}, f32[2,512,512,2]{2,1,3,0:T(8,128)S(1)}) fusion(pred[512,512]{0,1:T(8,128)(4,1)} %get-tuple-element.34, bf16[512,2,2,128]{0,3,2,1:T(8,128)(2,1)S(1)} %multiply_convert_fusion.1, f32[512,2]{0,1:T(2,128)S(1)} %add_rsqrt_fusion.1, f32[128]{0:T(128)S(1)} %copy-done.5, bf16[512,2,256]{0,2,1:T(8,128)(2,1)} %collective-permute-done.1), kind=kOutput, calls=%fused_computation.17 | convolution fusion | flops 271054848 | bytes 5255680 | tf_op jit(solution)/shard_map/tkgd,ukd->kgtu/dot_general | solution.py:114
  23.2 1.2 fusion.7
  25.4 2.2 %divide_convert_fusion.1 = (bf16[2,2,512,512]{2,3,1,0:T(8,128)(2,1)S(1)}, bf16[2,2,512,512]{2,3,1,0:T(8,128)(2,1)S(1)}, bf16[2,2,512,512]{2,3,1,0:T(8,128)(2,1)S(1)}) fusion(f32[2,512,512,2]{2,1,3,0:T(8,128)S(1)} %get-tuple-element.41, f32[2,2,512]{2,1,0:T(2,128)S(1)} %add_add_fusion, pred[512,512]{0,1:T(8,128)(4,1)S(1)} %get-tuple-element.33, ...), kind=kLoop, calls=%fused_computation.13 | loop fusion | flops 9437184 | bytes 19668992 | tf_op jit(solution)/shard_map/convert_element_type | solution.py:123
  28.9 1.4 %convolution_bitcast_fusion.1 = f32[512,2,2,128]{0,3,2,1:T(8,128)S(1)} fusion(bf16[2,2,512,512]{2,3,1,0:T(8,128)(2,1)S(1)} %get-tuple-element.31, bf16[512,2,256]{0,2,1:T(8,128)(2,1)} %collective-permute-done.1), kind=kOutput, calls=%fused_computation.19 | convolution fusion | flops 268435456 | bytes 3407872 | tf_op jit(solution)/shard_map/kgtu,ukd->tkgd/dot_general | solution.py:129
  33.1 1.7 %fusion.1 = bf16[2,2,512,512]{2,3,1,0:T(8,128)(2,1)S(1)} fusion(bf16[2,2,512,512]{2,3,1,0:T(8,128)(2,1)S(1)} %get-tuple-element.31, bf16[512,2,2,128]{0,3,2,1:T(8,128)(2,1)S(1)} %bitcast.192, f32[2,2,512]{2,1,0:T(2,128)S(1)} %bitcast.214, bf16[512,2,256]{0,2,1:T(8,128)(2,1)} %collective-permute-done.1), kind=kOutput, calls=%fused_computation.2 | convolution fusion | flops 272629760 | bytes 4988928 | tf_op jit(solution)/shard_map/tkgd,ukd->kgtu/dot_general | solution.py:141
  36.0 1.7 %multiply_reduce_fusion = (f32[512,2,2]{0,2,1:T(2,128)S(1)}, f32[128]{0:T(128)S(1)}, f32[512,2,2,128]{0,3,2,1:T(8,128)S(1)}) fusion(f32[512,2,2,128]{0,3,2,1:T(8,128)S(1)} %bitcast.198, f32[128]{0:T(128)S(1)} %copy-done.6, f32[512,2,2]{0,2,1:T(2,128)S(1)} %add_rsqrt_fusion, f32[2,128,2,512]{3,1,2,0:T(8,128)S(1)} %convolution_add_fusion.1, ...), kind=kOutput, calls=%fused_computation.39 | convolution fusion | flops 271054720 | bytes 5527040 | tf_op jit(solution)/shard_map/kgtu,ukd->tkgd/dot_general | solution.py:145
  37.7 1.8 %fusion.56 = (bf16[512,2,128]{0,2,1:T(8,128)(2,1)S(1)}, f32[128]{0:T(128)S(1)}) fusion(f32[512,2]{0,1:T(2,128)S(1)} %add_rsqrt_fusion.1, bf16[512,2,256]{0,2,1:T(8,128)(2,1)} %collective-permute-done.1, bf16[512,2,2,128]{0,3,2,1:T(8,128)(2,1)S(1)} %multiply_convert_fusion.1, bf16[2,2,512,512]{2,3,1,0:T(8,128)(2,1)S(1)} %fusion.1), kind=kOutput, calls=%fused_computation.107 | convolution fusion | flops 269090688 | bytes 3150336 | tf_op jit(solution)/shard_map/kgtu,tkgd->ukd/dot_general | solution.py:148
  40.5 7.1 %collective-permute-start.2 = (f32[2,128]{1,0:T(2,128)S(1)}, f32[2,128]{1,0:T(2,128)S(1)}, u32[]{:S(2)}, u32[]{:S(2)}) collective-permute-start(f32[2,128]{1,0:T(2,128)S(1)} %pad_maximum_fusion.3), channel_id=1, source_target_pairs={{0,1},{1,0},{2,3},{3,2},{4,5},{5,4},{6,7},{7,6},{8,9},{9,8},{10,11... | collective-permute-start | bytes 3080 | tf_op jit(solution)/shard_map/ppermute | solution.py:24
  49.0 1.9 %collective-permute-start.3 = (f32[2,128]{1,0:T(2,128)S(1)}, f32[2,128]{1,0:T(2,128)S(1)}, u32[]{:S(2)}, u32[]{:S(2)}) collective-permute-start(f32[2,128]{1,0:T(2,128)S(1)} %fusion.55), channel_id=1, source_target_pairs={{0,2},{1,3},{2,0},{3,1},{4,6},{5,7},{6,4},{7,5},{8,10},{9,11},{10,... | collective-permute-start | bytes 3080 | tf_op jit(solution)/shard_map/ppermute | solution.py:24
  50.9 1.3 %collective-permute-start.9 = (bf16[512,2,256]{0,2,1:T(8,128)(2,1)S(1)}, bf16[512,2,256]{0,2,1:T(8,128)(2,1)S(1)}, u32[]{:S(2)}, u32[]{:S(2)}) collective-permute-start(bf16[512,2,256]{0,2,1:T(8,128)(2,1)S(1)} %pad_maximum_fusion.2), channel_id=1, source_target_pairs={{8,0},{12,4},{16,8},{20,12},{24,16},{28,20},{32,24},{36,28},{40,32... | collective-permute-start | bytes 1572872 | tf_op jit(solution)/shard_map/ppermute | solution.py:19
  52.2 3.7 %collective-permute-done.3 = f32[2,128]{1,0:T(2,128)S(1)} collective-permute-done((f32[2,128]{1,0:T(2,128)S(1)}, f32[2,128]{1,0:T(2,128)S(1)}, u32[]{:S(2)}, u32[]{:S(2)}) %collective-permute-start.3) | collective-permute-done | bytes 1056 | tf_op jit(solution)/shard_map/ppermute | solution.py:24
  55.9 12.1 %collective-permute-start.4 = (f32[2,128]{1,0:T(2,128)S(1)}, f32[2,128]{1,0:T(2,128)S(1)}, u32[]{:S(2)}, u32[]{:S(2)}) collective-permute-start(f32[2,128]{1,0:T(2,128)S(1)} %fusion.84), channel_id=1, source_target_pairs={{0,384},{384,0},{1,385},{385,1},{2,386},{386,2},{3,387},{387,3},{4... | collective-permute-start | bytes 3080 | tf_op jit(solution)/shard_map/ppermute | solution.py:24
  68.1 1.3 %collective-permute-start.8 = (bf16[512,2,256]{0,2,1:T(8,128)(2,1)S(1)}, bf16[512,2,256]{0,2,1:T(8,128)(2,1)S(1)}, u32[]{:S(2)}, u32[]{:S(2)}) collective-permute-start(bf16[512,2,256]{0,2,1:T(8,128)(2,1)S(1)} %pad_maximum_fusion.1), channel_id=1, source_target_pairs={{4,0},{8,4},{12,8},{16,12},{20,16},{24,20},{28,24},{32,28},{36,32}... | collective-permute-start | bytes 1572872 | tf_op jit(solution)/shard_map/ppermute | solution.py:19
  69.6 12.1 %collective-permute-start.5 = (f32[2,128]{1,0:T(2,128)S(1)}, f32[2,128]{1,0:T(2,128)S(1)}, u32[]{:S(2)}, u32[]{:S(2)}) collective-permute-start(f32[2,128]{1,0:T(2,128)S(1)} %add.212), channel_id=1, source_target_pairs={{0,128},{4,132},{8,136},{12,140},{16,144},{20,148},{24,152},{28,15... | collective-permute-start | bytes 3080 | tf_op jit(solution)/shard_map/ppermute | solution.py:36
  81.7 5.3 %collective-permute-start.6 = (f32[2,128]{1,0:T(2,128)S(1)}, f32[2,128]{1,0:T(2,128)S(1)}, u32[]{:S(2)}, u32[]{:S(2)}) collective-permute-start(f32[2,128]{1,0:T(2,128)S(1)} %add.212), channel_id=1, source_target_pairs={{0,64},{4,68},{8,72},{12,76},{16,80},{20,84},{24,88},{28,92},{32,9... | collective-permute-start | bytes 3080 | tf_op jit(solution)/shard_map/ppermute | solution.py:36
  87.0 3.0 %collective-permute-done.6 = f32[2,128]{1,0:T(2,128)S(1)} collective-permute-done((f32[2,128]{1,0:T(2,128)S(1)}, f32[2,128]{1,0:T(2,128)S(1)}, u32[]{:S(2)}, u32[]{:S(2)}) %collective-permute-start.6) | collective-permute-done | bytes 1056 | tf_op jit(solution)/shard_map/ppermute | solution.py:36
  90.0 8.8 %collective-permute-start.7 = (f32[2,128]{1,0:T(2,128)S(1)}, f32[2,128]{1,0:T(2,128)S(1)}, u32[]{:S(2)}, u32[]{:S(2)}) collective-permute-start(f32[2,128]{1,0:T(2,128)S(1)} %select_add_fusion), channel_id=1, source_target_pairs={{0,192},{4,196},{8,200},{12,204},{16,208},{20,212},{24,216},{28,22... | collective-permute-start | bytes 3080 | tf_op jit(solution)/shard_map/ppermute | solution.py:54
  99.1 1.2 collective-permute-done.7
  100.5 1.9 %collective-permute-start.10 = (f32[2,128]{1,0:T(2,128)S(1)}, f32[2,128]{1,0:T(2,128)S(1)}, u32[]{:S(2)}, u32[]{:S(2)}) collective-permute-start(f32[2,128]{1,0:T(2,128)S(1)} %add.217), channel_id=1, source_target_pairs={{0,4},{4,0},{8,12},{12,8},{16,20},{20,16},{24,28},{28,24},{32,36},... | collective-permute-start | bytes 3080 | tf_op jit(solution)/shard_map/ppermute | solution.py:24
  103.6 1.9 %collective-permute-start.11 = (f32[2,128]{1,0:T(2,128)S(1)}, f32[2,128]{1,0:T(2,128)S(1)}, u32[]{:S(2)}, u32[]{:S(2)}) collective-permute-start(f32[2,128]{1,0:T(2,128)S(1)} %add.218), channel_id=1, source_target_pairs={{0,8},{4,12},{8,0},{12,4},{16,24},{20,28},{24,16},{28,20},{32,40},... | collective-permute-start | bytes 3080 | tf_op jit(solution)/shard_map/ppermute | solution.py:24
  105.5 3.5 %collective-permute-done.11 = f32[2,128]{1,0:T(2,128)S(1)} collective-permute-done((f32[2,128]{1,0:T(2,128)S(1)}, f32[2,128]{1,0:T(2,128)S(1)}, u32[]{:S(2)}, u32[]{:S(2)}) %collective-permute-start.11) | collective-permute-done | bytes 1056 | tf_op jit(solution)/shard_map/ppermute | solution.py:24
  109.1 1.9 %collective-permute-start.12 = (f32[2,128]{1,0:T(2,128)S(1)}, f32[2,128]{1,0:T(2,128)S(1)}, u32[]{:S(2)}, u32[]{:S(2)}) collective-permute-start(f32[2,128]{1,0:T(2,128)S(1)} %add.223), channel_id=1, source_target_pairs={{0,16},{4,20},{8,24},{12,28},{16,0},{20,4},{24,8},{28,12},{32,48},... | collective-permute-start | bytes 3080 | tf_op jit(solution)/shard_map/ppermute | solution.py:24
  111.0 4.4 %collective-permute-done.12 = f32[2,128]{1,0:T(2,128)S(1)} collective-permute-done((f32[2,128]{1,0:T(2,128)S(1)}, f32[2,128]{1,0:T(2,128)S(1)}, u32[]{:S(2)}, u32[]{:S(2)}) %collective-permute-start.12) | collective-permute-done | bytes 1056 | tf_op jit(solution)/shard_map/ppermute | solution.py:24
  115.4 1.9 %collective-permute-start.13 = (f32[2,128]{1,0:T(2,128)S(1)}, f32[2,128]{1,0:T(2,128)S(1)}, u32[]{:S(2)}, u32[]{:S(2)}) collective-permute-start(f32[2,128]{1,0:T(2,128)S(1)} %add.224), channel_id=1, source_target_pairs={{0,32},{4,36},{8,40},{12,44},{16,48},{20,52},{24,56},{28,60},{32,0... | collective-permute-start | bytes 3080 | tf_op jit(solution)/shard_map/ppermute | solution.py:24
  120.0 4.8 %collective-permute-done.13 = f32[2,128]{1,0:T(2,128)S(1)} collective-permute-done((f32[2,128]{1,0:T(2,128)S(1)}, f32[2,128]{1,0:T(2,128)S(1)}, u32[]{:S(2)}, u32[]{:S(2)}) %collective-permute-start.13) | collective-permute-done | bytes 1056 | tf_op jit(solution)/shard_map/ppermute | solution.py:24
  (72 shorter events, 17.6 us)
Async XLA Ops:
  0.6 9.0 %copy-start.4 = (bf16[1,512,512]{2,1,0:T(8,128)(2,1)S(1)}, bf16[1,512,512]{2,1,0:T(8,128)(2,1)}, u32[]{:S(2)}) copy-start(bf16[1,512,512]{2,1,0:T(8,128)(2,1)} %param.8) | copy-start | bytes 1572868
  2.9 7.1 %copy-start.6 = (f32[128]{0:T(128)S(1)}, f32[128]{0:T(128)}, u32[]{:S(2)}) copy-start(f32[128]{0:T(128)} %param.12) | copy-start | bytes 1540
  3.7 16.1 %collective-permute-start.1 = (bf16[512,2,256]{0,2,1:T(8,128)(2,1)}, bf16[512,2,256]{0,2,1:T(8,128)(2,1)}, u32[]{:S(2)}, u32[]{:S(2)}) collective-permute-start(bf16[512,2,256]{0,2,1:T(8,128)(2,1)} %pad_maximum_fusion), channel_id=1, source_target_pairs={{0,8},{4,12},{8,16},{12,20},{16,24},{20,28},{24,32},{28,36},{32,40... | collective-permute-start | bytes 1572872 | tf_op jit(solution)/shard_map/ppermute | solution.py:19
  8.0 12.9 %collective-permute-start = (bf16[512,2,256]{0,2,1:T(8,128)(2,1)}, bf16[512,2,256]{0,2,1:T(8,128)(2,1)S(1)}, u32[]{:S(2)}, u32[]{:S(2)}) collective-permute-start(bf16[512,2,256]{0,2,1:T(8,128)(2,1)} %pad_maximum_fusion), channel_id=1, source_target_pairs={{0,4},{4,8},{8,12},{12,16},{16,20},{20,24},{24,28},{28,32},{32,36}... | collective-permute-start | bytes 1572872 | tf_op jit(solution)/shard_map/ppermute | solution.py:19
  9.6 0.7 copy-start.7
  9.8 2.1 %copy-start.5 = (f32[128]{0:T(128)S(1)}, f32[128]{0:T(128)}, u32[]{:S(2)}) copy-start(f32[128]{0:T(128)} %param.13) | copy-start | bytes 1540
  11.9 3.0 %copy-start.2 = (pred[512,512]{0,1:T(8,128)(4,1)}, pred[512,512]{0,1:T(8,128)(4,1)S(1)}, u32[]{:S(2)}) copy-start(pred[512,512]{0,1:T(8,128)(4,1)S(1)} %get-tuple-element.35) | copy-start | bytes 786436
  23.1 2.2 %copy-start = (f32[2,512,512,2]{2,1,3,0:T(8,128)S(1)}, f32[2,512,512,2]{2,1,3,0:T(8,128)}, u32[]{:S(2)}) copy-start(f32[2,512,512,2]{2,1,3,0:T(8,128)} %get-tuple-element.39) | copy-start | bytes 12582916
  23.2 2.2 %copy-start.1 = (pred[512,512]{0,1:T(8,128)(4,1)S(1)}, pred[512,512]{0,1:T(8,128)(4,1)}, u32[]{:S(2)}) copy-start(pred[512,512]{0,1:T(8,128)(4,1)} %get-tuple-element.34) | copy-start | bytes 786436
  23.2 2.3 %copy-start.3 = (pred[512,512]{0,1:T(8,128)(4,1)S(1)}, pred[512,512]{0,1:T(8,128)(4,1)}, u32[]{:S(2)}) copy-start(pred[512,512]{0,1:T(8,128)(4,1)} %copy-done.2) | copy-start | bytes 786436
  40.5 8.5 %collective-permute-start.2 = (f32[2,128]{1,0:T(2,128)S(1)}, f32[2,128]{1,0:T(2,128)S(1)}, u32[]{:S(2)}, u32[]{:S(2)}) collective-permute-start(f32[2,128]{1,0:T(2,128)S(1)} %pad_maximum_fusion.3), channel_id=1, source_target_pairs={{0,1},{1,0},{2,3},{3,2},{4,5},{5,4},{6,7},{7,6},{8,9},{9,8},{10,11... | collective-permute-start | bytes 3080 | tf_op jit(solution)/shard_map/ppermute | solution.py:24
  49.0 7.0 %collective-permute-start.3 = (f32[2,128]{1,0:T(2,128)S(1)}, f32[2,128]{1,0:T(2,128)S(1)}, u32[]{:S(2)}, u32[]{:S(2)}) collective-permute-start(f32[2,128]{1,0:T(2,128)S(1)} %fusion.55), channel_id=1, source_target_pairs={{0,2},{1,3},{2,0},{3,1},{4,6},{5,7},{6,4},{7,5},{8,10},{9,11},{10,... | collective-permute-start | bytes 3080 | tf_op jit(solution)/shard_map/ppermute | solution.py:24
  50.9 49.4 %collective-permute-start.9 = (bf16[512,2,256]{0,2,1:T(8,128)(2,1)S(1)}, bf16[512,2,256]{0,2,1:T(8,128)(2,1)S(1)}, u32[]{:S(2)}, u32[]{:S(2)}) collective-permute-start(bf16[512,2,256]{0,2,1:T(8,128)(2,1)S(1)} %pad_maximum_fusion.2), channel_id=1, source_target_pairs={{8,0},{12,4},{16,8},{20,12},{24,16},{28,20},{32,24},{36,28},{40,32... | collective-permute-start | bytes 1572872 | tf_op jit(solution)/shard_map/ppermute | solution.py:19
  55.9 13.7 %collective-permute-start.4 = (f32[2,128]{1,0:T(2,128)S(1)}, f32[2,128]{1,0:T(2,128)S(1)}, u32[]{:S(2)}, u32[]{:S(2)}) collective-permute-start(f32[2,128]{1,0:T(2,128)S(1)} %fusion.84), channel_id=1, source_target_pairs={{0,384},{384,0},{1,385},{385,1},{2,386},{386,2},{3,387},{387,3},{4... | collective-permute-start | bytes 3080 | tf_op jit(solution)/shard_map/ppermute | solution.py:24
  68.1 32.2 %collective-permute-start.8 = (bf16[512,2,256]{0,2,1:T(8,128)(2,1)S(1)}, bf16[512,2,256]{0,2,1:T(8,128)(2,1)S(1)}, u32[]{:S(2)}, u32[]{:S(2)}) collective-permute-start(bf16[512,2,256]{0,2,1:T(8,128)(2,1)S(1)} %pad_maximum_fusion.1), channel_id=1, source_target_pairs={{4,0},{8,4},{12,8},{16,12},{20,16},{24,20},{28,24},{32,28},{36,32}... | collective-permute-start | bytes 1572872 | tf_op jit(solution)/shard_map/ppermute | solution.py:19
  69.6 17.4 %collective-permute-start.5 = (f32[2,128]{1,0:T(2,128)S(1)}, f32[2,128]{1,0:T(2,128)S(1)}, u32[]{:S(2)}, u32[]{:S(2)}) collective-permute-start(f32[2,128]{1,0:T(2,128)S(1)} %add.212), channel_id=1, source_target_pairs={{0,128},{4,132},{8,136},{12,140},{16,144},{20,148},{24,152},{28,15... | collective-permute-start | bytes 3080 | tf_op jit(solution)/shard_map/ppermute | solution.py:36
  81.7 8.3 %collective-permute-start.6 = (f32[2,128]{1,0:T(2,128)S(1)}, f32[2,128]{1,0:T(2,128)S(1)}, u32[]{:S(2)}, u32[]{:S(2)}) collective-permute-start(f32[2,128]{1,0:T(2,128)S(1)} %add.212), channel_id=1, source_target_pairs={{0,64},{4,68},{8,72},{12,76},{16,80},{20,84},{24,88},{28,92},{32,9... | collective-permute-start | bytes 3080 | tf_op jit(solution)/shard_map/ppermute | solution.py:36
  90.0 10.3 %collective-permute-start.7 = (f32[2,128]{1,0:T(2,128)S(1)}, f32[2,128]{1,0:T(2,128)S(1)}, u32[]{:S(2)}, u32[]{:S(2)}) collective-permute-start(f32[2,128]{1,0:T(2,128)S(1)} %select_add_fusion), channel_id=1, source_target_pairs={{0,192},{4,196},{8,200},{12,204},{16,208},{20,212},{24,216},{28,22... | collective-permute-start | bytes 3080 | tf_op jit(solution)/shard_map/ppermute | solution.py:54
  100.5 3.1 %collective-permute-start.10 = (f32[2,128]{1,0:T(2,128)S(1)}, f32[2,128]{1,0:T(2,128)S(1)}, u32[]{:S(2)}, u32[]{:S(2)}) collective-permute-start(f32[2,128]{1,0:T(2,128)S(1)} %add.217), channel_id=1, source_target_pairs={{0,4},{4,0},{8,12},{12,8},{16,20},{20,16},{24,28},{28,24},{32,36},... | collective-permute-start | bytes 3080 | tf_op jit(solution)/shard_map/ppermute | solution.py:24
  103.4 21.4 %copy-start.8 = (f32[2]{0:T(128)S(1)}, f32[2]{0:T(128)}, u32[]{:S(2)}) copy-start(f32[2]{0:T(128)} %constant.83) | copy-start | bytes 28
  103.6 5.5 %collective-permute-start.11 = (f32[2,128]{1,0:T(2,128)S(1)}, f32[2,128]{1,0:T(2,128)S(1)}, u32[]{:S(2)}, u32[]{:S(2)}) collective-permute-start(f32[2,128]{1,0:T(2,128)S(1)} %add.218), channel_id=1, source_target_pairs={{0,8},{4,12},{8,0},{12,4},{16,24},{20,28},{24,16},{28,20},{32,40},... | collective-permute-start | bytes 3080 | tf_op jit(solution)/shard_map/ppermute | solution.py:24
  109.1 6.4 %collective-permute-start.12 = (f32[2,128]{1,0:T(2,128)S(1)}, f32[2,128]{1,0:T(2,128)S(1)}, u32[]{:S(2)}, u32[]{:S(2)}) collective-permute-start(f32[2,128]{1,0:T(2,128)S(1)} %add.223), channel_id=1, source_target_pairs={{0,16},{4,20},{8,24},{12,28},{16,0},{20,4},{24,8},{28,12},{32,48},... | collective-permute-start | bytes 3080 | tf_op jit(solution)/shard_map/ppermute | solution.py:24
  115.4 9.4 %collective-permute-start.13 = (f32[2,128]{1,0:T(2,128)S(1)}, f32[2,128]{1,0:T(2,128)S(1)}, u32[]{:S(2)}, u32[]{:S(2)}) collective-permute-start(f32[2,128]{1,0:T(2,128)S(1)} %add.224), channel_id=1, source_target_pairs={{0,32},{4,36},{8,40},{12,44},{16,48},{20,52},{24,56},{28,60},{32,0... | collective-permute-start | bytes 3080 | tf_op jit(solution)/shard_map/ppermute | solution.py:24
